TPU v7x, 256 devices: a whole 4x4x8 slice. The times are simulated.
256 devices in a mesh: rows: 64 (over z, y, core), shock: 4 (over x).
Axes of the slice: x: 4, y: 4, z: 8, core: 2. Of those that a mesh axis runs over, the one named last changes fastest.
Arguments:
- coefs: bfloat16 [256, 16, 128, 128], P('rows'), may hold values from -0.125 to 0.125
- lag_pattern: int32 [256, 16], replicated, may hold values from 0 to 255, as said below
- loadings: float32 [32768, 128], P('rows'), may hold values from -0.5 to 0.5
- idiosyncratic: float32 [32768], P('rows'), may hold values from 0.5 to 2
- shocked: int32 [512], P('shock'), may hold values from 0 to 32767
Outputs:
- shares: float32 [32768, 512], P('rows', 'shock')
Inputs may be any that keep to these rules, and one draw needn't show every extreme that they name: `lag_pattern`: each row holds distinct blocks. The block rows held by any one device along `rows` together read exactly 1 distinct block from the 4 blocks held by every device along `rows`.
All inputs are finite; a program needn't handle non-finite values.
Results may differ from a plain program's by a relative error of at most 0.009.
Values may be sent and summed in bfloat16 or wider, within the bound.
No kernel may reach another device: no remote copies, remote signals or barrier semaphores. Data moves between devices by JAX's collectives and lax.ppermute only.
A program may use at most 64 MiB of HBM per device.

v0:
```python
import jax
import jax.numpy as jnp
from jax import lax
from jax.sharding import PartitionSpec as P

HORIZONS = 7


def on_device(coefs, lag_pattern, loadings, idiosyncratic, shocked):
    blk_dev = coefs.shape[0]
    lags = coefs.shape[1]
    block_size = coefs.shape[2]
    owners = lax.axis_size("rows")
    mine = lax.axis_index("rows")
    n_blocks = owners * blk_dev
    capacity = min(blk_dev, max(1, blk_dev * lags // owners))
    shock_columns = shocked.shape[0]
    local_rows = blk_dev * block_size
    row_ids = mine * local_rows + jnp.arange(local_rows, dtype=jnp.int32)
    pick_table = (shocked[:, None] == row_ids[None, :]).astype(jnp.float32)
    chosen = jnp.dot(
        pick_table, loadings, precision=lax.Precision.HIGHEST, preferred_element_type=jnp.float32
    )
    chosen_idio = jnp.dot(
        pick_table,
        idiosyncratic,
        precision=lax.Precision.HIGHEST,
        preferred_element_type=jnp.float32,
    )
    chosen, chosen_idio = lax.psum((chosen, chosen_idio), "rows")
    scale = jnp.sqrt(jnp.sum(chosen * chosen, axis=1) + chosen_idio)
    impact = jnp.dot(
        loadings, chosen.T, precision=lax.Precision.HIGHEST, preferred_element_type=jnp.float32
    )
    impact = impact + pick_table.T * idiosyncratic[:, None]
    impact = impact / scale[None, :]
    present_response = impact.astype(jnp.bfloat16).reshape(blk_dev, block_size, shock_columns)
    squared_terms = present_response.astype(jnp.float32) ** 2
    my_lags = lax.dynamic_slice_in_dim(lag_pattern, mine * blk_dev, blk_dev, 0)
    flat_lags = my_lags.reshape(-1)
    all_blocks_ids = jnp.arange(n_blocks, dtype=jnp.int32)
    read_need = jnp.any(flat_lags[:, None] == all_blocks_ids[None, :], axis=0).astype(jnp.int32)
    read_need = read_need.reshape(owners, blk_dev)
    read_before = jnp.cumsum(read_need, axis=1) - read_need
    owner_base = jnp.arange(owners, dtype=jnp.int32)[:, None] * capacity
    slot_of_block = (owner_base + read_before).reshape(-1)
    take_index = slot_of_block[flat_lags]
    reader_slots = lag_pattern.reshape(owners, blk_dev * lags)
    own_ids = mine * blk_dev + jnp.arange(blk_dev, dtype=jnp.int32)
    send_need = jnp.any(reader_slots[:, :, None] == own_ids[None, None, :], axis=1).astype(
        jnp.int32
    )
    send_before = jnp.cumsum(send_need, axis=1) - send_need
    cap_pos = jnp.arange(capacity, dtype=jnp.int32)
    routing_matrix = (
        (send_need[:, None, :] == 1) & (send_before[:, None, :] == cap_pos[None, :, None])
    ).astype(jnp.bfloat16)
    for step in range(HORIZONS - 1):
        outgoing = jnp.einsum(
            "vwq,qfn->vwfn", routing_matrix, present_response, preferred_element_type=jnp.float32
        ).astype(jnp.bfloat16)
        arriving_response = lax.all_to_all(
            outgoing, "rows", split_axis=0, concat_axis=0, tiled=True
        )
        stacked = arriving_response.reshape(owners * capacity, block_size, shock_columns)
        lagged = jnp.take(stacked, take_index, axis=0).reshape(
            blk_dev, lags, block_size, shock_columns
        )
        product = jnp.einsum("rlij,rljs->ris", coefs, lagged, preferred_element_type=jnp.float32)
        present_response = product.astype(jnp.bfloat16)
        squared_terms = squared_terms + present_response.astype(jnp.float32) ** 2
    totals = lax.psum(jnp.sum(squared_terms, axis=2), "shock")
    total_shocks = shock_columns * lax.axis_size("shock")
    shares = total_shocks * squared_terms / (totals[:, :, None] + 1e-06)
    return shares.reshape(local_rows, shock_columns)


def solution(mesh):
    placed = (P("rows", None, None, None), P(), P("rows", None), P("rows"), P("shock"))
    return jax.shard_map(
        on_device, mesh=mesh, in_specs=placed, out_specs=P("rows", "shock"), check_vma=False
    )
```

profile of v0, /device:TPU:96, one launch (start us, length us, event | category | flops | bytes accessed | tf_op | source)
XLA Modules:
  0.0 596.1 jit_solution(7297796239030286069)
XLA Ops:
  6.5 0.0 copy-start
  6.5 0.0 all-reduce.2.cloned.1.call-start
  6.5 2.1 fusion.19
  8.6 0.0 all-reduce.2.cloned.1.call-update
  8.6 0.8 copy.56
  9.5 0.1 eq.84
  9.5 0.2 compare_reduce_fusion
  9.8 0.9 convolution_bitcast_fusion.7
  10.8 110.0 %psum.22 = f32[128]{0:T(128)S(1)} all-reduce(f32[128]{0:T(128)S(1)} %convolution_bitcast_fusion.7), channel_id=1, replica_groups=mesh['rows'=64,'shock'=4] {'rows'}, use_global_device_ids=true, to_apply=%region_2.0 | all-reduce | flops 128 | bytes 1024 | tf_op jit(solution)/shard_map/psum | solution.py:30
  120.7 60.5 %all-reduce.2.cloned.1.call-done = f32[128,128]{1,0:T(8,128)} async-done(((f32[128,128]{1,0:T(8,128)}), f32[128,128]{1,0:T(8,128)}) %all-reduce.2.cloned.1.call-update) | async-done | bytes 65552 | tf_op jit(solution)/shard_map/psum | solution.py:30
  181.2 0.9 multiply_reduce_fusion
  182.2 1.3 fusion.2
  183.6 0.1 copy.57
  183.8 0.8 convert_bitcast_fusion.5
  184.5 2.6 copy.58
  187.2 8.4 %all-to-all-start = ((bf16[64,1,128,128]{3,2,1,0:T(8,128)(2,1)}), bf16[64,1,128,128]{3,2,1,0:T(8,128)(2,1)}, u32[]{:S(2)}, u32[]{:S(2)}) async-start(bf16[64,1,128,128]{3,2,1,0:T(8,128)(2,1)} %copy.58), calls=%async_computation | async-start | bytes 4194304 | tf_op jit(solution)/shard_map/all_to_all | solution.py:62
  195.6 0.1 constant_dynamic-slice_fusion
  195.6 0.1 copy.54
  195.7 0.1 reshape.125
  195.8 0.1 eq.92
  195.9 0.1 fusion.30
  196.0 0.1 reshape.138
  196.1 0.2 reduce_window_sum.20
  196.3 0.1 reduce_window_sum.21
  196.4 0.1 add.97
  196.5 0.8 gather_fusion
  197.4 47.5 %all-to-all-done = bf16[64,1,128,128]{3,2,1,0:T(8,128)(2,1)} async-done(((bf16[64,1,128,128]{3,2,1,0:T(8,128)(2,1)}), bf16[64,1,128,128]{3,2,1,0:T(8,128)(2,1)}, u32[]{:S(2)}, u32[]{:S(2)}) %all-to-all-start) | async-done | bytes 2097184 | tf_op jit(solution)/shard_map/all_to_all | solution.py:62
  244.9 3.7 gather_fusion.1
  248.6 1.8 broadcast_select_fusion.5
  250.4 0.7 fusion.17
  251.2 0.8 convert_bitcast_fusion.4
  251.9 1.4 copy.60
  253.3 56.6 %all_to_all.30 = bf16[64,1,128,128]{3,2,1,0:T(8,128)(2,1)} all-to-all(bf16[64,1,128,128]{3,2,1,0:T(8,128)(2,1)S(1)} %copy.60), channel_id=1, replica_groups=mesh['rows'=64,'shock'=4] {'rows'}, dimensions={0} | all-to-all | bytes 4194304 | tf_op jit(solution)/shard_map/all_to_all | solution.py:62
  309.9 3.7 gather_fusion.2
  313.6 1.8 broadcast_select_fusion.4
  315.4 0.7 fusion.16
  316.2 0.8 convert_bitcast_fusion.3
  316.9 1.4 copy.62
  318.3 56.6 %all_to_all.31 = bf16[64,1,128,128]{3,2,1,0:T(8,128)(2,1)} all-to-all(bf16[64,1,128,128]{3,2,1,0:T(8,128)(2,1)S(1)} %copy.62), channel_id=1, replica_groups=mesh['rows'=64,'shock'=4] {'rows'}, dimensions={0} | all-to-all | bytes 4194304 | tf_op jit(solution)/shard_map/all_to_all | solution.py:62
  374.9 3.7 gather_fusion.3
  378.6 1.8 broadcast_select_fusion.3
  380.4 0.7 fusion.15
  381.2 0.8 convert_bitcast_fusion.2
  381.9 1.4 copy.64
  383.3 56.6 %all_to_all.32 = bf16[64,1,128,128]{3,2,1,0:T(8,128)(2,1)} all-to-all(bf16[64,1,128,128]{3,2,1,0:T(8,128)(2,1)S(1)} %copy.64), channel_id=1, replica_groups=mesh['rows'=64,'shock'=4] {'rows'}, dimensions={0} | all-to-all | bytes 4194304 | tf_op jit(solution)/shard_map/all_to_all | solution.py:62
  439.9 3.7 gather_fusion.4
  443.6 1.8 broadcast_select_fusion.2
  445.4 0.7 fusion.14
  446.2 0.8 convert_bitcast_fusion.1
  446.9 1.4 copy.66
  448.3 56.8 %all_to_all.33 = bf16[64,1,128,128]{3,2,1,0:T(8,128)(2,1)} all-to-all(bf16[64,1,128,128]{3,2,1,0:T(8,128)(2,1)S(1)} %copy.66), channel_id=1, replica_groups=mesh['rows'=64,'shock'=4] {'rows'}, dimensions={0} | all-to-all | bytes 4194304 | tf_op jit(solution)/shard_map/all_to_all | solution.py:62
  505.1 3.7 gather_fusion.5
  508.8 1.8 broadcast_select_fusion.1
  510.6 0.7 fusion.13
  511.4 0.8 convert_bitcast_fusion
  512.1 2.6 copy.68
  514.8 7.5 %all-to-all-start.5 = ((bf16[64,1,128,128]{3,2,1,0:T(8,128)(2,1)}), bf16[64,1,128,128]{3,2,1,0:T(8,128)(2,1)}, u32[]{:S(2)}, u32[]{:S(2)}) async-start(bf16[64,1,128,128]{3,2,1,0:T(8,128)(2,1)} %copy.68), calls=%async_computation.5 | async-start | bytes 4194304 | tf_op jit(solution)/shard_map/all_to_all | solution.py:62
  522.3 0.1 copy.53
  522.4 49.2 %all-to-all-done.5 = bf16[64,1,128,128]{3,2,1,0:T(8,128)(2,1)} async-done(((bf16[64,1,128,128]{3,2,1,0:T(8,128)(2,1)}), bf16[64,1,128,128]{3,2,1,0:T(8,128)(2,1)}, u32[]{:S(2)}, u32[]{:S(2)}) %all-to-all-start.5) | async-done | bytes 2097184 | tf_op jit(solution)/shard_map/all_to_all | solution.py:62
  571.6 3.7 gather_fusion.6
  575.3 1.8 broadcast_select_fusion
  577.1 0.8 fusion.39
  578.0 10.4 %psum.23 = f32[4,128]{1,0:T(4,128)S(1)} all-reduce(f32[4,128]{1,0:T(4,128)S(1)} %get-tuple-element.6), channel_id=1, replica_groups=mesh['rows'=64,'shock'=4] {'shock'}, use_global_device_ids=true, to_apply=%region_8.10 | all-reduce | flops 512 | bytes 4096 | tf_op jit(solution)/shard_map/psum | solution.py:72
  588.4 0.8 multiply_divide_fusion
  (19 shorter events, 0.2 us)
Async XLA Ops:
  6.5 243.9 %copy-start = (bf16[4,16,128,128]{3,2,1,0:T(8,128)(2,1)S(1)}, bf16[4,16,128,128]{3,2,1,0:T(8,128)(2,1)}, u32[]{:S(2)}) copy-start(bf16[4,16,128,128]{3,2,1,0:T(8,128)(2,1)} %param.7) | copy-start | bytes 6291460
  6.5 174.7 %all-reduce.2.cloned.1.call-start = ((), (), s32[]{:S(2)}) async-start(), calls=%async_computation.6 | async-start | bytes 131072 | tf_op jit(solution)/shard_map/psum | solution.py:30
  187.2 8.4 %copy-start.1 = (s32[256,16]{0,1:T(8,128)S(1)}, s32[256,16]{0,1:T(8,128)}, u32[]{:S(2)}) copy-start(s32[256,16]{0,1:T(8,128)} %param.8) | copy-start | bytes 49156
  187.2 57.7 %all-to-all-start = ((bf16[64,1,128,128]{3,2,1,0:T(8,128)(2,1)}), bf16[64,1,128,128]{3,2,1,0:T(8,128)(2,1)}, u32[]{:S(2)}, u32[]{:S(2)}) async-start(bf16[64,1,128,128]{3,2,1,0:T(8,128)(2,1)} %copy.58), calls=%async_computation | async-start | bytes 4194304 | tf_op jit(solution)/shard_map/all_to_all | solution.py:62
  514.8 56.8 %all-to-all-start.5 = ((bf16[64,1,128,128]{3,2,1,0:T(8,128)(2,1)}), bf16[64,1,128,128]{3,2,1,0:T(8,128)(2,1)}, u32[]{:S(2)}, u32[]{:S(2)}) async-start(bf16[64,1,128,128]{3,2,1,0:T(8,128)(2,1)} %copy.68), calls=%async_computation.5 | async-start | bytes 4194304 | tf_op jit(solution)/shard_map/all_to_all | solution.py:62
Sparse Core Ops, SparseCore 0:
  10.8 170.4 all-reduce.1
where the time goes:
time: 600 us; the launch traced here: 596 us
  blocking collectives  347 us (58%)
  waiting for transfers between devices  157 us (26%)
  local copies, waits for them, and re-layouts  35.6 us (6%)
  starting transfers between devices  15.8 us (3%)
  between operations  13.7 us (2%)
  other arithmetic  13.4 us (2%)
  matrix products  13.4 us (2%)
    all_to_all x4, blocking collectives, on_device(): lax.all_to_all(outgoing, 'rows', split_axis=0, concat_axis=0, tiled=True)  227 us
    psum x1, blocking collectives, on_device(): chosen, chosen_idio = lax.psum((chosen, chosen_idio), 'rows')  110 us
    all_to_all x2, waiting for transfers between devices, on_device(): lax.all_to_all(outgoing, 'rows', split_axis=0, concat_axis=0, tiled=True)  96.7 us
    psum x1, waiting for transfers between devices, on_device(): chosen, chosen_idio = lax.psum((chosen, chosen_idio), 'rows')  60.5 us
    gather x6, local copies, waits for them, and re-layouts, on_device(): jnp.take(stacked, take_index, axis=0)  22.2 us
    all_to_all x2, starting transfers between devices, on_device(): lax.all_to_all(outgoing, 'rows', split_axis=0, concat_axis=0, tiled=True)  15.8 us
  transfers between devices with their start and end apart: 3, of which 3 were waited for; matrix products, arithmetic and copies ran while one was open for 1% of the time, Pallas kernels for 0%

commit v1 on v0

--- a/solution.py
+++ b/solution.py
@@ -4,6 +4,23 @@
 from jax.sharding import PartitionSpec as P
 
 HORIZONS = 7
+
+
+def gather_rows(chosen, chosen_idio, owners):
+    shocks, factors = chosen.shape
+    per = shocks // owners
+    packed = jnp.concatenate(
+        [
+            chosen.reshape(owners, per, factors),
+            jnp.pad(chosen_idio.reshape(owners, 1, per), ((0, 0), (0, 0), (0, factors - per))),
+        ],
+        axis=1,
+    )
+    arrived = lax.all_to_all(packed, "rows", 0, 0, tiled=True)
+    reduced = jnp.sum(arrived, axis=0, keepdims=True)
+    spread = jnp.broadcast_to(reduced, packed.shape)
+    full = lax.all_to_all(spread, "rows", 0, 0, tiled=True)
+    return full[:, :per, :].reshape(shocks, factors), full[:, per, :per].reshape(shocks)
 
 
 def on_device(coefs, lag_pattern, loadings, idiosyncratic, shocked):
@@ -27,7 +44,7 @@
         precision=lax.Precision.HIGHEST,
         preferred_element_type=jnp.float32,
     )
-    chosen, chosen_idio = lax.psum((chosen, chosen_idio), "rows")
+    chosen, chosen_idio = gather_rows(chosen, chosen_idio, owners)
     scale = jnp.sqrt(jnp.sum(chosen * chosen, axis=1) + chosen_idio)
     impact = jnp.dot(
         loadings, chosen.T, precision=lax.Precision.HIGHEST, preferred_element_type=jnp.float32

time: 600 us -> 450 us (0.75)
  blocking collectives: 347 us -> 237 us
  waiting for transfers between devices: 157 us -> 113 us
  starting transfers between devices: 15.8 us -> 33.2 us
  between operations: 13.7 us -> 0.42 us
    psum x1 -> x0, blocking collectives: 110 us -> none  [on_device(): chosen, chosen_idio = lax.psum((chosen, chosen_idio), 'rows')]
    psum x1 -> x0, waiting for transfers between devices: 60.5 us -> none  [on_device(): chosen, chosen_idio = lax.psum((chosen, chosen_idio), 'rows')]
    all_to_all x0 -> x2, starting transfers between devices: none -> 17.8 us  [the longest x1 10.9 us: gather_rows(): arrived = lax.all_to_all(packed, 'rows', 0, 0, tiled=True)]
    all_to_all x0 -> x2, waiting for transfers between devices: none -> 16.4 us  [the longest x1 8.78 us: gather_rows(): full = lax.all_to_all(spread, 'rows', 0, 0, tiled=True)]
  transfers between devices with their start and end apart: 3 -> 4, of which waited for: 3 -> 4; matrix products, arithmetic and copies ran while one was open for 1% -> 1% of each run, Pallas kernels for 0% -> 0%
where the time goes in v1:
time: 450 us; the launch traced here: 446 us
  blocking collectives  237 us (53%)
  waiting for transfers between devices  113 us (25%)
  local copies, waits for them, and re-layouts  37 us (8%)
  starting transfers between devices  33.2 us (7%)
  other arithmetic  13.4 us (3%)
  matrix products  11.8 us (3%)
    all_to_all x4, blocking collectives, on_device(): lax.all_to_all(outgoing, 'rows', split_axis=0, concat_axis=0, tiled=True)  226 us
    all_to_all x2, waiting for transfers between devices, on_device(): lax.all_to_all(outgoing, 'rows', split_axis=0, concat_axis=0, tiled=True)  96.8 us
    gather x6, local copies, waits for them, and re-layouts, on_device(): jnp.take(stacked, take_index, axis=0)  22.2 us
    all_to_all x2, starting transfers between devices, on_device(): lax.all_to_all(outgoing, 'rows', split_axis=0, concat_axis=0, tiled=True)  15.4 us
    select_n x7, other arithmetic, on_device(): jnp.take(stacked, take_index, axis=0)  11 us
    all_to_all x1, starting transfers between devices, gather_rows(): arrived = lax.all_to_all(packed, 'rows', 0, 0, tiled=True)  10.9 us
    convert_element_type x6, local copies, waits for them, and re-layouts, on_device(): outgoing = jnp.einsum('vwq,qfn->vwfn', routing_matrix, present_response,...  10.7 us
    psum x1, blocking collectives, on_device(): totals = lax.psum(jnp.sum(squared_terms, axis=2), 'shock')  10.5 us
  transfers between devices with their start and end apart: 4, of which 4 were waited for; matrix products, arithmetic and copies ran while one was open for 1% of the time, Pallas kernels for 0%

profile of v1, /device:TPU:96, one launch (start us, length us, event | category | flops | bytes accessed | tf_op | source)
XLA Modules:
  0.0 445.9 jit_solution(4151517080665676403)
XLA Ops:
  0.0 1.1 convolution_bitcast_fusion.7
  1.1 0.2 reshape.145
  1.3 1.3 fusion.19
  2.6 0.7 pad_maximum_fusion
  3.3 10.9 %all-to-all-start = ((f32[64,3,128]{2,1,0:T(4,128)}), f32[64,3,128]{2,1,0:T(4,128)S(1)}, u32[]{:S(2)}, u32[]{:S(2)}) async-start(f32[64,3,128]{2,1,0:T(4,128)} %pad_maximum_fusion), calls=%async_computation | async-start | bytes 262144 | tf_op jit(solution)/shard_map/all_to_all | solution.py:19
  14.3 0.8 copy.85
  15.2 0.2 compare_reduce_fusion
  15.4 7.6 %all-to-all-done = f32[64,3,128]{2,1,0:T(4,128)S(1)} async-done(((f32[64,3,128]{2,1,0:T(4,128)}), f32[64,3,128]{2,1,0:T(4,128)S(1)}, u32[]{:S(2)}, u32[]{:S(2)}) %all-to-all-start) | async-done | bytes 98336 | tf_op jit(solution)/shard_map/all_to_all | solution.py:19
  23.1 0.7 broadcast_in_dim.8
  23.8 6.9 %all-to-all-start.1 = ((f32[64,3,128]{2,1,0:T(4,128)}), f32[64,3,128]{2,1,0:T(4,128)S(1)}, u32[]{:S(2)}, u32[]{:S(2)}) async-start(f32[64,3,128]{2,1,0:T(4,128)} %broadcast_in_dim.8), calls=%async_computation.1 | async-start | bytes 262144 | tf_op jit(solution)/shard_map/all_to_all | solution.py:22
  30.7 8.8 %all-to-all-done.1 = f32[64,3,128]{2,1,0:T(4,128)S(1)} async-done(((f32[64,3,128]{2,1,0:T(4,128)}), f32[64,3,128]{2,1,0:T(4,128)S(1)}, u32[]{:S(2)}, u32[]{:S(2)}) %all-to-all-start.1) | async-done | bytes 98336 | tf_op jit(solution)/shard_map/all_to_all | solution.py:22
  39.5 0.1 slice_reduce_fusion
  39.6 0.1 reshape_squeeze.3
  39.8 0.1 copy.81
  39.9 0.1 reduce_sum.31
  40.1 0.4 fusion.2
  40.5 0.1 copy.86
  40.7 0.8 convert_bitcast_fusion.5
  41.5 2.6 copy.87
  44.1 8.0 %all-to-all-start.2 = ((bf16[64,1,128,128]{3,2,1,0:T(8,128)(2,1)}), bf16[64,1,128,128]{3,2,1,0:T(8,128)(2,1)}, u32[]{:S(2)}, u32[]{:S(2)}) async-start(bf16[64,1,128,128]{3,2,1,0:T(8,128)(2,1)} %copy.87), calls=%async_computation.2 | async-start | bytes 4194304 | tf_op jit(solution)/shard_map/all_to_all | solution.py:79
  52.4 0.1 fusion.31
  52.5 0.1 reshape.162
  52.7 0.2 reduce_window_sum.20
  52.8 0.1 reduce_window_sum.21
  52.9 0.1 add.99
  53.1 0.8 gather_fusion
  53.9 47.7 %all-to-all-done.2 = bf16[64,1,128,128]{3,2,1,0:T(8,128)(2,1)} async-done(((bf16[64,1,128,128]{3,2,1,0:T(8,128)(2,1)}), bf16[64,1,128,128]{3,2,1,0:T(8,128)(2,1)}, u32[]{:S(2)}, u32[]{:S(2)}) %all-to-all-start.2) | async-done | bytes 2097184 | tf_op jit(solution)/shard_map/all_to_all | solution.py:79
  101.6 3.7 gather_fusion.1
  105.3 1.8 broadcast_select_fusion.5
  107.1 0.7 fusion.17
  107.9 0.8 convert_bitcast_fusion.4
  108.6 1.4 copy.89
  110.0 56.4 %all_to_all.40 = bf16[64,1,128,128]{3,2,1,0:T(8,128)(2,1)} all-to-all(bf16[64,1,128,128]{3,2,1,0:T(8,128)(2,1)S(1)} %copy.89), channel_id=1, replica_groups=mesh['rows'=64,'shock'=4] {'rows'}, dimensions={0} | all-to-all | bytes 4194304 | tf_op jit(solution)/shard_map/all_to_all | solution.py:79
  166.4 3.7 gather_fusion.2
  170.1 1.8 broadcast_select_fusion.4
  172.0 0.7 fusion.16
  172.7 0.8 convert_bitcast_fusion.3
  173.5 1.4 copy.91
  174.8 56.6 %all_to_all.41 = bf16[64,1,128,128]{3,2,1,0:T(8,128)(2,1)} all-to-all(bf16[64,1,128,128]{3,2,1,0:T(8,128)(2,1)S(1)} %copy.91), channel_id=1, replica_groups=mesh['rows'=64,'shock'=4] {'rows'}, dimensions={0} | all-to-all | bytes 4194304 | tf_op jit(solution)/shard_map/all_to_all | solution.py:79
  231.4 3.7 gather_fusion.3
  235.1 1.8 broadcast_select_fusion.3
  237.0 0.7 fusion.15
  237.7 0.8 convert_bitcast_fusion.2
  238.5 1.4 copy.93
  239.8 56.6 %all_to_all.42 = bf16[64,1,128,128]{3,2,1,0:T(8,128)(2,1)} all-to-all(bf16[64,1,128,128]{3,2,1,0:T(8,128)(2,1)S(1)} %copy.93), channel_id=1, replica_groups=mesh['rows'=64,'shock'=4] {'rows'}, dimensions={0} | all-to-all | bytes 4194304 | tf_op jit(solution)/shard_map/all_to_all | solution.py:79
  296.4 3.7 gather_fusion.4
  300.1 1.8 broadcast_select_fusion.2
  302.0 0.7 fusion.14
  302.7 0.8 convert_bitcast_fusion.1
  303.5 1.4 copy.95
  304.8 56.8 %all_to_all.43 = bf16[64,1,128,128]{3,2,1,0:T(8,128)(2,1)} all-to-all(bf16[64,1,128,128]{3,2,1,0:T(8,128)(2,1)S(1)} %copy.95), channel_id=1, replica_groups=mesh['rows'=64,'shock'=4] {'rows'}, dimensions={0} | all-to-all | bytes 4194304 | tf_op jit(solution)/shard_map/all_to_all | solution.py:79
  361.6 3.7 gather_fusion.5
  365.3 1.8 broadcast_select_fusion.1
  367.2 0.7 fusion.13
  367.9 0.8 convert_bitcast_fusion
  368.7 2.6 copy.97
  371.3 7.5 %all-to-all-start.7 = ((bf16[64,1,128,128]{3,2,1,0:T(8,128)(2,1)}), bf16[64,1,128,128]{3,2,1,0:T(8,128)(2,1)}, u32[]{:S(2)}, u32[]{:S(2)}) async-start(bf16[64,1,128,128]{3,2,1,0:T(8,128)(2,1)} %copy.97), calls=%async_computation.7 | async-start | bytes 4194304 | tf_op jit(solution)/shard_map/all_to_all | solution.py:79
  378.8 0.1 copy.82
  378.9 49.2 %all-to-all-done.7 = bf16[64,1,128,128]{3,2,1,0:T(8,128)(2,1)} async-done(((bf16[64,1,128,128]{3,2,1,0:T(8,128)(2,1)}), bf16[64,1,128,128]{3,2,1,0:T(8,128)(2,1)}, u32[]{:S(2)}, u32[]{:S(2)}) %all-to-all-start.7) | async-done | bytes 2097184 | tf_op jit(solution)/shard_map/all_to_all | solution.py:79
  428.1 3.7 gather_fusion.6
  431.8 1.8 broadcast_select_fusion
  433.7 0.8 fusion.40
  434.5 10.5 %psum.7 = f32[4,128]{1,0:T(4,128)S(1)} all-reduce(f32[4,128]{1,0:T(4,128)S(1)} %get-tuple-element.6), channel_id=1, replica_groups=mesh['rows'=64,'shock'=4] {'shock'}, use_global_device_ids=true, to_apply=%region_7.9 | all-reduce | flops 512 | bytes 4096 | tf_op jit(solution)/shard_map/psum | solution.py:89
  445.0 0.8 multiply_divide_fusion
  (35 shorter events, 0.8 us)
Async XLA Ops:
  0.0 107.1 %copy-start = (bf16[4,16,128,128]{3,2,1,0:T(8,128)(2,1)S(1)}, bf16[4,16,128,128]{3,2,1,0:T(8,128)(2,1)}, u32[]{:S(2)}) copy-start(bf16[4,16,128,128]{3,2,1,0:T(8,128)(2,1)} %param.7) | copy-start | bytes 6291460
  0.0 40.1 %copy-start.3 = (s32[128]{0:T(128)S(1)}, s32[128]{0:T(128)}, u32[]{:S(2)}) copy-start(s32[128]{0:T(128)} %param.11) | copy-start | bytes 1540
  0.0 40.1 %copy-start.4 = (f32[512]{0:T(512)S(1)}, f32[512]{0:T(512)}, u32[]{:S(2)}) copy-start(f32[512]{0:T(512)} %param.10) | copy-start | bytes 6148
  0.0 40.1 %copy-start.1 = (f32[512,128]{1,0:T(8,128)S(1)}, f32[512,128]{1,0:T(8,128)}, u32[]{:S(2)}) copy-start(f32[512,128]{1,0:T(8,128)} %param.9) | copy-start | bytes 786436
  3.3 19.7 %all-to-all-start = ((f32[64,3,128]{2,1,0:T(4,128)}), f32[64,3,128]{2,1,0:T(4,128)S(1)}, u32[]{:S(2)}, u32[]{:S(2)}) async-start(f32[64,3,128]{2,1,0:T(4,128)} %pad_maximum_fusion), calls=%async_computation | async-start | bytes 262144 | tf_op jit(solution)/shard_map/all_to_all | solution.py:19
  23.8 15.7 %all-to-all-start.1 = ((f32[64,3,128]{2,1,0:T(4,128)}), f32[64,3,128]{2,1,0:T(4,128)S(1)}, u32[]{:S(2)}, u32[]{:S(2)}) async-start(f32[64,3,128]{2,1,0:T(4,128)} %broadcast_in_dim.8), calls=%async_computation.1 | async-start | bytes 262144 | tf_op jit(solution)/shard_map/all_to_all | solution.py:22
  44.1 8.0 %copy-start.2 = (s32[256,16]{0,1:T(8,128)S(1)}, s32[256,16]{0,1:T(8,128)}, u32[]{:S(2)}) copy-start(s32[256,16]{0,1:T(8,128)} %param.8) | copy-start | bytes 49156
  44.1 57.5 %all-to-all-start.2 = ((bf16[64,1,128,128]{3,2,1,0:T(8,128)(2,1)}), bf16[64,1,128,128]{3,2,1,0:T(8,128)(2,1)}, u32[]{:S(2)}, u32[]{:S(2)}) async-start(bf16[64,1,128,128]{3,2,1,0:T(8,128)(2,1)} %copy.87), calls=%async_computation.2 | async-start | bytes 4194304 | tf_op jit(solution)/shard_map/all_to_all | solution.py:79
  371.3 56.8 %all-to-all-start.7 = ((bf16[64,1,128,128]{3,2,1,0:T(8,128)(2,1)}), bf16[64,1,128,128]{3,2,1,0:T(8,128)(2,1)}, u32[]{:S(2)}, u32[]{:S(2)}) async-start(bf16[64,1,128,128]{3,2,1,0:T(8,128)(2,1)} %copy.97), calls=%async_computation.7 | async-start | bytes 4194304 | tf_op jit(solution)/shard_map/all_to_all | solution.py:79

commit v2 on v1

v2 whole, which is shorter than its diff:
```python
import numpy as np
import jax
import jax.numpy as jnp
from jax import lax
from jax.sharding import Mesh
from jax.sharding import PartitionSpec as P

HORIZONS = 7
CORE = 2
YS = 4
ZL = 2
ALL = ("zh", "zl", "y", "c", "x")
BOX = ("zl", "y", "c", "x")


def layout(zh, xs):
    zs = zh * ZL
    flat = lambda k, zl, y, c, x: (((k * ZL + zl) * YS + y) * CORE + c) * xs + x
    group_of = np.zeros((zh, ZL * YS * CORE * xs), np.int32)
    pos_of = np.zeros((zh, zs * YS * CORE), np.int32)
    zsrc = np.zeros((zh, ZL, YS, CORE, xs), np.int32)
    perm_in, perm_out = [], []
    for k in range(zh):
        for zl in range(ZL):
            for y in range(YS):
                for c in range(CORE):
                    for x in range(xs):
                        d = x if c == 0 else xs - 1 - x
                        z = (ZL * k - d) % zs if zl == 0 else (ZL * k + 1 + d) % zs
                        zsrc[k, zl, y, c, x] = z
                        g = (z * YS + y) * CORE + c
                        pos = ((zl * YS + y) * CORE + c) * xs + x
                        group_of[k, pos] = g
                        pos_of[k, g] = pos
                        src = flat(z // ZL, z % ZL, y, c, x)
                        me = flat(k, zl, y, c, x)
                        perm_in.append((src, me))
                        perm_out.append((me, flat(z // ZL, z % ZL, y, c, k)))
    return zsrc, group_of, pos_of, perm_in, perm_out


def gather_rows(chosen, chosen_idio, owners):
    shocks, factors = chosen.shape
    per = shocks // owners
    packed = jnp.concatenate(
        [
            chosen.reshape(owners, per, factors),
            jnp.pad(chosen_idio.reshape(owners, 1, per), ((0, 0), (0, 0), (0, factors - per))),
        ],
        axis=1,
    )
    arrived = lax.all_to_all(packed, BOX, 0, 0, tiled=True)
    reduced = jnp.sum(arrived, axis=0, keepdims=True)
    spread = jnp.broadcast_to(reduced, packed.shape)
    full = lax.all_to_all(spread, BOX, 0, 0, tiled=True)
    return full[:, :per, :].reshape(shocks, factors), full[:, per, :per].reshape(shocks)


def make_body(zh, xs):
    zsrc_t, group_t, pos_t, perm_in, perm_out = layout(zh, xs)

    def on_device(coefs, lag_pattern, loadings, idiosyncratic, shocked):
        loadings, idiosyncratic = lax.ppermute((loadings, idiosyncratic), ALL, perm_in)
        coefs = lax.ppermute(coefs, ALL, perm_in)
        blk_dev = coefs.shape[0]
        lags = coefs.shape[1]
        block_size = coefs.shape[2]
        k = lax.axis_index("zh")
        zl = lax.axis_index("zl")
        y = lax.axis_index("y")
        c = lax.axis_index("c")
        x = lax.axis_index("x")
        owners = ZL * YS * CORE * xs
        mine = (jnp.asarray(zsrc_t)[k, zl, y, c, x] * YS + y) * CORE + c
        group_of_pos = jnp.asarray(group_t)[k]
        pos_of_group = jnp.asarray(pos_t)[k]
        n_blocks = owners * blk_dev
        capacity = min(blk_dev, max(1, blk_dev * lags // owners))
        all_shocks = lax.all_gather(shocked, "x", axis=0, tiled=True)
        shock_columns = shocked.shape[0]
        shocked = lax.dynamic_slice_in_dim(all_shocks, k * shock_columns, shock_columns, 0)
        local_rows = blk_dev * block_size
        row_ids = mine * local_rows + jnp.arange(local_rows, dtype=jnp.int32)
        pick_table = (shocked[:, None] == row_ids[None, :]).astype(jnp.float32)
        chosen = jnp.dot(
            pick_table, loadings, precision=lax.Precision.HIGHEST, preferred_element_type=jnp.float32
        )
        chosen_idio = jnp.dot(
            pick_table,
            idiosyncratic,
            precision=lax.Precision.HIGHEST,
            preferred_element_type=jnp.float32,
        )
        chosen, chosen_idio = gather_rows(chosen, chosen_idio, owners)
        scale = jnp.sqrt(jnp.sum(chosen * chosen, axis=1) + chosen_idio)
        impact = jnp.dot(
            loadings, chosen.T, precision=lax.Precision.HIGHEST, preferred_element_type=jnp.float32
        )
        impact = impact + pick_table.T * idiosyncratic[:, None]
        impact = impact / scale[None, :]
        present_response = impact.astype(jnp.bfloat16).reshape(blk_dev, block_size, shock_columns)
        squared_terms = present_response.astype(jnp.float32) ** 2
        my_lags = lax.dynamic_slice_in_dim(lag_pattern, mine * blk_dev, blk_dev, 0)
        flat_lags = my_lags.reshape(-1)
        all_blocks_ids = jnp.arange(n_blocks, dtype=jnp.int32)
        read_need = jnp.any(flat_lags[:, None] == all_blocks_ids[None, :], axis=0).astype(jnp.int32)
        read_need = read_need.reshape(owners, blk_dev)[group_of_pos]
        read_before = jnp.cumsum(read_need, axis=1) - read_need
        owner_base = jnp.arange(owners, dtype=jnp.int32)[:, None] * capacity
        slot_of_pos = (owner_base + read_before).reshape(-1)
        block_at = pos_of_group[flat_lags // blk_dev] * blk_dev + flat_lags % blk_dev
        take_index = slot_of_pos[block_at]
        reader_slots = lag_pattern.reshape(owners, blk_dev * lags)[group_of_pos]
        own_ids = mine * blk_dev + jnp.arange(blk_dev, dtype=jnp.int32)
        send_need = jnp.any(reader_slots[:, :, None] == own_ids[None, None, :], axis=1).astype(
            jnp.int32
        )
        send_before = jnp.cumsum(send_need, axis=1) - send_need
        cap_pos = jnp.arange(capacity, dtype=jnp.int32)
        routing_matrix = (
            (send_need[:, None, :] == 1) & (send_before[:, None, :] == cap_pos[None, :, None])
        ).astype(jnp.bfloat16)
        for step in range(HORIZONS - 1):
            outgoing = jnp.einsum(
                "vwq,qfn->vwfn", routing_matrix, present_response, preferred_element_type=jnp.float32
            ).astype(jnp.bfloat16)
            arriving_response = lax.all_to_all(outgoing, BOX, split_axis=0, concat_axis=0, tiled=True)
            stacked = arriving_response.reshape(owners * capacity, block_size, shock_columns)
            lagged = jnp.take(stacked, take_index, axis=0).reshape(
                blk_dev, lags, block_size, shock_columns
            )
            product = jnp.einsum("rlij,rljs->ris", coefs, lagged, preferred_element_type=jnp.float32)
            present_response = product.astype(jnp.bfloat16)
            squared_terms = squared_terms + present_response.astype(jnp.float32) ** 2
        partial = jnp.sum(squared_terms, axis=2)
        squared_terms, partial = lax.ppermute((squared_terms, partial), ALL, perm_out)
        totals = lax.psum(partial, "x")
        total_shocks = shock_columns * xs
        shares = total_shocks * squared_terms / (totals[:, :, None] + 1e-06)
        return shares.reshape(local_rows, shock_columns)

    return on_device


def solution(mesh):
    rows = mesh.shape["rows"]
    xs = mesh.shape["shock"]
    zh = rows // (ZL * YS * CORE)
    mesh5 = Mesh(mesh.devices.reshape(zh, ZL, YS, CORE, xs), ALL)
    rows_axes = ("zh", "zl", "y", "c")
    placed = (
        P(rows_axes, None, None, None),
        P(),
        P(rows_axes, None),
        P(rows_axes),
        P("x"),
    )
    return jax.shard_map(
        make_body(zh, xs), mesh=mesh5, in_specs=placed, out_specs=P(rows_axes, "x"), check_vma=False
    )
```

time: 450 us -> 365 us (0.81)
  waiting for transfers between devices: 113 us -> 59.4 us
  blocking collectives: 237 us -> 202 us
  local copies, waits for them, and re-layouts: 37 us -> 41.7 us
    all_to_all x4 -> x3, waiting for transfers between devices: 113 us -> 55.8 us  [the longest x1 41.7 us: on_device(): lax.all_to_all(outgoing, BOX, split_axis=0, concat_axis=0, tiled=True)]
    all_to_all x4 -> x5, blocking collectives: 226 us -> 173 us  [on_device(): lax.all_to_all(outgoing, BOX, split_axis=0, concat_axis=0, tiled=True)]
    all_gather x0 -> x1, blocking collectives: none -> 15.8 us  [on_device(): all_shocks = lax.all_gather(shocked, 'x', axis=0, tiled=True)]
    ppermute x0 -> x5, starting transfers between devices: none -> 13.9 us  [the longest x2 8.76 us: on_device(): lax.ppermute((squared_terms, partial), ALL, perm_out)]
    all_to_all x4 -> x3, starting transfers between devices: 33.2 us -> 19.6 us  [the longest x1 6.84 us: gather_rows(): arrived = lax.all_to_all(packed, BOX, 0, 0, tiled=True)]
  transfers between devices with their start and end apart: 4 -> 8, of which waited for: 4 -> 4; matrix products, arithmetic and copies ran while one was open for 1% -> 4% of each run, Pallas kernels for 0% -> 0%
where the time goes in v2:
time: 365 us; the launch traced here: 362 us
  blocking collectives  202 us (55%)
  waiting for transfers between devices  59.4 us (16%)
  local copies, waits for them, and re-layouts  41.7 us (11%)
  starting transfers between devices  33.5 us (9%)
  other arithmetic  13.3 us (4%)
  matrix products  10.8 us (3%)
    all_to_all x5, blocking collectives, on_device(): lax.all_to_all(outgoing, BOX, split_axis=0, concat_axis=0, tiled=True)  173 us
    all_to_all x1, waiting for transfers between devices, on_device(): lax.all_to_all(outgoing, BOX, split_axis=0, concat_axis=0, tiled=True)  41.7 us
    gather x6, local copies, waits for them, and re-layouts, on_device(): jnp.take(stacked, take_index, axis=0)  22.2 us
    all_gather x1, blocking collectives, on_device(): all_shocks = lax.all_gather(shocked, 'x', axis=0, tiled=True)  15.8 us
    psum x1, blocking collectives, on_device(): totals = lax.psum(partial, 'x')  13.4 us
    select_n x7, other arithmetic, on_device(): jnp.take(stacked, take_index, axis=0)  11 us
    convert_element_type x6, local copies, waits for them, and re-layouts, on_device(): outgoing = jnp.einsum('vwq,qfn->vwfn', routing_matrix, present_response,...  9.42 us
    ppermute x2, starting transfers between devices, on_device(): lax.ppermute((squared_terms, partial), ALL, perm_out)  8.76 us
  transfers between devices with their start and end apart: 8, of which 4 were waited for; matrix products, arithmetic and copies ran while one was open for 4% of the time, Pallas kernels for 0%

profile of v2, /device:TPU:96, one launch (start us, length us, event | category | flops | bytes accessed | tf_op | source)
XLA Modules:
  0.0 362.0 jit_solution(7962456362149952889)
XLA Ops:
  0.0 1.3 collective-permute-start.1
  1.3 1.6 collective-permute-start
  2.9 1.3 dynamic_slice.16
  4.9 0.8 constant_dynamic-slice_fusion.1
  5.8 0.7 fusion.36
  6.5 0.8 copy.110
  7.4 15.8 %all-gather = s32[4,1,128]{2,1,0:T(1,128)S(1)} all-gather(s32[1,1,128]{2,1,0:T(1,128)} %bitcast.176), channel_id=1, replica_groups=mesh['zh'=4,'zl'=2,'y'=4,'c'=2,'x'=4] {'x'}, dimensions={0}, use_global_device_ids=true | all-gather | bytes 2560 | tf_op jit(solution)/shard_map/all_gather | solution.py:79
  23.4 0.6 gather_fusion
  24.0 0.2 convolution_bitcast_fusion.7
  24.4 0.3 fusion.18
  24.7 0.7 pad_maximum_fusion
  25.5 6.8 %all-to-all-start = ((f32[64,3,128]{2,1,0:T(4,128)}), f32[64,3,128]{2,1,0:T(4,128)S(1)}, u32[]{:S(2)}, u32[]{:S(2)}) async-start(f32[64,3,128]{2,1,0:T(4,128)} %pad_maximum_fusion), calls=%async_computation | async-start | bytes 262144 | tf_op jit(solution)/shard_map/all_to_all | solution.py:52
  32.6 7.0 %all-to-all-done = f32[64,3,128]{2,1,0:T(4,128)S(1)} async-done(((f32[64,3,128]{2,1,0:T(4,128)}), f32[64,3,128]{2,1,0:T(4,128)S(1)}, u32[]{:S(2)}, u32[]{:S(2)}) %all-to-all-start) | async-done | bytes 98336 | tf_op jit(solution)/shard_map/all_to_all | solution.py:52
  39.6 0.7 broadcast_in_dim.8
  40.3 5.9 %all-to-all-start.1 = ((f32[64,3,128]{2,1,0:T(4,128)}), f32[64,3,128]{2,1,0:T(4,128)S(1)}, u32[]{:S(2)}, u32[]{:S(2)}) async-start(f32[64,3,128]{2,1,0:T(4,128)} %broadcast_in_dim.8), calls=%async_computation.1 | async-start | bytes 262144 | tf_op jit(solution)/shard_map/all_to_all | solution.py:55
  46.3 7.2 %all-to-all-done.1 = f32[64,3,128]{2,1,0:T(4,128)S(1)} async-done(((f32[64,3,128]{2,1,0:T(4,128)}), f32[64,3,128]{2,1,0:T(4,128)S(1)}, u32[]{:S(2)}, u32[]{:S(2)}) %all-to-all-start.1) | async-done | bytes 98336 | tf_op jit(solution)/shard_map/all_to_all | solution.py:55
  54.1 0.4 fusion.2
  54.7 0.8 convert_bitcast_fusion.5
  55.4 2.6 copy.112
  58.1 6.8 %all-to-all-start.2 = ((bf16[64,1,128,128]{3,2,1,0:T(8,128)(2,1)}), bf16[64,1,128,128]{3,2,1,0:T(8,128)(2,1)}, u32[]{:S(2)}, u32[]{:S(2)}) async-start(bf16[64,1,128,128]{3,2,1,0:T(8,128)(2,1)} %copy.112), calls=%async_computation.2 | async-start | bytes 4194304 | tf_op jit(solution)/shard_map/all_to_all | solution.py:127
  64.9 2.3 collective-permute-start.2
  67.5 0.6 gather_fusion.1
  68.4 0.7 fusion.35
  69.1 0.8 gather_fusion.2
  69.9 0.8 gather_fusion.3
  70.7 41.7 %all-to-all-done.2 = bf16[64,1,128,128]{3,2,1,0:T(8,128)(2,1)} async-done(((bf16[64,1,128,128]{3,2,1,0:T(8,128)(2,1)}), bf16[64,1,128,128]{3,2,1,0:T(8,128)(2,1)}, u32[]{:S(2)}, u32[]{:S(2)}) %all-to-all-start.2) | async-done | bytes 2097184 | tf_op jit(solution)/shard_map/all_to_all | solution.py:127
  112.3 3.7 %gather_fusion.4 = bf16[64,128,128]{2,1,0:T(8,128)(2,1)} fusion(bf16[64,128,128]{2,1,0:T(8,128)(2,1)} %bitcast.17, s32[1024]{0:T(1024)S(1)} %pad_clamp_fusion), kind=kCustom, calls=%fused_computation.clone | custom fusion | bytes 4194560 | tf_op jit(solution)/shard_map/jit(_take)/gather | solution.py:129
  116.0 1.8 broadcast_select_fusion.5
  117.9 0.9 fusion.16
  118.9 0.8 convert_bitcast_fusion.4
  119.7 1.4 copy.115
  121.1 36.3 %all_to_all.40 = bf16[64,1,128,128]{3,2,1,0:T(8,128)(2,1)} all-to-all(bf16[64,1,128,128]{3,2,1,0:T(8,128)(2,1)S(1)} %copy.115), channel_id=1, replica_groups=mesh['zh'=4,'zl'=2,'y'=4,'c'=2,'x'=4] {'zl','y','c','x'}, dimensions={0} | all-to-all | bytes 4194304 | tf_op jit(solution)/shard_map/all_to_all | solution.py:127
  157.4 3.7 %gather_fusion.5 = bf16[64,128,128]{2,1,0:T(8,128)(2,1)} fusion(bf16[64,128,128]{2,1,0:T(8,128)(2,1)} %bitcast.164, s32[1024]{0:T(1024)S(1)} %pad_clamp_fusion), kind=kCustom, calls=%fused_computation.1.clone | custom fusion | bytes 4194560 | tf_op jit(solution)/shard_map/jit(_take)/gather | solution.py:129
  161.1 1.8 broadcast_select_fusion.4
  162.9 0.9 fusion.15
  163.9 0.8 convert_bitcast_fusion.3
  164.7 1.4 copy.118
  166.1 34.2 %all_to_all.41 = bf16[64,1,128,128]{3,2,1,0:T(8,128)(2,1)} all-to-all(bf16[64,1,128,128]{3,2,1,0:T(8,128)(2,1)S(1)} %copy.118), channel_id=1, replica_groups=mesh['zh'=4,'zl'=2,'y'=4,'c'=2,'x'=4] {'zl','y','c','x'}, dimensions={0} | all-to-all | bytes 4194304 | tf_op jit(solution)/shard_map/all_to_all | solution.py:127
  200.3 3.7 %gather_fusion.6 = bf16[64,128,128]{2,1,0:T(8,128)(2,1)} fusion(bf16[64,128,128]{2,1,0:T(8,128)(2,1)} %bitcast.166, s32[1024]{0:T(1024)S(1)} %pad_clamp_fusion), kind=kCustom, calls=%fused_computation.2.clone | custom fusion | bytes 4194560 | tf_op jit(solution)/shard_map/jit(_take)/gather | solution.py:129
  204.0 1.8 broadcast_select_fusion.3
  205.8 0.9 fusion.14
  206.8 0.8 convert_bitcast_fusion.2
  207.6 1.4 copy.121
  209.0 34.2 %all_to_all.42 = bf16[64,1,128,128]{3,2,1,0:T(8,128)(2,1)} all-to-all(bf16[64,1,128,128]{3,2,1,0:T(8,128)(2,1)S(1)} %copy.121), channel_id=1, replica_groups=mesh['zh'=4,'zl'=2,'y'=4,'c'=2,'x'=4] {'zl','y','c','x'}, dimensions={0} | all-to-all | bytes 4194304 | tf_op jit(solution)/shard_map/all_to_all | solution.py:127
  243.2 3.7 %gather_fusion.7 = bf16[64,128,128]{2,1,0:T(8,128)(2,1)} fusion(bf16[64,128,128]{2,1,0:T(8,128)(2,1)} %bitcast.168, s32[1024]{0:T(1024)S(1)} %pad_clamp_fusion), kind=kCustom, calls=%fused_computation.3.clone | custom fusion | bytes 4194560 | tf_op jit(solution)/shard_map/jit(_take)/gather | solution.py:129
  246.9 1.8 broadcast_select_fusion.2
  248.7 0.9 fusion.13
  249.8 0.8 convert_bitcast_fusion.1
  250.5 1.4 copy.124
  251.9 34.2 %all_to_all.43 = bf16[64,1,128,128]{3,2,1,0:T(8,128)(2,1)} all-to-all(bf16[64,1,128,128]{3,2,1,0:T(8,128)(2,1)S(1)} %copy.124), channel_id=1, replica_groups=mesh['zh'=4,'zl'=2,'y'=4,'c'=2,'x'=4] {'zl','y','c','x'}, dimensions={0} | all-to-all | bytes 4194304 | tf_op jit(solution)/shard_map/all_to_all | solution.py:127
  286.1 3.7 %gather_fusion.8 = bf16[64,128,128]{2,1,0:T(8,128)(2,1)} fusion(bf16[64,128,128]{2,1,0:T(8,128)(2,1)} %bitcast.170, s32[1024]{0:T(1024)S(1)} %pad_clamp_fusion), kind=kCustom, calls=%fused_computation.4.clone | custom fusion | bytes 4194560 | tf_op jit(solution)/shard_map/jit(_take)/gather | solution.py:129
  289.8 1.8 broadcast_select_fusion.1
  291.6 0.9 fusion.12
  292.6 0.8 convert_bitcast_fusion
  293.4 1.4 copy.127
  294.8 34.2 %all_to_all.44 = bf16[64,1,128,128]{3,2,1,0:T(8,128)(2,1)} all-to-all(bf16[64,1,128,128]{3,2,1,0:T(8,128)(2,1)S(1)} %copy.127), channel_id=1, replica_groups=mesh['zh'=4,'zl'=2,'y'=4,'c'=2,'x'=4] {'zl','y','c','x'}, dimensions={0} | all-to-all | bytes 4194304 | tf_op jit(solution)/shard_map/all_to_all | solution.py:127
  329.0 3.7 %gather_fusion.9 = bf16[64,128,128]{2,1,0:T(8,128)(2,1)} fusion(bf16[64,128,128]{2,1,0:T(8,128)(2,1)} %bitcast.163, s32[1024]{0:T(1024)S(1)} %pad_clamp_fusion), kind=kCustom, calls=%fused_computation.5.clone | custom fusion | bytes 4194560 | tf_op jit(solution)/shard_map/jit(_take)/gather | solution.py:129
  332.7 1.8 broadcast_select_fusion
  334.5 0.9 fusion.39
  335.5 2.3 collective-permute-start.3
  337.8 6.5 %collective-permute-start.4 = (f32[4,128]{1,0:T(4,128)S(1)}, f32[4,128]{1,0:T(4,128)S(1)}, u32[]{:S(2)}, u32[]{:S(2)}) collective-permute-start(f32[4,128]{1,0:T(4,128)S(1)} %get-tuple-element.6), channel_id=1, source_target_pairs={{0,0},{1,224},{2,192},{3,160},{4,164},{5,196},{6,228},{7,4},{8,8},... | collective-permute-start | bytes 6152 | tf_op jit(solution)/shard_map/ppermute | solution.py:136
  344.3 3.5 collective-permute-done.4
  347.8 13.4 %psum.7 = f32[4,128]{1,0:T(4,128)S(1)} all-reduce(f32[4,128]{1,0:T(4,128)S(1)} %collective-permute-done.4), channel_id=1, replica_groups=mesh['zh'=4,'zl'=2,'y'=4,'c'=2,'x'=4] {'x'}, use_global_device_ids=true, to_apply=%region_7.9 | all-reduce | flops 512 | bytes 4096 | tf_op jit(solution)/shard_map/psum | solution.py:137
  361.2 0.8 copy.129
  (47 shorter events, 3.0 us)
Async XLA Ops:
  0.0 23.9 %collective-permute-start.1 = (f32[512]{0:T(512)}, f32[512]{0:T(512)S(1)}, u32[]{:S(2)}, u32[]{:S(2)}) collective-permute-start(f32[512]{0:T(512)} %param.13), channel_id=1, source_target_pairs={{0,0},{225,1},{194,2},{163,3},{164,4},{197,5},{230,6},{7,7},{8,8},... | collective-permute-start | bytes 6152 | tf_op jit(solution)/shard_map/ppermute | solution.py:63
  1.3 23.1 %collective-permute-start = (f32[512,128]{1,0:T(8,128)}, f32[512,128]{1,0:T(8,128)S(1)}, u32[]{:S(2)}, u32[]{:S(2)}) collective-permute-start(f32[512,128]{1,0:T(8,128)} %param.12), channel_id=1, source_target_pairs={{0,0},{225,1},{194,2},{163,3},{164,4},{197,5},{230,6},{7,7},{8,8},... | collective-permute-start | bytes 786440 | tf_op jit(solution)/shard_map/ppermute | solution.py:63
  25.5 14.1 %all-to-all-start = ((f32[64,3,128]{2,1,0:T(4,128)}), f32[64,3,128]{2,1,0:T(4,128)S(1)}, u32[]{:S(2)}, u32[]{:S(2)}) async-start(f32[64,3,128]{2,1,0:T(4,128)} %pad_maximum_fusion), calls=%async_computation | async-start | bytes 262144 | tf_op jit(solution)/shard_map/all_to_all | solution.py:52
  40.3 13.2 %all-to-all-start.1 = ((f32[64,3,128]{2,1,0:T(4,128)}), f32[64,3,128]{2,1,0:T(4,128)S(1)}, u32[]{:S(2)}, u32[]{:S(2)}) async-start(f32[64,3,128]{2,1,0:T(4,128)} %broadcast_in_dim.8), calls=%async_computation.1 | async-start | bytes 262144 | tf_op jit(solution)/shard_map/all_to_all | solution.py:55
  58.1 54.2 %all-to-all-start.2 = ((bf16[64,1,128,128]{3,2,1,0:T(8,128)(2,1)}), bf16[64,1,128,128]{3,2,1,0:T(8,128)(2,1)}, u32[]{:S(2)}, u32[]{:S(2)}) async-start(bf16[64,1,128,128]{3,2,1,0:T(8,128)(2,1)} %copy.112), calls=%async_computation.2 | async-start | bytes 4194304 | tf_op jit(solution)/shard_map/all_to_all | solution.py:127
  64.9 53.0 %collective-permute-start.2 = (bf16[4,16,128,128]{3,2,1,0:T(8,128)(2,1)}, bf16[4,16,128,128]{3,2,1,0:T(8,128)(2,1)S(1)}, u32[]{:S(2)}, u32[]{:S(2)}) collective-permute-start(bf16[4,16,128,128]{3,2,1,0:T(8,128)(2,1)} %param.10), channel_id=1, source_target_pairs={{0,0},{225,1},{194,2},{163,3},{164,4},{197,5},{230,6},{7,7},{8,8},... | collective-permute-start | bytes 6291464 | tf_op jit(solution)/shard_map/ppermute | solution.py:64
  335.5 25.7 %collective-permute-start.3 = (f32[4,128,128]{1,2,0:T(8,128)S(1)}, f32[4,128,128]{1,2,0:T(8,128)S(1)}, u32[]{:S(2)}, u32[]{:S(2)}) collective-permute-start(f32[4,128,128]{1,2,0:T(8,128)S(1)} %get-tuple-element.7), channel_id=1, source_target_pairs={{0,0},{1,224},{2,192},{3,160},{4,164},{5,196},{6,228},{7,4},{8,8},... | collective-permute-start | bytes 786440 | tf_op jit(solution)/shard_map/ppermute | solution.py:136
  337.8 10.0 %collective-permute-start.4 = (f32[4,128]{1,0:T(4,128)S(1)}, f32[4,128]{1,0:T(4,128)S(1)}, u32[]{:S(2)}, u32[]{:S(2)}) collective-permute-start(f32[4,128]{1,0:T(4,128)S(1)} %get-tuple-element.6), channel_id=1, source_target_pairs={{0,0},{1,224},{2,192},{3,160},{4,164},{5,196},{6,228},{7,4},{8,8},... | collective-permute-start | bytes 6152 | tf_op jit(solution)/shard_map/ppermute | solution.py:136

commit v3 on v2

--- a/solution.py
+++ b/solution.py
@@ -35,8 +35,14 @@
                         src = flat(z // ZL, z % ZL, y, c, x)
                         me = flat(k, zl, y, c, x)
                         perm_in.append((src, me))
-                        perm_out.append((me, flat(z // ZL, z % ZL, y, c, k)))
-    return zsrc, group_of, pos_of, perm_in, perm_out
+                        perm_out.append([(me, flat(z // ZL, z % ZL, y, c, (k + j) % xs)) for j in range(xs)])
+    perm_out = [[p[j] for p in perm_out] for j in range(xs)]
+    perm_x = [
+        [(flat(k, zl, y, c, x), flat(k, zl, y, c, (x + j) % xs)) for k in range(zh) for zl in range(ZL)
+         for y in range(YS) for c in range(CORE) for x in range(xs)]
+        for j in range(xs)
+    ]
+    return zsrc, group_of, pos_of, perm_in, perm_out, perm_x
 
 
 def gather_rows(chosen, chosen_idio, owners):
@@ -57,7 +63,7 @@
 
 
 def make_body(zh, xs):
-    zsrc_t, group_t, pos_t, perm_in, perm_out = layout(zh, xs)
+    zsrc_t, group_t, pos_t, perm_in, perm_out, perm_x = layout(zh, xs)
 
     def on_device(coefs, lag_pattern, loadings, idiosyncratic, shocked):
         loadings, idiosyncratic = lax.ppermute((loadings, idiosyncratic), ALL, perm_in)
@@ -76,9 +82,9 @@
         pos_of_group = jnp.asarray(pos_t)[k]
         n_blocks = owners * blk_dev
         capacity = min(blk_dev, max(1, blk_dev * lags // owners))
-        all_shocks = lax.all_gather(shocked, "x", axis=0, tiled=True)
+        shifted = jnp.stack([shocked] + [lax.ppermute(shocked, ALL, perm_x[j]) for j in range(1, xs)])
         shock_columns = shocked.shape[0]
-        shocked = lax.dynamic_slice_in_dim(all_shocks, k * shock_columns, shock_columns, 0)
+        shocked = shifted[(x - k) % xs]
         local_rows = blk_dev * block_size
         row_ids = mine * local_rows + jnp.arange(local_rows, dtype=jnp.int32)
         pick_table = (shocked[:, None] == row_ids[None, :]).astype(jnp.float32)
@@ -120,7 +126,8 @@
         routing_matrix = (
             (send_need[:, None, :] == 1) & (send_before[:, None, :] == cap_pos[None, :, None])
         ).astype(jnp.bfloat16)
-        for step in range(HORIZONS - 1):
+        def one_step(step, carry):
+            present_response, squared_terms = carry
             outgoing = jnp.einsum(
                 "vwq,qfn->vwfn", routing_matrix, present_response, preferred_element_type=jnp.float32
             ).astype(jnp.bfloat16)
@@ -132,9 +139,17 @@
             product = jnp.einsum("rlij,rljs->ris", coefs, lagged, preferred_element_type=jnp.float32)
             present_response = product.astype(jnp.bfloat16)
             squared_terms = squared_terms + present_response.astype(jnp.float32) ** 2
+            return present_response, squared_terms
+
+        present_response, squared_terms = lax.fori_loop(
+            0, HORIZONS - 1, one_step, (present_response, squared_terms)
+        )
         partial = jnp.sum(squared_terms, axis=2)
-        squared_terms, partial = lax.ppermute((squared_terms, partial), ALL, perm_out)
-        totals = lax.psum(partial, "x")
+        squared_terms = lax.ppermute(squared_terms, ALL, perm_out[0])
+        parts = [lax.ppermute(partial, ALL, perm_out[j]) for j in range(xs)]
+        totals = parts[0]
+        for more in parts[1:]:
+            totals = totals + more
         total_shocks = shock_columns * xs
         shares = total_shocks * squared_terms / (totals[:, :, None] + 1e-06)
         return shares.reshape(local_rows, shock_columns)

time: 365 us -> 405 us (1.11)
  blocking collectives: 202 us -> 0 us
  waiting for transfers between devices: 59.4 us -> 189 us
  starting transfers between devices: 33.5 us -> 131 us
  local copies, waits for them, and re-layouts: 41.7 us -> 57.2 us
  other arithmetic: 13.3 us -> 3.04 us
  matrix products: 10.8 us -> 20.1 us
    all_to_all x5 -> x0, blocking collectives: 173 us -> none  [on_device(): lax.all_to_all(outgoing, BOX, split_axis=0, concat_axis=0, tiled=True)]
    all_to_all x1 -> x6, waiting for transfers between devices: 41.7 us -> 167 us  [one_step(): lax.all_to_all(outgoing, BOX, split_axis=0, concat_axis=0, tiled=True)]
    all_to_all x1, starting transfers between devices: 6.84 us -> 44 us  [gather_rows(): arrived = lax.all_to_all(packed, BOX, 0, 0, tiled=True)]
    all_to_all x1 -> x6, starting transfers between devices: 6.81 us -> 37.5 us  [one_step(): lax.all_to_all(outgoing, BOX, split_axis=0, concat_axis=0, tiled=True)]
    all_gather x1 -> x0, blocking collectives: 15.8 us -> none  [on_device(): all_shocks = lax.all_gather(shocked, 'x', axis=0, tiled=True)]
    ppermute x1, starting transfers between devices: 2.25 us -> 17.1 us  [on_device(): coefs = lax.ppermute(coefs, ALL, perm_in)]
    ppermute x2 -> x8, starting transfers between devices: 8.76 us -> 23.2 us  [the longest x4 16.5 us: on_device(): parts = [lax.ppermute(partial, ALL, perm_out[j]) for j in range(xs)]]
    psum x1 -> x0, blocking collectives: 13.4 us -> none  [on_device(): totals = lax.psum(partial, 'x')]
  transfers between devices with their start and end apart: 8 -> 19, of which waited for: 4 -> 10; matrix products, arithmetic and copies ran while one was open for 4% -> 3% of each run, Pallas kernels for 0% -> 0%
where the time goes in v3:
time: 405 us; the launch traced here: 402 us
  waiting for transfers between devices  189 us (47%)
  starting transfers between devices  131 us (32%)
  local copies, waits for them, and re-layouts  57.2 us (14%)
  matrix products  20.1 us (5%)
    all_to_all x6, waiting for transfers between devices, one_step(): lax.all_to_all(outgoing, BOX, split_axis=0, concat_axis=0, tiled=True)  167 us
    all_to_all x1, starting transfers between devices, gather_rows(): arrived = lax.all_to_all(packed, BOX, 0, 0, tiled=True)  44 us
    all_to_all x6, starting transfers between devices, one_step(): lax.all_to_all(outgoing, BOX, split_axis=0, concat_axis=0, tiled=True)  37.5 us
    gather x12, local copies, waits for them, and re-layouts, one_step(): jnp.take(stacked, take_index, axis=0)  30.9 us
    ppermute x1, starting transfers between devices, on_device(): coefs = lax.ppermute(coefs, ALL, perm_in)  17.1 us
    ppermute x4, starting transfers between devices, on_device(): parts = [lax.ppermute(partial, ALL, perm_out[j]) for j in range(xs)]  16.5 us
    convert_element_type x6, local copies, waits for them, and re-layouts, one_step(): outgoing = jnp.einsum('vwq,qfn->vwfn', routing_matrix, present_response,...  15.9 us
    dot_general x6, matrix products, one_step(): jnp.einsum('rlij,rljs->ris', coefs, lagged, preferred_element_type=jnp.fl...  14.6 us
  transfers between devices with their start and end apart: 19, of which 10 were waited for; matrix products, arithmetic and copies ran while one was open for 3% of the time, Pallas kernels for 0%

profile of v3, /device:TPU:96, one launch (start us, length us, event | category | flops | bytes accessed | tf_op | source)
XLA Modules:
  0.0 401.8 jit_solution(4386321769466386884)
XLA Ops:
  0.0 2.8 collective-permute-start.2
  2.8 0.8 collective-permute-start.1
  3.6 0.9 collective-permute-start
  4.4 1.3 collective-permute-start.4
  5.8 17.1 %collective-permute-start.5 = (bf16[4,16,128,128]{3,2,1,0:T(8,128)(2,1)}, bf16[4,16,128,128]{3,2,1,0:T(8,128)(2,1)}, u32[]{:S(2)}, u32[]{:S(2)}) collective-permute-start(bf16[4,16,128,128]{3,2,1,0:T(8,128)(2,1)} %param.10), channel_id=1, source_target_pairs={{0,0},{225,1},{194,2},{163,3},{164,4},{197,5},{230,6},{7,7},{8,8},... | collective-permute-start | bytes 6291464 | tf_op jit(solution)/shard_map/ppermute | solution.py:70
  22.9 1.3 dynamic_slice.16
  24.8 0.8 constant_dynamic-slice_fusion.2
  25.8 0.8 copy.63
  30.0 0.8 gather_fusion.2
  30.8 1.6 collective-permute-start.3
  34.6 44.0 %all-to-all-start.1 = ((f32[64,3,128]{2,1,0:T(4,128)}), f32[64,3,128]{2,1,0:T(4,128)S(1)}, u32[]{:S(2)}, u32[]{:S(2)}) async-start(f32[64,3,128]{2,1,0:T(4,128)} %pad_maximum_fusion), calls=%async_computation.1 | async-start | bytes 262144 | tf_op jit(solution)/shard_map/all_to_all | solution.py:58
  78.8 0.8 gather_fusion.3
  79.5 6.3 %all-to-all-done.1 = f32[64,3,128]{2,1,0:T(4,128)S(1)} async-done(((f32[64,3,128]{2,1,0:T(4,128)}), f32[64,3,128]{2,1,0:T(4,128)S(1)}, u32[]{:S(2)}, u32[]{:S(2)}) %all-to-all-start.1) | async-done | bytes 98336 | tf_op jit(solution)/shard_map/all_to_all | solution.py:58
  86.6 5.9 %all-to-all-start.2 = ((f32[64,3,128]{2,1,0:T(4,128)}), f32[64,3,128]{2,1,0:T(4,128)S(1)}, u32[]{:S(2)}, u32[]{:S(2)}) async-start(f32[64,3,128]{2,1,0:T(4,128)} %broadcast_in_dim.9), calls=%async_computation.2 | async-start | bytes 262144 | tf_op jit(solution)/shard_map/all_to_all | solution.py:61
  92.5 7.2 %all-to-all-done.2 = f32[64,3,128]{2,1,0:T(4,128)S(1)} async-done(((f32[64,3,128]{2,1,0:T(4,128)}), f32[64,3,128]{2,1,0:T(4,128)S(1)}, u32[]{:S(2)}, u32[]{:S(2)}) %all-to-all-start.2) | async-done | bytes 98336 | tf_op jit(solution)/shard_map/all_to_all | solution.py:61
  100.8 272.6 %while.12 = (s32[]{:T(128)}, bf16[4,128,128]{1,2,0:T(8,128)(2,1)S(1)}, f32[4,128,128]{1,2,0:T(8,128)S(1)}, s32[64]{0:T(128)S(1)}, bf16[64,1,4]{0,2,1:T(4,128)(2,...) while((s32[]{:T(128)}, bf16[4,128,128]{1,2,0:T(8,128)(2,1)S(1)}, f32[4,128,128]{1,2,0:T(8,128)S(1)}, ...), condition=%wide.region_7.8_spmd, body=%wide.region_6.7_spmd.sunk | while | flops 279184960 | bytes 26221036 | solution.py:144
  101.0 0.8 convert_bitcast_fusion.3
  101.8 2.6 copy.80
  104.4 6.0 %all-to-all-start = ((bf16[64,1,128,128]{3,2,1,0:T(8,128)(2,1)}), bf16[64,1,128,128]{3,2,1,0:T(8,128)(2,1)S(1)}, u32[]{:S(2)}, u32[]{:S(2)}) async-start(bf16[64,1,128,128]{3,2,1,0:T(8,128)(2,1)} %copy.80), calls=%async_computation | async-start | bytes 4194304 | tf_op jit(solution)/shard_map/while/body/eval_jaxpr/all_to_all | solution.py:134
  110.6 27.9 %all-to-all-done = bf16[64,1,128,128]{3,2,1,0:T(8,128)(2,1)S(1)} async-done(((bf16[64,1,128,128]{3,2,1,0:T(8,128)(2,1)}), bf16[64,1,128,128]{3,2,1,0:T(8,128)(2,1)S(1)}, u32[]{:S(2)}, u32[]{:S(2)}) %all-to-all-start) | async-done | bytes 2097184 | tf_op jit(solution)/shard_map/while/body/eval_jaxpr/all_to_all | solution.py:134
  138.4 2.1 gather_fusion
  140.5 3.0 copy.81
  143.6 2.4 multiply_add_fusion.2
  147.0 2.6 copy.80
  149.6 6.4 %all-to-all-start = ((bf16[64,1,128,128]{3,2,1,0:T(8,128)(2,1)}), bf16[64,1,128,128]{3,2,1,0:T(8,128)(2,1)S(1)}, u32[]{:S(2)}, u32[]{:S(2)}) async-start(bf16[64,1,128,128]{3,2,1,0:T(8,128)(2,1)} %copy.80), calls=%async_computation | async-start | bytes 4194304 | tf_op jit(solution)/shard_map/while/body/eval_jaxpr/all_to_all | solution.py:134
  156.1 27.9 %all-to-all-done = bf16[64,1,128,128]{3,2,1,0:T(8,128)(2,1)S(1)} async-done(((bf16[64,1,128,128]{3,2,1,0:T(8,128)(2,1)}), bf16[64,1,128,128]{3,2,1,0:T(8,128)(2,1)S(1)}, u32[]{:S(2)}, u32[]{:S(2)}) %all-to-all-start) | async-done | bytes 2097184 | tf_op jit(solution)/shard_map/while/body/eval_jaxpr/all_to_all | solution.py:134
  184.0 2.1 gather_fusion
  186.1 3.0 copy.81
  189.1 2.4 multiply_add_fusion.2
  191.7 0.8 convert_bitcast_fusion.3
  192.5 2.6 copy.80
  195.2 6.3 %all-to-all-start = ((bf16[64,1,128,128]{3,2,1,0:T(8,128)(2,1)}), bf16[64,1,128,128]{3,2,1,0:T(8,128)(2,1)S(1)}, u32[]{:S(2)}, u32[]{:S(2)}) async-start(bf16[64,1,128,128]{3,2,1,0:T(8,128)(2,1)} %copy.80), calls=%async_computation | async-start | bytes 4194304 | tf_op jit(solution)/shard_map/while/body/eval_jaxpr/all_to_all | solution.py:134
  201.6 27.9 %all-to-all-done = bf16[64,1,128,128]{3,2,1,0:T(8,128)(2,1)S(1)} async-done(((bf16[64,1,128,128]{3,2,1,0:T(8,128)(2,1)}), bf16[64,1,128,128]{3,2,1,0:T(8,128)(2,1)S(1)}, u32[]{:S(2)}, u32[]{:S(2)}) %all-to-all-start) | async-done | bytes 2097184 | tf_op jit(solution)/shard_map/while/body/eval_jaxpr/all_to_all | solution.py:134
  229.4 2.1 gather_fusion
  231.5 3.0 copy.81
  234.6 2.4 multiply_add_fusion.2
  237.2 0.8 convert_bitcast_fusion.3
  238.0 2.6 copy.80
  240.6 6.3 %all-to-all-start = ((bf16[64,1,128,128]{3,2,1,0:T(8,128)(2,1)}), bf16[64,1,128,128]{3,2,1,0:T(8,128)(2,1)S(1)}, u32[]{:S(2)}, u32[]{:S(2)}) async-start(bf16[64,1,128,128]{3,2,1,0:T(8,128)(2,1)} %copy.80), calls=%async_computation | async-start | bytes 4194304 | tf_op jit(solution)/shard_map/while/body/eval_jaxpr/all_to_all | solution.py:134
  247.0 27.9 %all-to-all-done = bf16[64,1,128,128]{3,2,1,0:T(8,128)(2,1)S(1)} async-done(((bf16[64,1,128,128]{3,2,1,0:T(8,128)(2,1)}), bf16[64,1,128,128]{3,2,1,0:T(8,128)(2,1)S(1)}, u32[]{:S(2)}, u32[]{:S(2)}) %all-to-all-start) | async-done | bytes 2097184 | tf_op jit(solution)/shard_map/while/body/eval_jaxpr/all_to_all | solution.py:134
  274.9 2.1 gather_fusion
  277.0 3.0 copy.81
  280.1 2.4 multiply_add_fusion.2
  282.7 0.8 convert_bitcast_fusion.3
  283.4 2.6 copy.80
  286.1 6.3 %all-to-all-start = ((bf16[64,1,128,128]{3,2,1,0:T(8,128)(2,1)}), bf16[64,1,128,128]{3,2,1,0:T(8,128)(2,1)S(1)}, u32[]{:S(2)}, u32[]{:S(2)}) async-start(bf16[64,1,128,128]{3,2,1,0:T(8,128)(2,1)} %copy.80), calls=%async_computation | async-start | bytes 4194304 | tf_op jit(solution)/shard_map/while/body/eval_jaxpr/all_to_all | solution.py:134
  292.5 27.9 %all-to-all-done = bf16[64,1,128,128]{3,2,1,0:T(8,128)(2,1)S(1)} async-done(((bf16[64,1,128,128]{3,2,1,0:T(8,128)(2,1)}), bf16[64,1,128,128]{3,2,1,0:T(8,128)(2,1)S(1)}, u32[]{:S(2)}, u32[]{:S(2)}) %all-to-all-start) | async-done | bytes 2097184 | tf_op jit(solution)/shard_map/while/body/eval_jaxpr/all_to_all | solution.py:134
  320.4 2.1 gather_fusion
  322.5 3.0 copy.81
  325.5 2.4 multiply_add_fusion.2
  328.1 0.8 convert_bitcast_fusion.3
  328.9 2.6 copy.80
  331.5 6.3 %all-to-all-start = ((bf16[64,1,128,128]{3,2,1,0:T(8,128)(2,1)}), bf16[64,1,128,128]{3,2,1,0:T(8,128)(2,1)S(1)}, u32[]{:S(2)}, u32[]{:S(2)}) async-start(bf16[64,1,128,128]{3,2,1,0:T(8,128)(2,1)} %copy.80), calls=%async_computation | async-start | bytes 4194304 | tf_op jit(solution)/shard_map/while/body/eval_jaxpr/all_to_all | solution.py:134
  337.9 27.9 %all-to-all-done = bf16[64,1,128,128]{3,2,1,0:T(8,128)(2,1)S(1)} async-done(((bf16[64,1,128,128]{3,2,1,0:T(8,128)(2,1)}), bf16[64,1,128,128]{3,2,1,0:T(8,128)(2,1)S(1)}, u32[]{:S(2)}, u32[]{:S(2)}) %all-to-all-start) | async-done | bytes 2097184 | tf_op jit(solution)/shard_map/while/body/eval_jaxpr/all_to_all | solution.py:134
  365.8 2.1 gather_fusion
  367.9 3.0 copy.81
  371.0 2.4 multiply_add_fusion.2
  373.4 2.3 collective-permute-start.6
  376.4 8.1 %collective-permute-start.9 = (f32[4,128]{1,0:T(4,128)S(1)}, f32[4,128]{1,0:T(4,128)S(1)}, u32[]{:S(2)}, u32[]{:S(2)}) collective-permute-start(f32[4,128]{1,0:T(4,128)S(1)} %reduce_sum.32), channel_id=1, source_target_pairs={{0,2},{1,226},{2,194},{3,162},{4,166},{5,198},{6,230},{7,6},{8,10}... | collective-permute-start | bytes 6152 | tf_op jit(solution)/shard_map/ppermute | solution.py:149
  384.5 5.8 %collective-permute-start.7 = (f32[4,128]{1,0:T(4,128)S(1)}, f32[4,128]{1,0:T(4,128)S(1)}, u32[]{:S(2)}, u32[]{:S(2)}) collective-permute-start(f32[4,128]{1,0:T(4,128)S(1)} %reduce_sum.32), channel_id=1, source_target_pairs={{0,0},{1,224},{2,192},{3,160},{4,164},{5,196},{6,228},{7,4},{8,8},... | collective-permute-start | bytes 6152 | tf_op jit(solution)/shard_map/ppermute | solution.py:149
  390.4 1.9 collective-permute-start.8
  392.3 1.0 collective-permute-done.7
  393.3 7.7 %collective-permute-done.8 = f32[4,128]{1,0:T(4,128)S(1)} collective-permute-done((f32[4,128]{1,0:T(4,128)S(1)}, f32[4,128]{1,0:T(4,128)S(1)}, u32[]{:S(2)}, u32[]{:S(2)}) %collective-permute-start.8) | collective-permute-done | bytes 2080 | tf_op jit(solution)/shard_map/ppermute | solution.py:149
  401.0 0.8 copy.65
  (87 shorter events, 10.6 us)
Async XLA Ops:
  0.0 30.8 %collective-permute-start.2 = (s32[128]{0:T(128)}, s32[128]{0:T(128)S(1)}, u32[]{:S(2)}, u32[]{:S(2)}) collective-permute-start(s32[128]{0:T(128)} %param.14), channel_id=1, source_target_pairs={{0,3},{1,0},{2,1},{3,2},{4,7},{5,4},{6,5},{7,6},{8,11},{9,8},{10,9... | collective-permute-start | bytes 1544 | tf_op jit(solution)/shard_map/ppermute | solution.py:85
  2.8 29.6 %collective-permute-start.1 = (s32[128]{0:T(128)}, s32[128]{0:T(128)S(1)}, u32[]{:S(2)}, u32[]{:S(2)}) collective-permute-start(s32[128]{0:T(128)} %param.14), channel_id=1, source_target_pairs={{0,2},{1,3},{2,0},{3,1},{4,6},{5,7},{6,4},{7,5},{8,10},{9,11},{10,... | collective-permute-start | bytes 1544 | tf_op jit(solution)/shard_map/ppermute | solution.py:85
  3.6 28.8 %collective-permute-start = (s32[128]{0:T(128)}, s32[128]{0:T(128)S(1)}, u32[]{:S(2)}, u32[]{:S(2)}) collective-permute-start(s32[128]{0:T(128)} %param.14), channel_id=1, source_target_pairs={{0,1},{1,2},{2,3},{3,0},{4,5},{5,6},{6,7},{7,4},{8,9},{9,10},{10,1... | collective-permute-start | bytes 1544 | tf_op jit(solution)/shard_map/ppermute | solution.py:85
  4.4 28.6 %collective-permute-start.4 = (f32[512]{0:T(512)}, f32[512]{0:T(512)S(1)}, u32[]{:S(2)}, u32[]{:S(2)}) collective-permute-start(f32[512]{0:T(512)} %param.13), channel_id=1, source_target_pairs={{0,0},{225,1},{194,2},{163,3},{164,4},{197,5},{230,6},{7,7},{8,8},... | collective-permute-start | bytes 6152 | tf_op jit(solution)/shard_map/ppermute | solution.py:69
  5.8 95.1 %collective-permute-start.5 = (bf16[4,16,128,128]{3,2,1,0:T(8,128)(2,1)}, bf16[4,16,128,128]{3,2,1,0:T(8,128)(2,1)}, u32[]{:S(2)}, u32[]{:S(2)}) collective-permute-start(bf16[4,16,128,128]{3,2,1,0:T(8,128)(2,1)} %param.10), channel_id=1, source_target_pairs={{0,0},{225,1},{194,2},{163,3},{164,4},{197,5},{230,6},{7,7},{8,8},... | collective-permute-start | bytes 6291464 | tf_op jit(solution)/shard_map/ppermute | solution.py:70
  30.8 2.8 collective-permute-start.3
  34.6 51.2 %all-to-all-start.1 = ((f32[64,3,128]{2,1,0:T(4,128)}), f32[64,3,128]{2,1,0:T(4,128)S(1)}, u32[]{:S(2)}, u32[]{:S(2)}) async-start(f32[64,3,128]{2,1,0:T(4,128)} %pad_maximum_fusion), calls=%async_computation.1 | async-start | bytes 262144 | tf_op jit(solution)/shard_map/all_to_all | solution.py:58
  86.6 13.2 %all-to-all-start.2 = ((f32[64,3,128]{2,1,0:T(4,128)}), f32[64,3,128]{2,1,0:T(4,128)S(1)}, u32[]{:S(2)}, u32[]{:S(2)}) async-start(f32[64,3,128]{2,1,0:T(4,128)} %broadcast_in_dim.9), calls=%async_computation.2 | async-start | bytes 262144 | tf_op jit(solution)/shard_map/all_to_all | solution.py:61
  104.4 34.0 %all-to-all-start = ((bf16[64,1,128,128]{3,2,1,0:T(8,128)(2,1)}), bf16[64,1,128,128]{3,2,1,0:T(8,128)(2,1)S(1)}, u32[]{:S(2)}, u32[]{:S(2)}) async-start(bf16[64,1,128,128]{3,2,1,0:T(8,128)(2,1)} %copy.80), calls=%async_computation | async-start | bytes 4194304 | tf_op jit(solution)/shard_map/while/body/eval_jaxpr/all_to_all | solution.py:134
  149.6 34.4 %all-to-all-start = ((bf16[64,1,128,128]{3,2,1,0:T(8,128)(2,1)}), bf16[64,1,128,128]{3,2,1,0:T(8,128)(2,1)S(1)}, u32[]{:S(2)}, u32[]{:S(2)}) async-start(bf16[64,1,128,128]{3,2,1,0:T(8,128)(2,1)} %copy.80), calls=%async_computation | async-start | bytes 4194304 | tf_op jit(solution)/shard_map/while/body/eval_jaxpr/all_to_all | solution.py:134
  195.2 34.3 %all-to-all-start = ((bf16[64,1,128,128]{3,2,1,0:T(8,128)(2,1)}), bf16[64,1,128,128]{3,2,1,0:T(8,128)(2,1)S(1)}, u32[]{:S(2)}, u32[]{:S(2)}) async-start(bf16[64,1,128,128]{3,2,1,0:T(8,128)(2,1)} %copy.80), calls=%async_computation | async-start | bytes 4194304 | tf_op jit(solution)/shard_map/while/body/eval_jaxpr/all_to_all | solution.py:134
  240.6 34.3 %all-to-all-start = ((bf16[64,1,128,128]{3,2,1,0:T(8,128)(2,1)}), bf16[64,1,128,128]{3,2,1,0:T(8,128)(2,1)S(1)}, u32[]{:S(2)}, u32[]{:S(2)}) async-start(bf16[64,1,128,128]{3,2,1,0:T(8,128)(2,1)} %copy.80), calls=%async_computation | async-start | bytes 4194304 | tf_op jit(solution)/shard_map/while/body/eval_jaxpr/all_to_all | solution.py:134
  286.1 34.3 %all-to-all-start = ((bf16[64,1,128,128]{3,2,1,0:T(8,128)(2,1)}), bf16[64,1,128,128]{3,2,1,0:T(8,128)(2,1)S(1)}, u32[]{:S(2)}, u32[]{:S(2)}) async-start(bf16[64,1,128,128]{3,2,1,0:T(8,128)(2,1)} %copy.80), calls=%async_computation | async-start | bytes 4194304 | tf_op jit(solution)/shard_map/while/body/eval_jaxpr/all_to_all | solution.py:134
  331.5 34.3 %all-to-all-start = ((bf16[64,1,128,128]{3,2,1,0:T(8,128)(2,1)}), bf16[64,1,128,128]{3,2,1,0:T(8,128)(2,1)S(1)}, u32[]{:S(2)}, u32[]{:S(2)}) async-start(bf16[64,1,128,128]{3,2,1,0:T(8,128)(2,1)} %copy.80), calls=%async_computation | async-start | bytes 4194304 | tf_op jit(solution)/shard_map/while/body/eval_jaxpr/all_to_all | solution.py:134
  373.4 27.5 %collective-permute-start.6 = (f32[4,128,128]{1,2,0:T(8,128)S(1)}, f32[4,128,128]{1,2,0:T(8,128)S(1)}, u32[]{:S(2)}, u32[]{:S(2)}) collective-permute-start(f32[4,128,128]{1,2,0:T(8,128)S(1)} %get-tuple-element.37), channel_id=1, source_target_pairs={{0,0},{1,224},{2,192},{3,160},{4,164},{5,196},{6,228},{7,4},{8,8},... | collective-permute-start | bytes 786440 | tf_op jit(solution)/shard_map/ppermute | solution.py:148
  375.8 16.5 %collective-permute-start.10 = (f32[4,128]{1,0:T(4,128)S(1)}, f32[4,128]{1,0:T(4,128)S(1)}, u32[]{:S(2)}, u32[]{:S(2)}) collective-permute-start(f32[4,128]{1,0:T(4,128)S(1)} %reduce_sum.32), channel_id=1, source_target_pairs={{0,3},{1,227},{2,195},{3,163},{4,167},{5,199},{6,231},{7,7},{8,11}... | collective-permute-start | bytes 6152 | tf_op jit(solution)/shard_map/ppermute | solution.py:149
  376.4 15.9 %collective-permute-start.9 = (f32[4,128]{1,0:T(4,128)S(1)}, f32[4,128]{1,0:T(4,128)S(1)}, u32[]{:S(2)}, u32[]{:S(2)}) collective-permute-start(f32[4,128]{1,0:T(4,128)S(1)} %reduce_sum.32), channel_id=1, source_target_pairs={{0,2},{1,226},{2,194},{3,162},{4,166},{5,198},{6,230},{7,6},{8,10}... | collective-permute-start | bytes 6152 | tf_op jit(solution)/shard_map/ppermute | solution.py:149
  384.5 8.8 %collective-permute-start.7 = (f32[4,128]{1,0:T(4,128)S(1)}, f32[4,128]{1,0:T(4,128)S(1)}, u32[]{:S(2)}, u32[]{:S(2)}) collective-permute-start(f32[4,128]{1,0:T(4,128)S(1)} %reduce_sum.32), channel_id=1, source_target_pairs={{0,0},{1,224},{2,192},{3,160},{4,164},{5,196},{6,228},{7,4},{8,8},... | collective-permute-start | bytes 6152 | tf_op jit(solution)/shard_map/ppermute | solution.py:149
  390.4 10.6 %collective-permute-start.8 = (f32[4,128]{1,0:T(4,128)S(1)}, f32[4,128]{1,0:T(4,128)S(1)}, u32[]{:S(2)}, u32[]{:S(2)}) collective-permute-start(f32[4,128]{1,0:T(4,128)S(1)} %reduce_sum.32), channel_id=1, source_target_pairs={{0,1},{1,225},{2,193},{3,161},{4,165},{5,197},{6,229},{7,5},{8,9},... | collective-permute-start | bytes 6152 | tf_op jit(solution)/shard_map/ppermute | solution.py:149

commit v4 on v2

--- a/solution.py
+++ b/solution.py
@@ -4,6 +4,8 @@
 from jax import lax
 from jax.sharding import Mesh
 from jax.sharding import PartitionSpec as P
+from jax.experimental import pallas as pl
+from jax.experimental.pallas import tpu as pltpu
 
 HORIZONS = 7
 CORE = 2
@@ -37,6 +39,42 @@
                         perm_in.append((src, me))
                         perm_out.append((me, flat(z // ZL, z % ZL, y, c, k)))
     return zsrc, group_of, pos_of, perm_in, perm_out
+
+
+def step_kernel(take_ref, send_ref, arrived_ref, coefs_ref, sq_ref, present_ref, sq_out_ref, out_ref):
+    blk_dev, lags = coefs_ref.shape[0], coefs_ref.shape[1]
+    for r in range(blk_dev):
+        def body(l, acc):
+            blk = arrived_ref[take_ref[r * lags + l]]
+            return acc + jnp.dot(coefs_ref[r, l], blk, preferred_element_type=jnp.float32)
+        acc = lax.fori_loop(0, lags, body, jnp.zeros(present_ref.shape[1:], jnp.float32))
+        rounded = acc.astype(jnp.bfloat16)
+        present_ref[r] = rounded
+        wide = rounded.astype(jnp.float32)
+        sq_out_ref[r] = sq_ref[r] + wide * wide
+
+    def send(v, carry):
+        out_ref[v] = present_ref[send_ref[v]]
+        return carry
+    lax.fori_loop(0, out_ref.shape[0], send, 0)
+
+def step(take, send, arrived, coefs, squares):
+    blk_dev, lags, bs, _ = coefs.shape
+    cols = arrived.shape[2]
+    n_out = send.shape[0]
+    smem = pl.BlockSpec(memory_space=pltpu.SMEM)
+    vmem = pl.BlockSpec(memory_space=pltpu.VMEM)
+    return pl.pallas_call(
+        step_kernel,
+        out_shape=(
+            jax.ShapeDtypeStruct((blk_dev, bs, cols), jnp.bfloat16),
+            jax.ShapeDtypeStruct((blk_dev, bs, cols), jnp.float32),
+            jax.ShapeDtypeStruct((n_out, bs, cols), jnp.bfloat16),
+        ),
+        in_specs=[smem, smem, vmem, vmem, vmem],
+        out_specs=(vmem, vmem, vmem),
+        input_output_aliases={4: 1},
+    )(take, send, arrived, coefs, squares)
 
 
 def gather_rows(chosen, chosen_idio, owners):
@@ -115,23 +153,13 @@
         send_need = jnp.any(reader_slots[:, :, None] == own_ids[None, None, :], axis=1).astype(
             jnp.int32
         )
-        send_before = jnp.cumsum(send_need, axis=1) - send_need
-        cap_pos = jnp.arange(capacity, dtype=jnp.int32)
-        routing_matrix = (
-            (send_need[:, None, :] == 1) & (send_before[:, None, :] == cap_pos[None, :, None])
-        ).astype(jnp.bfloat16)
-        for step in range(HORIZONS - 1):
-            outgoing = jnp.einsum(
-                "vwq,qfn->vwfn", routing_matrix, present_response, preferred_element_type=jnp.float32
-            ).astype(jnp.bfloat16)
+        send_idx = jnp.argmax(send_need, axis=1).astype(jnp.int32)
+        outgoing = jnp.take(present_response, send_idx, axis=0)
+        for step_no in range(HORIZONS - 1):
             arriving_response = lax.all_to_all(outgoing, BOX, split_axis=0, concat_axis=0, tiled=True)
-            stacked = arriving_response.reshape(owners * capacity, block_size, shock_columns)
-            lagged = jnp.take(stacked, take_index, axis=0).reshape(
-                blk_dev, lags, block_size, shock_columns
+            present_response, squared_terms, outgoing = step(
+                take_index, send_idx, arriving_response, coefs, squared_terms
             )
-            product = jnp.einsum("rlij,rljs->ris", coefs, lagged, preferred_element_type=jnp.float32)
-            present_response = product.astype(jnp.bfloat16)
-            squared_terms = squared_terms + present_response.astype(jnp.float32) ** 2
         partial = jnp.sum(squared_terms, axis=2)
         squared_terms, partial = lax.ppermute((squared_terms, partial), ALL, perm_out)
         totals = lax.psum(partial, "x")

time: 365 us -> 403 us (1.10)
  Pallas kernels: 0 us -> 78.9 us
  local copies, waits for them, and re-layouts: 41.7 us -> 9.91 us
  matrix products: 10.8 us -> 0.91 us
  blocking collectives: 202 us -> 211 us
  other arithmetic: 13.3 us -> 6.94 us
    pallas_call x0 -> x6, Pallas kernels: none -> 78.9 us  [step(): pl.pallas_call(step_kernel, out_shape=(jax.ShapeDtypeStruct((blk_dev, bs,...]
    gather x6 -> x1, local copies, waits for them, and re-layouts: 22.2 us -> 0.96 us  [on_device(): outgoing = jnp.take(present_response, send_idx, axis=0)]
    convert_element_type x11 -> x1, local copies, waits for them, and re-layouts: 10.1 us -> 0.12 us  [on_device(): impact.astype(jnp.bfloat16).reshape(blk_dev, block_size, shock_columns)]
    dot_general x12 -> x0, matrix products: 9.86 us -> none  [the longest x6 5.27 us: on_device(): jnp.einsum('rlij,rljs->ris', coefs, lagged, preferred_element_type=jnp.fl...]
    select_n x8 -> x3, other arithmetic: 11.7 us -> 2.29 us  [the longest x2 1.59 us: on_device(): outgoing = jnp.take(present_response, send_idx, axis=0)]
    all_to_all x5, blocking collectives: 173 us -> 181 us  [on_device(): lax.all_to_all(outgoing, BOX, split_axis=0, concat_axis=0, tiled=True)]
  transfers between devices with their start and end apart: 8 -> 8, of which waited for: 4 -> 4; matrix products, arithmetic and copies ran while one was open for 4% -> 3% of each run, Pallas kernels for 0% -> 0%
where the time goes in v4:
time: 403 us; the launch traced here: 400 us
  blocking collectives  211 us (52%)
  Pallas kernels  78.9 us (20%)
  waiting for transfers between devices  57.5 us (14%)
  starting transfers between devices  33.5 us (8%)
  local copies, waits for them, and re-layouts  9.91 us (2%)
  other arithmetic  6.94 us (2%)
    all_to_all x5, blocking collectives, on_device(): lax.all_to_all(outgoing, BOX, split_axis=0, concat_axis=0, tiled=True)  181 us
    pallas_call x6, Pallas kernels, step(): pl.pallas_call(step_kernel, out_shape=(jax.ShapeDtypeStruct((blk_dev, bs,...  78.9 us
    all_to_all x1, waiting for transfers between devices, on_device(): lax.all_to_all(outgoing, BOX, split_axis=0, concat_axis=0, tiled=True)  40.5 us
    all_gather x1, blocking collectives, on_device(): all_shocks = lax.all_gather(shocked, 'x', axis=0, tiled=True)  15.8 us
    psum x1, blocking collectives, on_device(): totals = lax.psum(partial, 'x')  14.3 us
    ppermute x2, starting transfers between devices, on_device(): lax.ppermute((squared_terms, partial), ALL, perm_out)  8.76 us
  transfers between devices with their start and end apart: 8, of which 4 were waited for; matrix products, arithmetic and copies ran while one was open for 3% of the time, Pallas kernels for 0%

profile of v4, /device:TPU:96, one launch (start us, length us, event | category | flops | bytes accessed | tf_op | source)
XLA Modules:
  0.0 399.6 jit_solution(15439931444332693837)
XLA Ops:
  0.0 1.3 collective-permute-start.1
  1.3 1.6 collective-permute-start
  2.9 1.3 dynamic_slice.15
  4.9 0.8 copy.42
  5.7 0.8 constant_dynamic-slice_fusion.2
  6.5 0.1 copy.40
  6.5 0.1 reshape.225
  6.6 0.7 fusion.15
  7.3 0.1 reshape.226
  7.4 0.6 gather_fusion.3
  8.0 0.2 compare_reduce_fusion
  8.2 0.5 iota_reduce_fusion
  8.8 15.8 %all-gather = s32[4,1,128]{2,1,0:T(1,128)S(1)} all-gather(s32[1,1,128]{2,1,0:T(1,128)} %bitcast.47), channel_id=1, replica_groups=mesh['zh'=4,'zl'=2,'y'=4,'c'=2,'x'=4] {'x'}, dimensions={0}, use_global_device_ids=true | all-gather | bytes 2560 | tf_op jit(solution)/shard_map/all_gather | solution.py:117
  24.6 0.1 dynamic_slice.19
  24.7 0.2 convolution_bitcast_fusion.1
  24.9 0.2 reshape.228
  25.1 0.0 collective-permute-done
  25.2 0.3 fusion.4
  25.5 0.7 pad_maximum_fusion
  26.2 6.8 %all-to-all-start = ((f32[64,3,128]{2,1,0:T(4,128)}), f32[64,3,128]{2,1,0:T(4,128)S(1)}, u32[]{:S(2)}, u32[]{:S(2)}) async-start(f32[64,3,128]{2,1,0:T(4,128)} %pad_maximum_fusion), calls=%async_computation | async-start | bytes 262144 | tf_op jit(solution)/shard_map/all_to_all | solution.py:90
  33.1 7.2 %all-to-all-done = f32[64,3,128]{2,1,0:T(4,128)S(1)} async-done(((f32[64,3,128]{2,1,0:T(4,128)}), f32[64,3,128]{2,1,0:T(4,128)S(1)}, u32[]{:S(2)}, u32[]{:S(2)}) %all-to-all-start) | async-done | bytes 98336 | tf_op jit(solution)/shard_map/all_to_all | solution.py:90
  40.3 0.1 reduce_sum.29
  40.4 0.7 broadcast_in_dim.12
  41.0 5.9 %all-to-all-start.1 = ((f32[64,3,128]{2,1,0:T(4,128)}), f32[64,3,128]{2,1,0:T(4,128)S(1)}, u32[]{:S(2)}, u32[]{:S(2)}) async-start(f32[64,3,128]{2,1,0:T(4,128)} %broadcast_in_dim.12), calls=%async_computation.1 | async-start | bytes 262144 | tf_op jit(solution)/shard_map/all_to_all | solution.py:93
  47.0 7.2 %all-to-all-done.1 = f32[64,3,128]{2,1,0:T(4,128)S(1)} async-done(((f32[64,3,128]{2,1,0:T(4,128)}), f32[64,3,128]{2,1,0:T(4,128)S(1)}, u32[]{:S(2)}, u32[]{:S(2)}) %all-to-all-start.1) | async-done | bytes 98336 | tf_op jit(solution)/shard_map/all_to_all | solution.py:93
  54.2 0.1 slice_reduce_fusion
  54.3 0.1 reshape_squeeze.3
  54.5 0.1 fusion.10
  54.6 0.1 copy.46
  54.7 0.1 reduce_sum.31
  54.8 0.4 fusion.2
  55.2 0.1 copy.47
  55.3 1.0 gather_fusion.4
  56.3 1.6 broadcast_select_fusion
  57.9 6.8 %all-to-all-start.2 = ((bf16[64,128,128]{2,1,0:T(8,128)(2,1)}), bf16[64,128,128]{2,1,0:T(8,128)(2,1)}, u32[]{:S(2)}, u32[]{:S(2)}) async-start(bf16[64,128,128]{2,1,0:T(8,128)(2,1)} %broadcast_select_fusion), calls=%async_computation.2 | async-start | bytes 4194304 | tf_op jit(solution)/shard_map/all_to_all | solution.py:159
  64.7 2.3 collective-permute-start.2
  67.0 0.1 eq.52
  67.1 0.1 fusion.11
  67.2 0.1 reshape.232
  67.3 0.6 gather_fusion
  67.9 0.2 reduce_window_sum.11
  68.1 0.1 add.164
  68.2 0.7 fusion.14
  68.9 0.8 gather_fusion.1
  69.7 1.3 gather_fusion.2
  71.0 0.7 convert_multiply_fusion.sq_ref
  71.7 40.5 %all-to-all-done.2.arrived_ref = bf16[64,128,128]{2,1,0:T(8,128)(2,1)} async-done(((bf16[64,128,128]{2,1,0:T(8,128)(2,1)}), bf16[64,128,128]{2,1,0:T(8,128)(2,1)}, u32[]{:S(2)}, u32[]{:S(2)}) %all-to-all-start.2) | async-done | bytes 2097184 | tf_op jit(solution)/shard_map/all_to_all | solution.py:159
  112.2 13.2 %shard_map.82 = (bf16[4,128,128]{2,1,0:T(8,128)(2,1)}, f32[4,128,128]{2,1,0:T(8,128)}, bf16[64,128,128]{2,1,0:T(8,128)(2,1)}) custom-call(s32[64]{0:T(128)} %gather_fusion.2, s32[64]{0:T(128)} %copy-done.1, bf16[64,128,128]{2,1,0:T(8,128)(2,1)} %all-to-all-done.2.arrived_ref, bf16[4,16,128,128]{3,2,1,0:T(8,128)(2,1)} %copy-done, ...), custom_call_target="tpu_custom_call", output_to_operand_aliasing={{1}: (4, {})} | custom-call | tf_op jit(solution)/shard_map/pallas_call | solution.py:67
  125.3 43.2 %all_to_all.40.arrived_ref = bf16[64,128,128]{2,1,0:T(8,128)(2,1)} all-to-all(bf16[64,128,128]{2,1,0:T(8,128)(2,1)} %get-tuple-element.18), channel_id=1, replica_groups=mesh['zh'=4,'zl'=2,'y'=4,'c'=2,'x'=4] {'zl','y','c','x'}, dimensions={0} | all-to-all | bytes 4194304 | tf_op jit(solution)/shard_map/all_to_all | solution.py:159
  168.5 13.2 %shard_map.83 = (bf16[4,128,128]{2,1,0:T(8,128)(2,1)}, f32[4,128,128]{2,1,0:T(8,128)}, bf16[64,128,128]{2,1,0:T(8,128)(2,1)}) custom-call(s32[64]{0:T(128)} %gather_fusion.2, s32[64]{0:T(128)} %copy-done.1, bf16[64,128,128]{2,1,0:T(8,128)(2,1)} %all_to_all.40.arrived_ref, bf16[4,16,128,128]{3,2,1,0:T(8,128)(2,1)} %copy-done, ...), custom_call_target="tpu_custom_call", output_to_operand_aliasing={{1}: (4, {})} | custom-call | tf_op jit(solution)/shard_map/pallas_call | solution.py:67
  181.7 34.4 %all_to_all.41.arrived_ref = bf16[64,128,128]{2,1,0:T(8,128)(2,1)} all-to-all(bf16[64,128,128]{2,1,0:T(8,128)(2,1)} %get-tuple-element.20), channel_id=1, replica_groups=mesh['zh'=4,'zl'=2,'y'=4,'c'=2,'x'=4] {'zl','y','c','x'}, dimensions={0} | all-to-all | bytes 4194304 | tf_op jit(solution)/shard_map/all_to_all | solution.py:159
  216.1 13.2 %shard_map.84 = (bf16[4,128,128]{2,1,0:T(8,128)(2,1)}, f32[4,128,128]{2,1,0:T(8,128)}, bf16[64,128,128]{2,1,0:T(8,128)(2,1)}) custom-call(s32[64]{0:T(128)} %gather_fusion.2, s32[64]{0:T(128)} %copy-done.1, bf16[64,128,128]{2,1,0:T(8,128)(2,1)} %all_to_all.41.arrived_ref, bf16[4,16,128,128]{3,2,1,0:T(8,128)(2,1)} %copy-done, ...), custom_call_target="tpu_custom_call", output_to_operand_aliasing={{1}: (4, {})} | custom-call | tf_op jit(solution)/shard_map/pallas_call | solution.py:67
  229.2 34.4 %all_to_all.42.arrived_ref = bf16[64,128,128]{2,1,0:T(8,128)(2,1)} all-to-all(bf16[64,128,128]{2,1,0:T(8,128)(2,1)} %get-tuple-element.22), channel_id=1, replica_groups=mesh['zh'=4,'zl'=2,'y'=4,'c'=2,'x'=4] {'zl','y','c','x'}, dimensions={0} | all-to-all | bytes 4194304 | tf_op jit(solution)/shard_map/all_to_all | solution.py:159
  263.7 13.2 %shard_map.85 = (bf16[4,128,128]{2,1,0:T(8,128)(2,1)}, f32[4,128,128]{2,1,0:T(8,128)}, bf16[64,128,128]{2,1,0:T(8,128)(2,1)}) custom-call(s32[64]{0:T(128)} %gather_fusion.2, s32[64]{0:T(128)} %copy-done.1, bf16[64,128,128]{2,1,0:T(8,128)(2,1)} %all_to_all.42.arrived_ref, bf16[4,16,128,128]{3,2,1,0:T(8,128)(2,1)} %copy-done, ...), custom_call_target="tpu_custom_call", output_to_operand_aliasing={{1}: (4, {})} | custom-call | tf_op jit(solution)/shard_map/pallas_call | solution.py:67
  276.8 34.4 %all_to_all.43.arrived_ref = bf16[64,128,128]{2,1,0:T(8,128)(2,1)} all-to-all(bf16[64,128,128]{2,1,0:T(8,128)(2,1)} %get-tuple-element.24), channel_id=1, replica_groups=mesh['zh'=4,'zl'=2,'y'=4,'c'=2,'x'=4] {'zl','y','c','x'}, dimensions={0} | all-to-all | bytes 4194304 | tf_op jit(solution)/shard_map/all_to_all | solution.py:159
  311.2 13.2 %shard_map.86 = (bf16[4,128,128]{2,1,0:T(8,128)(2,1)}, f32[4,128,128]{2,1,0:T(8,128)}, bf16[64,128,128]{2,1,0:T(8,128)(2,1)}) custom-call(s32[64]{0:T(128)} %gather_fusion.2, s32[64]{0:T(128)} %copy-done.1, bf16[64,128,128]{2,1,0:T(8,128)(2,1)} %all_to_all.43.arrived_ref, bf16[4,16,128,128]{3,2,1,0:T(8,128)(2,1)} %copy-done, ...), custom_call_target="tpu_custom_call", output_to_operand_aliasing={{1}: (4, {})} | custom-call | tf_op jit(solution)/shard_map/pallas_call | solution.py:67
  324.4 34.4 %all_to_all.44.arrived_ref = bf16[64,128,128]{2,1,0:T(8,128)(2,1)} all-to-all(bf16[64,128,128]{2,1,0:T(8,128)(2,1)} %get-tuple-element.26), channel_id=1, replica_groups=mesh['zh'=4,'zl'=2,'y'=4,'c'=2,'x'=4] {'zl','y','c','x'}, dimensions={0} | all-to-all | bytes 4194304 | tf_op jit(solution)/shard_map/all_to_all | solution.py:159
  358.8 13.2 %shard_map.87 = (bf16[4,128,128]{2,1,0:T(8,128)(2,1)}, f32[4,128,128]{2,1,0:T(8,128)}, bf16[64,128,128]{2,1,0:T(8,128)(2,1)}) custom-call(s32[64]{0:T(128)} %gather_fusion.2, s32[64]{0:T(128)} %copy-done.1, bf16[64,128,128]{2,1,0:T(8,128)(2,1)} %all_to_all.44.arrived_ref, bf16[4,16,128,128]{3,2,1,0:T(8,128)(2,1)} %copy-done, ...), custom_call_target="tpu_custom_call", output_to_operand_aliasing={{1}: (4, {})} | custom-call | tf_op jit(solution)/shard_map/pallas_call | solution.py:67
  371.9 2.3 collective-permute-start.3
  374.2 1.1 reduce_sum.32
  375.3 6.5 %collective-permute-start.4 = (f32[4,128]{1,0:T(4,128)S(1)}, f32[4,128]{1,0:T(4,128)S(1)}, u32[]{:S(2)}, u32[]{:S(2)}) collective-permute-start(f32[4,128]{1,0:T(4,128)S(1)} %reduce_sum.32), channel_id=1, source_target_pairs={{0,0},{1,224},{2,192},{3,160},{4,164},{5,196},{6,228},{7,4},{8,8},... | collective-permute-start | bytes 6152 | tf_op jit(solution)/shard_map/ppermute | solution.py:164
  381.8 2.6 collective-permute-done.4
  384.4 14.3 %psum.7 = f32[4,128]{1,0:T(4,128)S(1)} all-reduce(f32[4,128]{1,0:T(4,128)S(1)} %collective-permute-done.4), channel_id=1, replica_groups=mesh['zh'=4,'zl'=2,'y'=4,'c'=2,'x'=4] {'x'}, use_global_device_ids=true, to_apply=%region_7.8 | all-reduce | flops 512 | bytes 4096 | tf_op jit(solution)/shard_map/psum | solution.py:165
  398.7 0.8 multiply_divide_fusion
  (22 shorter events, 0.1 us)
Async XLA Ops:
  0.0 24.7 %collective-permute-start.1 = (f32[512]{0:T(512)}, f32[512]{0:T(512)S(1)}, u32[]{:S(2)}, u32[]{:S(2)}) collective-permute-start(f32[512]{0:T(512)} %param.11), channel_id=1, source_target_pairs={{0,0},{225,1},{194,2},{163,3},{164,4},{197,5},{230,6},{7,7},{8,8},... | collective-permute-start | bytes 6152 | tf_op jit(solution)/shard_map/ppermute | solution.py:101
  1.3 23.8 %collective-permute-start = (f32[512,128]{1,0:T(8,128)}, f32[512,128]{1,0:T(8,128)S(1)}, u32[]{:S(2)}, u32[]{:S(2)}) collective-permute-start(f32[512,128]{1,0:T(8,128)} %param.10), channel_id=1, source_target_pairs={{0,0},{225,1},{194,2},{163,3},{164,4},{197,5},{230,6},{7,7},{8,8},... | collective-permute-start | bytes 786440 | tf_op jit(solution)/shard_map/ppermute | solution.py:101
  8.8 47.5 %copy-start.1 = (s32[64]{0:T(128)}, s32[64]{0:T(128)S(1)}, u32[]{:S(2)}) copy-start(s32[64]{0:T(128)S(1)} %get-tuple-element.17.send_ref) | copy-start | bytes 772
  26.2 14.1 %all-to-all-start = ((f32[64,3,128]{2,1,0:T(4,128)}), f32[64,3,128]{2,1,0:T(4,128)S(1)}, u32[]{:S(2)}, u32[]{:S(2)}) async-start(f32[64,3,128]{2,1,0:T(4,128)} %pad_maximum_fusion), calls=%async_computation | async-start | bytes 262144 | tf_op jit(solution)/shard_map/all_to_all | solution.py:90
  41.0 13.2 %all-to-all-start.1 = ((f32[64,3,128]{2,1,0:T(4,128)}), f32[64,3,128]{2,1,0:T(4,128)S(1)}, u32[]{:S(2)}, u32[]{:S(2)}) async-start(f32[64,3,128]{2,1,0:T(4,128)} %broadcast_in_dim.12), calls=%async_computation.1 | async-start | bytes 262144 | tf_op jit(solution)/shard_map/all_to_all | solution.py:93
  57.9 54.2 %all-to-all-start.2 = ((bf16[64,128,128]{2,1,0:T(8,128)(2,1)}), bf16[64,128,128]{2,1,0:T(8,128)(2,1)}, u32[]{:S(2)}, u32[]{:S(2)}) async-start(bf16[64,128,128]{2,1,0:T(8,128)(2,1)} %broadcast_select_fusion), calls=%async_computation.2 | async-start | bytes 4194304 | tf_op jit(solution)/shard_map/all_to_all | solution.py:159
  64.7 7.0 %collective-permute-start.2 = (bf16[4,16,128,128]{3,2,1,0:T(8,128)(2,1)}, bf16[4,16,128,128]{3,2,1,0:T(8,128)(2,1)S(1)}, u32[]{:S(2)}, u32[]{:S(2)}) collective-permute-start(bf16[4,16,128,128]{3,2,1,0:T(8,128)(2,1)} %param.8), channel_id=1, source_target_pairs={{0,0},{225,1},{194,2},{163,3},{164,4},{197,5},{230,6},{7,7},{8,8},... | collective-permute-start | bytes 6291464 | tf_op jit(solution)/shard_map/ppermute | solution.py:102
  71.7 40.5 %copy-start = (bf16[4,16,128,128]{3,2,1,0:T(8,128)(2,1)}, bf16[4,16,128,128]{3,2,1,0:T(8,128)(2,1)S(1)}, u32[]{:S(2)}) copy-start(bf16[4,16,128,128]{3,2,1,0:T(8,128)(2,1)S(1)} %collective-permute-done.2.coefs_ref) | copy-start | bytes 6291460
  371.9 26.8 %collective-permute-start.3 = (f32[4,128,128]{2,1,0:T(8,128)}, f32[4,128,128]{2,1,0:T(8,128)S(1)}, u32[]{:S(2)}, u32[]{:S(2)}) collective-permute-start(f32[4,128,128]{2,1,0:T(8,128)} %get-tuple-element.28), channel_id=1, source_target_pairs={{0,0},{1,224},{2,192},{3,160},{4,164},{5,196},{6,228},{7,4},{8,8},... | collective-permute-start | bytes 786440 | tf_op jit(solution)/shard_map/ppermute | solution.py:164
  375.3 9.1 %collective-permute-start.4 = (f32[4,128]{1,0:T(4,128)S(1)}, f32[4,128]{1,0:T(4,128)S(1)}, u32[]{:S(2)}, u32[]{:S(2)}) collective-permute-start(f32[4,128]{1,0:T(4,128)S(1)} %reduce_sum.32), channel_id=1, source_target_pairs={{0,0},{1,224},{2,192},{3,160},{4,164},{5,196},{6,228},{7,4},{8,8},... | collective-permute-start | bytes 6152 | tf_op jit(solution)/shard_map/ppermute | solution.py:164

commit v5 on v4

--- a/solution.py
+++ b/solution.py
@@ -41,29 +41,33 @@
     return zsrc, group_of, pos_of, perm_in, perm_out
 
 
-def step_kernel(take_ref, send_ref, arrived_ref, coefs_ref, sq_ref, present_ref, sq_out_ref, out_ref):
-    blk_dev, lags = coefs_ref.shape[0], coefs_ref.shape[1]
+def step_kernel(take_ref, send_ref, arrived_ref, coefs_ref, sq_ref, present_ref, sq_out_ref, out_hbm, lag_buf, sems):
+    blk_dev, bs = coefs_ref.shape[0], coefs_ref.shape[1]
+    lags = coefs_ref.shape[2] // bs
     for r in range(blk_dev):
-        def body(l, acc):
-            blk = arrived_ref[take_ref[r * lags + l]]
-            return acc + jnp.dot(coefs_ref[r, l], blk, preferred_element_type=jnp.float32)
-        acc = lax.fori_loop(0, lags, body, jnp.zeros(present_ref.shape[1:], jnp.float32))
+        for l in range(lags):
+            lag_buf[l * bs:(l + 1) * bs, :] = arrived_ref[take_ref[r * lags + l]]
+        acc = jnp.dot(coefs_ref[r], lag_buf[...], preferred_element_type=jnp.float32)
         rounded = acc.astype(jnp.bfloat16)
         present_ref[r] = rounded
         wide = rounded.astype(jnp.float32)
         sq_out_ref[r] = sq_ref[r] + wide * wide
+    copies = []
+    for v in range(out_hbm.shape[0]):
+        cp = pltpu.make_async_copy(present_ref.at[send_ref[v]], out_hbm.at[v], sems.at[v])
+        cp.start()
+        copies.append(cp)
+    for cp in copies:
+        cp.wait()
 
-    def send(v, carry):
-        out_ref[v] = present_ref[send_ref[v]]
-        return carry
-    lax.fori_loop(0, out_ref.shape[0], send, 0)
 
-def step(take, send, arrived, coefs, squares):
-    blk_dev, lags, bs, _ = coefs.shape
+def step(take, send, arrived, coefs_wide, squares):
+    blk_dev, bs, width = coefs_wide.shape
     cols = arrived.shape[2]
     n_out = send.shape[0]
     smem = pl.BlockSpec(memory_space=pltpu.SMEM)
     vmem = pl.BlockSpec(memory_space=pltpu.VMEM)
+    hbm = pl.BlockSpec(memory_space=pl.ANY)
     return pl.pallas_call(
         step_kernel,
         out_shape=(
@@ -72,9 +76,13 @@
             jax.ShapeDtypeStruct((n_out, bs, cols), jnp.bfloat16),
         ),
         in_specs=[smem, smem, vmem, vmem, vmem],
-        out_specs=(vmem, vmem, vmem),
+        out_specs=(vmem, vmem, hbm),
+        scratch_shapes=[
+            pltpu.VMEM((width, cols), jnp.bfloat16),
+            pltpu.SemaphoreType.DMA((n_out,)),
+        ],
         input_output_aliases={4: 1},
-    )(take, send, arrived, coefs, squares)
+    )(take, send, arrived, coefs_wide, squares)
 
 
 def gather_rows(chosen, chosen_idio, owners):
@@ -155,10 +163,11 @@
         )
         send_idx = jnp.argmax(send_need, axis=1).astype(jnp.int32)
         outgoing = jnp.take(present_response, send_idx, axis=0)
+        coefs_wide = coefs.transpose(0, 2, 1, 3).reshape(blk_dev, block_size, lags * block_size)
         for step_no in range(HORIZONS - 1):
             arriving_response = lax.all_to_all(outgoing, BOX, split_axis=0, concat_axis=0, tiled=True)
             present_response, squared_terms, outgoing = step(
-                take_index, send_idx, arriving_response, coefs, squared_terms
+                take_index, send_idx, arriving_response, coefs_wide, squared_terms
             )
         partial = jnp.sum(squared_terms, axis=2)
         squared_terms, partial = lax.ppermute((squared_terms, partial), ALL, perm_out)

time: 403 us -> 362 us (0.90)
  Pallas kernels: 78.9 us -> 33.6 us
  waiting for transfers between devices: 57.5 us -> 39.4 us
  starting transfers between devices: 33.5 us -> 47.6 us
  local copies, waits for them, and re-layouts: 9.91 us -> 14.5 us
    pallas_call x6, Pallas kernels: 78.9 us -> 33.6 us  [step(): pl.pallas_call(step_kernel, out_shape=(jax.ShapeDtypeStruct((blk_dev, bs,...]
    all_to_all x1, waiting for transfers between devices: 40.5 us -> 22.4 us  [on_device(): lax.all_to_all(outgoing, BOX, split_axis=0, concat_axis=0, tiled=True)]
    ppermute x1, starting transfers between devices: 2.25 us -> 17.1 us  [on_device(): coefs = lax.ppermute(coefs, ALL, perm_in)]
  transfers between devices with their start and end apart: 8 -> 8, of which waited for: 4 -> 4; matrix products, arithmetic and copies ran while one was open for 3% -> 4% of each run, Pallas kernels for 0% -> 0%
where the time goes in v5:
time: 362 us; the launch traced here: 357 us
  blocking collectives  213 us (59%)
  starting transfers between devices  47.6 us (13%)
  waiting for transfers between devices  39.4 us (11%)
  Pallas kernels  33.6 us (9%)
  local copies, waits for them, and re-layouts  14.5 us (4%)
  other arithmetic  6.9 us (2%)
    all_to_all x5, blocking collectives, on_device(): lax.all_to_all(outgoing, BOX, split_axis=0, concat_axis=0, tiled=True)  183 us
    pallas_call x6, Pallas kernels, step(): pl.pallas_call(step_kernel, out_shape=(jax.ShapeDtypeStruct((blk_dev, bs,...  33.6 us
    all_to_all x1, waiting for transfers between devices, on_device(): lax.all_to_all(outgoing, BOX, split_axis=0, concat_axis=0, tiled=True)  22.4 us
    ppermute x1, starting transfers between devices, on_device(): coefs = lax.ppermute(coefs, ALL, perm_in)  17.1 us
    all_gather x1, blocking collectives, on_device(): all_shocks = lax.all_gather(shocked, 'x', axis=0, tiled=True)  15.8 us
    psum x1, blocking collectives, on_device(): totals = lax.psum(partial, 'x')  14.3 us
    ppermute x2, starting transfers between devices, on_device(): lax.ppermute((squared_terms, partial), ALL, perm_out)  8.78 us
  transfers between devices with their start and end apart: 8, of which 4 were waited for; matrix products, arithmetic and copies ran while one was open for 4% of the time, Pallas kernels for 0%

profile of v5, /device:TPU:96, one launch (start us, length us, event | category | flops | bytes accessed | tf_op | source)
XLA Modules:
  0.0 357.1 jit_solution(6819042476979432300)
XLA Ops:
  0.0 1.3 collective-permute-start.1
  1.3 1.6 collective-permute-start
  2.9 1.3 dynamic_slice.15
  4.9 0.8 copy.46
  5.7 0.8 constant_dynamic-slice_fusion.2
  6.5 0.1 copy.44
  6.5 0.1 reshape.228
  6.6 0.7 fusion.15
  7.3 0.1 reshape.229
  7.4 0.6 gather_fusion.3
  8.0 0.2 compare_reduce_fusion
  8.2 0.5 iota_reduce_fusion
  8.8 15.8 %all-gather = s32[4,1,128]{2,1,0:T(1,128)S(1)} all-gather(s32[1,1,128]{2,1,0:T(1,128)} %bitcast.53), channel_id=1, replica_groups=mesh['zh'=4,'zl'=2,'y'=4,'c'=2,'x'=4] {'x'}, dimensions={0}, use_global_device_ids=true | all-gather | bytes 2560 | tf_op jit(solution)/shard_map/all_gather | solution.py:125
  24.7 0.2 convolution_bitcast_fusion.1
  24.9 0.2 reshape.231
  25.2 0.3 fusion.4
  25.5 0.7 pad_maximum_fusion
  26.2 6.8 %all-to-all-start = ((f32[64,3,128]{2,1,0:T(4,128)}), f32[64,3,128]{2,1,0:T(4,128)S(1)}, u32[]{:S(2)}, u32[]{:S(2)}) async-start(f32[64,3,128]{2,1,0:T(4,128)} %pad_maximum_fusion), calls=%async_computation | async-start | bytes 262144 | tf_op jit(solution)/shard_map/all_to_all | solution.py:98
  33.1 7.2 %all-to-all-done = f32[64,3,128]{2,1,0:T(4,128)S(1)} async-done(((f32[64,3,128]{2,1,0:T(4,128)}), f32[64,3,128]{2,1,0:T(4,128)S(1)}, u32[]{:S(2)}, u32[]{:S(2)}) %all-to-all-start) | async-done | bytes 98336 | tf_op jit(solution)/shard_map/all_to_all | solution.py:98
  40.3 0.1 reduce_sum.29
  40.4 0.7 broadcast_in_dim.12
  41.0 5.9 %all-to-all-start.1 = ((f32[64,3,128]{2,1,0:T(4,128)}), f32[64,3,128]{2,1,0:T(4,128)S(1)}, u32[]{:S(2)}, u32[]{:S(2)}) async-start(f32[64,3,128]{2,1,0:T(4,128)} %broadcast_in_dim.12), calls=%async_computation.1 | async-start | bytes 262144 | tf_op jit(solution)/shard_map/all_to_all | solution.py:101
  47.0 7.2 %all-to-all-done.1 = f32[64,3,128]{2,1,0:T(4,128)S(1)} async-done(((f32[64,3,128]{2,1,0:T(4,128)}), f32[64,3,128]{2,1,0:T(4,128)S(1)}, u32[]{:S(2)}, u32[]{:S(2)}) %all-to-all-start.1) | async-done | bytes 98336 | tf_op jit(solution)/shard_map/all_to_all | solution.py:101
  54.2 0.1 slice_reduce_fusion
  54.3 0.1 reshape_squeeze.3
  54.5 0.1 fusion.10
  54.6 0.1 copy.50
  54.7 0.1 reduce_sum.31
  54.8 0.4 fusion.2
  55.2 0.1 copy.51
  55.3 1.0 gather_fusion.4
  56.3 1.6 broadcast_select_fusion
  57.9 6.0 %all-to-all-start.2 = ((bf16[64,128,128]{2,1,0:T(8,128)(2,1)}), bf16[64,128,128]{2,1,0:T(8,128)(2,1)S(1)}, u32[]{:S(2)}, u32[]{:S(2)}) async-start(bf16[64,128,128]{2,1,0:T(8,128)(2,1)} %broadcast_select_fusion), calls=%async_computation.2 | async-start | bytes 4194304 | tf_op jit(solution)/shard_map/all_to_all | solution.py:168
  63.9 17.1 %collective-permute-start.2 = (bf16[4,16,128,128]{3,2,1,0:T(8,128)(2,1)}, bf16[4,16,128,128]{3,2,1,0:T(8,128)(2,1)}, u32[]{:S(2)}, u32[]{:S(2)}) collective-permute-start(bf16[4,16,128,128]{3,2,1,0:T(8,128)(2,1)} %param.8), channel_id=1, source_target_pairs={{0,0},{225,1},{194,2},{163,3},{164,4},{197,5},{230,6},{7,7},{8,8},... | collective-permute-start | bytes 6291464 | tf_op jit(solution)/shard_map/ppermute | solution.py:110
  81.0 0.1 eq.52
  81.1 0.1 fusion.11
  81.2 0.1 reshape.236
  81.3 0.6 gather_fusion
  81.9 0.2 reduce_window_sum.11
  82.1 0.1 add.164
  82.2 0.7 fusion.14
  82.9 0.8 gather_fusion.1
  83.7 1.3 gather_fusion.2
  85.0 0.7 convert_multiply_fusion.sq_ref
  85.8 3.3 copy_bitcast_fusion.coefs_ref
  89.0 22.4 %all-to-all-done.2.arrived_ref = bf16[64,128,128]{2,1,0:T(8,128)(2,1)S(1)} async-done(((bf16[64,128,128]{2,1,0:T(8,128)(2,1)}), bf16[64,128,128]{2,1,0:T(8,128)(2,1)S(1)}, u32[]{:S(2)}, u32[]{:S(2)}) %all-to-all-start.2) | async-done | bytes 2097184 | tf_op jit(solution)/shard_map/all_to_all | solution.py:168
  111.4 1.3 copy-done
  112.7 5.6 %shard_map.82 = (bf16[4,128,128]{2,1,0:T(8,128)(2,1)}, f32[4,128,128]{2,1,0:T(8,128)}, bf16[64,128,128]{2,1,0:T(8,128)(2,1)}) custom-call(s32[64]{0:T(128)} %gather_fusion.2, s32[64]{0:T(128)} %copy-done.1, bf16[64,128,128]{2,1,0:T(8,128)(2,1)} %copy-done, bf16[4,128,2048]{2,1,0:T(8,128)(2,1)} %copy_bitcast_fusion.coefs_ref, ...), custom_call_target="tpu_custom_call", output_to_operand_aliasing={{1}: (4, {})} | custom-call | tf_op jit(solution)/shard_map/pallas_call | solution.py:71
  118.3 45.2 %all_to_all.40.arrived_ref = bf16[64,128,128]{2,1,0:T(8,128)(2,1)} all-to-all(bf16[64,128,128]{2,1,0:T(8,128)(2,1)} %get-tuple-element.18), channel_id=1, replica_groups=mesh['zh'=4,'zl'=2,'y'=4,'c'=2,'x'=4] {'zl','y','c','x'}, dimensions={0} | all-to-all | bytes 4194304 | tf_op jit(solution)/shard_map/all_to_all | solution.py:168
  163.5 5.6 %shard_map.83 = (bf16[4,128,128]{2,1,0:T(8,128)(2,1)}, f32[4,128,128]{2,1,0:T(8,128)}, bf16[64,128,128]{2,1,0:T(8,128)(2,1)}) custom-call(s32[64]{0:T(128)} %gather_fusion.2, s32[64]{0:T(128)} %copy-done.1, bf16[64,128,128]{2,1,0:T(8,128)(2,1)} %all_to_all.40.arrived_ref, ...), custom_call_target="tpu_custom_call", output_to_operand_aliasing={{1}: (4, {})} | custom-call | tf_op jit(solution)/shard_map/pallas_call | solution.py:71
  169.1 34.4 %all_to_all.41.arrived_ref = bf16[64,128,128]{2,1,0:T(8,128)(2,1)} all-to-all(bf16[64,128,128]{2,1,0:T(8,128)(2,1)} %get-tuple-element.20), channel_id=1, replica_groups=mesh['zh'=4,'zl'=2,'y'=4,'c'=2,'x'=4] {'zl','y','c','x'}, dimensions={0} | all-to-all | bytes 4194304 | tf_op jit(solution)/shard_map/all_to_all | solution.py:168
  203.5 5.6 %shard_map.84 = (bf16[4,128,128]{2,1,0:T(8,128)(2,1)}, f32[4,128,128]{2,1,0:T(8,128)}, bf16[64,128,128]{2,1,0:T(8,128)(2,1)}) custom-call(s32[64]{0:T(128)} %gather_fusion.2, s32[64]{0:T(128)} %copy-done.1, bf16[64,128,128]{2,1,0:T(8,128)(2,1)} %all_to_all.41.arrived_ref, ...), custom_call_target="tpu_custom_call", output_to_operand_aliasing={{1}: (4, {})} | custom-call | tf_op jit(solution)/shard_map/pallas_call | solution.py:71
  209.1 34.6 %all_to_all.42.arrived_ref = bf16[64,128,128]{2,1,0:T(8,128)(2,1)} all-to-all(bf16[64,128,128]{2,1,0:T(8,128)(2,1)} %get-tuple-element.22), channel_id=1, replica_groups=mesh['zh'=4,'zl'=2,'y'=4,'c'=2,'x'=4] {'zl','y','c','x'}, dimensions={0} | all-to-all | bytes 4194304 | tf_op jit(solution)/shard_map/all_to_all | solution.py:168
  243.7 5.6 %shard_map.85 = (bf16[4,128,128]{2,1,0:T(8,128)(2,1)}, f32[4,128,128]{2,1,0:T(8,128)}, bf16[64,128,128]{2,1,0:T(8,128)(2,1)}) custom-call(s32[64]{0:T(128)} %gather_fusion.2, s32[64]{0:T(128)} %copy-done.1, bf16[64,128,128]{2,1,0:T(8,128)(2,1)} %all_to_all.42.arrived_ref, ...), custom_call_target="tpu_custom_call", output_to_operand_aliasing={{1}: (4, {})} | custom-call | tf_op jit(solution)/shard_map/pallas_call | solution.py:71
  249.3 34.4 %all_to_all.43.arrived_ref = bf16[64,128,128]{2,1,0:T(8,128)(2,1)} all-to-all(bf16[64,128,128]{2,1,0:T(8,128)(2,1)} %get-tuple-element.24), channel_id=1, replica_groups=mesh['zh'=4,'zl'=2,'y'=4,'c'=2,'x'=4] {'zl','y','c','x'}, dimensions={0} | all-to-all | bytes 4194304 | tf_op jit(solution)/shard_map/all_to_all | solution.py:168
  283.8 5.6 %shard_map.86 = (bf16[4,128,128]{2,1,0:T(8,128)(2,1)}, f32[4,128,128]{2,1,0:T(8,128)}, bf16[64,128,128]{2,1,0:T(8,128)(2,1)}) custom-call(s32[64]{0:T(128)} %gather_fusion.2, s32[64]{0:T(128)} %copy-done.1, bf16[64,128,128]{2,1,0:T(8,128)(2,1)} %all_to_all.43.arrived_ref, ...), custom_call_target="tpu_custom_call", output_to_operand_aliasing={{1}: (4, {})} | custom-call | tf_op jit(solution)/shard_map/pallas_call | solution.py:71
  289.4 34.4 %all_to_all.44.arrived_ref = bf16[64,128,128]{2,1,0:T(8,128)(2,1)} all-to-all(bf16[64,128,128]{2,1,0:T(8,128)(2,1)} %get-tuple-element.26), channel_id=1, replica_groups=mesh['zh'=4,'zl'=2,'y'=4,'c'=2,'x'=4] {'zl','y','c','x'}, dimensions={0} | all-to-all | bytes 4194304 | tf_op jit(solution)/shard_map/all_to_all | solution.py:168
  323.8 5.6 %shard_map.87 = (bf16[4,128,128]{2,1,0:T(8,128)(2,1)}, f32[4,128,128]{2,1,0:T(8,128)}, bf16[64,128,128]{2,1,0:T(8,128)(2,1)}) custom-call(s32[64]{0:T(128)} %gather_fusion.2, s32[64]{0:T(128)} %copy-done.1, bf16[64,128,128]{2,1,0:T(8,128)(2,1)} %all_to_all.44.arrived_ref, ...), custom_call_target="tpu_custom_call", output_to_operand_aliasing={{1}: (4, {})} | custom-call | tf_op jit(solution)/shard_map/pallas_call | solution.py:71
  329.5 2.3 collective-permute-start.3
  331.7 1.1 reduce_sum.32
  332.9 6.5 %collective-permute-start.4 = (f32[4,128]{1,0:T(4,128)S(1)}, f32[4,128]{1,0:T(4,128)S(1)}, u32[]{:S(2)}, u32[]{:S(2)}) collective-permute-start(f32[4,128]{1,0:T(4,128)S(1)} %reduce_sum.32), channel_id=1, source_target_pairs={{0,0},{1,224},{2,192},{3,160},{4,164},{5,196},{6,228},{7,4},{8,8},... | collective-permute-start | bytes 6152 | tf_op jit(solution)/shard_map/ppermute | solution.py:173
  339.4 2.6 collective-permute-done.4
  342.0 14.3 %psum.7 = f32[4,128]{1,0:T(4,128)S(1)} all-reduce(f32[4,128]{1,0:T(4,128)S(1)} %collective-permute-done.4), channel_id=1, replica_groups=mesh['zh'=4,'zl'=2,'y'=4,'c'=2,'x'=4] {'x'}, use_global_device_ids=true, to_apply=%region_7.8 | all-reduce | flops 512 | bytes 4096 | tf_op jit(solution)/shard_map/psum | solution.py:174
  356.2 0.8 multiply_divide_fusion
  (23 shorter events, 0.2 us)
Async XLA Ops:
  0.0 24.7 %collective-permute-start.1 = (f32[512]{0:T(512)}, f32[512]{0:T(512)S(1)}, u32[]{:S(2)}, u32[]{:S(2)}) collective-permute-start(f32[512]{0:T(512)} %param.11), channel_id=1, source_target_pairs={{0,0},{225,1},{194,2},{163,3},{164,4},{197,5},{230,6},{7,7},{8,8},... | collective-permute-start | bytes 6152 | tf_op jit(solution)/shard_map/ppermute | solution.py:109
  1.3 23.8 %collective-permute-start = (f32[512,128]{1,0:T(8,128)}, f32[512,128]{1,0:T(8,128)S(1)}, u32[]{:S(2)}, u32[]{:S(2)}) collective-permute-start(f32[512,128]{1,0:T(8,128)} %param.10), channel_id=1, source_target_pairs={{0,0},{225,1},{194,2},{163,3},{164,4},{197,5},{230,6},{7,7},{8,8},... | collective-permute-start | bytes 786440 | tf_op jit(solution)/shard_map/ppermute | solution.py:109
  8.8 47.5 %copy-start.1 = (s32[64]{0:T(128)}, s32[64]{0:T(128)S(1)}, u32[]{:S(2)}) copy-start(s32[64]{0:T(128)S(1)} %get-tuple-element.17.send_ref) | copy-start | bytes 772
  26.2 14.1 %all-to-all-start = ((f32[64,3,128]{2,1,0:T(4,128)}), f32[64,3,128]{2,1,0:T(4,128)S(1)}, u32[]{:S(2)}, u32[]{:S(2)}) async-start(f32[64,3,128]{2,1,0:T(4,128)} %pad_maximum_fusion), calls=%async_computation | async-start | bytes 262144 | tf_op jit(solution)/shard_map/all_to_all | solution.py:98
  41.0 13.2 %all-to-all-start.1 = ((f32[64,3,128]{2,1,0:T(4,128)}), f32[64,3,128]{2,1,0:T(4,128)S(1)}, u32[]{:S(2)}, u32[]{:S(2)}) async-start(f32[64,3,128]{2,1,0:T(4,128)} %broadcast_in_dim.12), calls=%async_computation.1 | async-start | bytes 262144 | tf_op jit(solution)/shard_map/all_to_all | solution.py:101
  57.9 53.5 %all-to-all-start.2 = ((bf16[64,128,128]{2,1,0:T(8,128)(2,1)}), bf16[64,128,128]{2,1,0:T(8,128)(2,1)S(1)}, u32[]{:S(2)}, u32[]{:S(2)}) async-start(bf16[64,128,128]{2,1,0:T(8,128)(2,1)} %broadcast_select_fusion), calls=%async_computation.2 | async-start | bytes 4194304 | tf_op jit(solution)/shard_map/all_to_all | solution.py:168
  63.9 21.9 %collective-permute-start.2 = (bf16[4,16,128,128]{3,2,1,0:T(8,128)(2,1)}, bf16[4,16,128,128]{3,2,1,0:T(8,128)(2,1)}, u32[]{:S(2)}, u32[]{:S(2)}) collective-permute-start(bf16[4,16,128,128]{3,2,1,0:T(8,128)(2,1)} %param.8), channel_id=1, source_target_pairs={{0,0},{225,1},{194,2},{163,3},{164,4},{197,5},{230,6},{7,7},{8,8},... | collective-permute-start | bytes 6291464 | tf_op jit(solution)/shard_map/ppermute | solution.py:110
  111.4 1.3 copy-start
  329.5 26.8 %collective-permute-start.3 = (f32[4,128,128]{2,1,0:T(8,128)}, f32[4,128,128]{2,1,0:T(8,128)S(1)}, u32[]{:S(2)}, u32[]{:S(2)}) collective-permute-start(f32[4,128,128]{2,1,0:T(8,128)} %get-tuple-element.28), channel_id=1, source_target_pairs={{0,0},{1,224},{2,192},{3,160},{4,164},{5,196},{6,228},{7,4},{8,8},... | collective-permute-start | bytes 786440 | tf_op jit(solution)/shard_map/ppermute | solution.py:173
  332.9 9.1 %collective-permute-start.4 = (f32[4,128]{1,0:T(4,128)S(1)}, f32[4,128]{1,0:T(4,128)S(1)}, u32[]{:S(2)}, u32[]{:S(2)}) collective-permute-start(f32[4,128]{1,0:T(4,128)S(1)} %reduce_sum.32), channel_id=1, source_target_pairs={{0,0},{1,224},{2,192},{3,160},{4,164},{5,196},{6,228},{7,4},{8,8},... | collective-permute-start | bytes 6152 | tf_op jit(solution)/shard_map/ppermute | solution.py:173

commit v6 on v5

--- a/solution.py
+++ b/solution.py
@@ -38,7 +38,12 @@
                         me = flat(k, zl, y, c, x)
                         perm_in.append((src, me))
                         perm_out.append((me, flat(z // ZL, z % ZL, y, c, k)))
-    return zsrc, group_of, pos_of, perm_in, perm_out
+    perm_x = [
+        [(flat(k, zl, y, c, x), flat(k, zl, y, c, (x + j) % xs)) for k in range(zh) for zl in range(ZL)
+         for y in range(YS) for c in range(CORE) for x in range(xs)]
+        for j in range(xs)
+    ]
+    return zsrc, group_of, pos_of, perm_in, perm_out, perm_x
 
 
 def step_kernel(take_ref, send_ref, arrived_ref, coefs_ref, sq_ref, present_ref, sq_out_ref, out_hbm, lag_buf, sems):
@@ -103,7 +108,7 @@
 
 
 def make_body(zh, xs):
-    zsrc_t, group_t, pos_t, perm_in, perm_out = layout(zh, xs)
+    zsrc_t, group_t, pos_t, perm_in, perm_out, perm_x = layout(zh, xs)
 
     def on_device(coefs, lag_pattern, loadings, idiosyncratic, shocked):
         loadings, idiosyncratic = lax.ppermute((loadings, idiosyncratic), ALL, perm_in)
@@ -122,9 +127,9 @@
         pos_of_group = jnp.asarray(pos_t)[k]
         n_blocks = owners * blk_dev
         capacity = min(blk_dev, max(1, blk_dev * lags // owners))
-        all_shocks = lax.all_gather(shocked, "x", axis=0, tiled=True)
+        shifted = jnp.stack([shocked] + [lax.ppermute(shocked, ALL, perm_x[j]) for j in range(1, xs)])
         shock_columns = shocked.shape[0]
-        shocked = lax.dynamic_slice_in_dim(all_shocks, k * shock_columns, shock_columns, 0)
+        shocked = shifted[(x - k) % xs]
         local_rows = blk_dev * block_size
         row_ids = mine * local_rows + jnp.arange(local_rows, dtype=jnp.int32)
         pick_table = (shocked[:, None] == row_ids[None, :]).astype(jnp.float32)

time: 362 us -> 359 us (level)
  blocking collectives: 213 us -> 196 us
  starting transfers between devices: 47.6 us -> 58.6 us
    all_gather x1 -> x0, blocking collectives: 15.8 us -> none  [on_device(): all_shocks = lax.all_gather(shocked, 'x', axis=0, tiled=True)]
    all_to_all x1, starting transfers between devices: 6.85 us -> 17 us  [gather_rows(): arrived = lax.all_to_all(packed, BOX, 0, 0, tiled=True)]
    ppermute x0 -> x3, starting transfers between devices: none -> 5.05 us  [on_device(): lax.ppermute(shocked, ALL, perm_x[j])]
    ppermute x2, waiting for transfers between devices: 2.61 us -> 6.81 us  [on_device(): lax.ppermute((squared_terms, partial), ALL, perm_out)]
    ppermute x2, starting transfers between devices: 8.78 us -> 4.6 us  [on_device(): lax.ppermute((squared_terms, partial), ALL, perm_out)]
    psum x1, blocking collectives: 14.3 us -> 10.1 us  [on_device(): totals = lax.psum(partial, 'x')]
  transfers between devices with their start and end apart: 8 -> 11, of which waited for: 4 -> 4; matrix products, arithmetic and copies ran while one was open for 4% -> 4% of each run, Pallas kernels for 0% -> 0%
where the time goes in v6:
time: 359 us; the launch traced here: 354 us
  blocking collectives  196 us (55%)
  starting transfers between devices  58.6 us (16%)
  waiting for transfers between devices  41.1 us (11%)
  Pallas kernels  33.6 us (9%)
  local copies, waits for them, and re-layouts  14.4 us (4%)
  other arithmetic  7.57 us (2%)
    all_to_all x5, blocking collectives, on_device(): lax.all_to_all(outgoing, BOX, split_axis=0, concat_axis=0, tiled=True)  186 us
    pallas_call x6, Pallas kernels, step(): pl.pallas_call(step_kernel, out_shape=(jax.ShapeDtypeStruct((blk_dev, bs,...  33.6 us
    all_to_all x1, waiting for transfers between devices, on_device(): lax.all_to_all(outgoing, BOX, split_axis=0, concat_axis=0, tiled=True)  19.9 us
    ppermute x1, starting transfers between devices, on_device(): coefs = lax.ppermute(coefs, ALL, perm_in)  17.1 us
    all_to_all x1, starting transfers between devices, gather_rows(): arrived = lax.all_to_all(packed, BOX, 0, 0, tiled=True)  17 us
    psum x1, blocking collectives, on_device(): totals = lax.psum(partial, 'x')  10.1 us
    all_to_all x1, waiting for transfers between devices, gather_rows(): full = lax.all_to_all(spread, BOX, 0, 0, tiled=True)  7.21 us
    all_to_all x1, waiting for transfers between devices, gather_rows(): arrived = lax.all_to_all(packed, BOX, 0, 0, tiled=True)  7.2 us
  transfers between devices with their start and end apart: 11, of which 4 were waited for; matrix products, arithmetic and copies ran while one was open for 4% of the time, Pallas kernels for 0%

profile of v6, /device:TPU:96, one launch (start us, length us, event | category | flops | bytes accessed | tf_op | source)
XLA Modules:
  0.0 353.8 jit_solution(9709705465790710265)
XLA Ops:
  0.0 1.5 collective-permute-start
  1.5 1.7 collective-permute-start.2
  3.2 1.8 collective-permute-start.1
  5.1 1.3 collective-permute-start.4
  6.4 1.6 collective-permute-start.3
  8.0 1.3 dynamic_slice.15
  9.9 0.8 copy.46
  10.7 0.8 constant_dynamic-slice_fusion.3
  11.6 0.1 reshape.228
  11.7 0.7 fusion.16
  12.4 0.1 reshape.229
  12.5 0.6 gather_fusion.3
  13.1 0.2 compare_reduce_fusion
  13.3 0.5 iota_reduce_fusion
  13.9 0.7 pad_add_fusion
  14.6 0.2 convolution_bitcast_fusion.1
  14.8 0.2 reshape.231
  15.0 0.3 fusion.4
  15.3 0.7 pad_maximum_fusion
  16.0 17.0 %all-to-all-start = ((f32[64,3,128]{2,1,0:T(4,128)}), f32[64,3,128]{2,1,0:T(4,128)S(1)}, u32[]{:S(2)}, u32[]{:S(2)}) async-start(f32[64,3,128]{2,1,0:T(4,128)} %pad_maximum_fusion), calls=%async_computation | async-start | bytes 262144 | tf_op jit(solution)/shard_map/all_to_all | solution.py:103
  33.1 7.2 %all-to-all-done = f32[64,3,128]{2,1,0:T(4,128)S(1)} async-done(((f32[64,3,128]{2,1,0:T(4,128)}), f32[64,3,128]{2,1,0:T(4,128)S(1)}, u32[]{:S(2)}, u32[]{:S(2)}) %all-to-all-start) | async-done | bytes 98336 | tf_op jit(solution)/shard_map/all_to_all | solution.py:103
  40.3 0.7 broadcast_in_dim.12
  41.0 5.9 %all-to-all-start.1 = ((f32[64,3,128]{2,1,0:T(4,128)}), f32[64,3,128]{2,1,0:T(4,128)S(1)}, u32[]{:S(2)}, u32[]{:S(2)}) async-start(f32[64,3,128]{2,1,0:T(4,128)} %broadcast_in_dim.12), calls=%async_computation.1 | async-start | bytes 262144 | tf_op jit(solution)/shard_map/all_to_all | solution.py:106
  47.0 7.2 %all-to-all-done.1 = f32[64,3,128]{2,1,0:T(4,128)S(1)} async-done(((f32[64,3,128]{2,1,0:T(4,128)}), f32[64,3,128]{2,1,0:T(4,128)S(1)}, u32[]{:S(2)}, u32[]{:S(2)}) %all-to-all-start.1) | async-done | bytes 98336 | tf_op jit(solution)/shard_map/all_to_all | solution.py:106
  54.2 0.1 slice_reduce_fusion
  54.3 0.1 reshape_squeeze.3
  54.5 0.1 fusion.10
  54.6 0.1 copy.50
  54.7 0.1 reduce_sum.31
  54.8 0.4 fusion.2
  55.2 0.1 copy.51
  55.3 1.0 gather_fusion.4
  56.3 1.6 broadcast_select_fusion
  57.9 6.0 %all-to-all-start.2 = ((bf16[64,128,128]{2,1,0:T(8,128)(2,1)}), bf16[64,128,128]{2,1,0:T(8,128)(2,1)S(1)}, u32[]{:S(2)}, u32[]{:S(2)}) async-start(bf16[64,128,128]{2,1,0:T(8,128)(2,1)} %broadcast_select_fusion), calls=%async_computation.2 | async-start | bytes 4194304 | tf_op jit(solution)/shard_map/all_to_all | solution.py:173
  63.9 17.1 %collective-permute-start.5 = (bf16[4,16,128,128]{3,2,1,0:T(8,128)(2,1)}, bf16[4,16,128,128]{3,2,1,0:T(8,128)(2,1)}, u32[]{:S(2)}, u32[]{:S(2)}) collective-permute-start(bf16[4,16,128,128]{3,2,1,0:T(8,128)(2,1)} %param.8), channel_id=1, source_target_pairs={{0,0},{225,1},{194,2},{163,3},{164,4},{197,5},{230,6},{7,7},{8,8},... | collective-permute-start | bytes 6291464 | tf_op jit(solution)/shard_map/ppermute | solution.py:115
  81.1 0.1 fusion.11
  81.2 0.1 reshape.236
  81.3 0.6 gather_fusion
  81.9 0.2 reduce_window_sum.11
  82.1 0.1 add.168
  82.2 0.7 fusion.14
  82.9 0.8 gather_fusion.1
  83.7 1.3 gather_fusion.2
  85.0 0.7 convert_multiply_fusion.sq_ref
  85.7 3.3 copy_bitcast_fusion.coefs_ref
  89.0 19.9 %all-to-all-done.2.arrived_ref = bf16[64,128,128]{2,1,0:T(8,128)(2,1)S(1)} async-done(((bf16[64,128,128]{2,1,0:T(8,128)(2,1)}), bf16[64,128,128]{2,1,0:T(8,128)(2,1)S(1)}, u32[]{:S(2)}, u32[]{:S(2)}) %all-to-all-start.2) | async-done | bytes 2097184 | tf_op jit(solution)/shard_map/all_to_all | solution.py:173
  108.9 1.3 copy-done
  110.2 5.6 %shard_map.82 = (bf16[4,128,128]{2,1,0:T(8,128)(2,1)}, f32[4,128,128]{2,1,0:T(8,128)}, bf16[64,128,128]{2,1,0:T(8,128)(2,1)}) custom-call(s32[64]{0:T(128)} %gather_fusion.2, s32[64]{0:T(128)} %copy-done.1, bf16[64,128,128]{2,1,0:T(8,128)(2,1)} %copy-done, bf16[4,128,2048]{2,1,0:T(8,128)(2,1)} %copy_bitcast_fusion.coefs_ref, ...), custom_call_target="tpu_custom_call", output_to_operand_aliasing={{1}: (4, {})} | custom-call | tf_op jit(solution)/shard_map/pallas_call | solution.py:76
  115.8 48.5 %all_to_all.40.arrived_ref = bf16[64,128,128]{2,1,0:T(8,128)(2,1)} all-to-all(bf16[64,128,128]{2,1,0:T(8,128)(2,1)} %get-tuple-element.18), channel_id=1, replica_groups=mesh['zh'=4,'zl'=2,'y'=4,'c'=2,'x'=4] {'zl','y','c','x'}, dimensions={0} | all-to-all | bytes 4194304 | tf_op jit(solution)/shard_map/all_to_all | solution.py:173
  164.3 5.6 %shard_map.83 = (bf16[4,128,128]{2,1,0:T(8,128)(2,1)}, f32[4,128,128]{2,1,0:T(8,128)}, bf16[64,128,128]{2,1,0:T(8,128)(2,1)}) custom-call(s32[64]{0:T(128)} %gather_fusion.2, s32[64]{0:T(128)} %copy-done.1, bf16[64,128,128]{2,1,0:T(8,128)(2,1)} %all_to_all.40.arrived_ref, ...), custom_call_target="tpu_custom_call", output_to_operand_aliasing={{1}: (4, {})} | custom-call | tf_op jit(solution)/shard_map/pallas_call | solution.py:76
  169.9 34.6 %all_to_all.41.arrived_ref = bf16[64,128,128]{2,1,0:T(8,128)(2,1)} all-to-all(bf16[64,128,128]{2,1,0:T(8,128)(2,1)} %get-tuple-element.20), channel_id=1, replica_groups=mesh['zh'=4,'zl'=2,'y'=4,'c'=2,'x'=4] {'zl','y','c','x'}, dimensions={0} | all-to-all | bytes 4194304 | tf_op jit(solution)/shard_map/all_to_all | solution.py:173
  204.5 5.6 %shard_map.84 = (bf16[4,128,128]{2,1,0:T(8,128)(2,1)}, f32[4,128,128]{2,1,0:T(8,128)}, bf16[64,128,128]{2,1,0:T(8,128)(2,1)}) custom-call(s32[64]{0:T(128)} %gather_fusion.2, s32[64]{0:T(128)} %copy-done.1, bf16[64,128,128]{2,1,0:T(8,128)(2,1)} %all_to_all.41.arrived_ref, ...), custom_call_target="tpu_custom_call", output_to_operand_aliasing={{1}: (4, {})} | custom-call | tf_op jit(solution)/shard_map/pallas_call | solution.py:76
  210.1 34.4 %all_to_all.42.arrived_ref = bf16[64,128,128]{2,1,0:T(8,128)(2,1)} all-to-all(bf16[64,128,128]{2,1,0:T(8,128)(2,1)} %get-tuple-element.22), channel_id=1, replica_groups=mesh['zh'=4,'zl'=2,'y'=4,'c'=2,'x'=4] {'zl','y','c','x'}, dimensions={0} | all-to-all | bytes 4194304 | tf_op jit(solution)/shard_map/all_to_all | solution.py:173
  244.5 5.6 %shard_map.85 = (bf16[4,128,128]{2,1,0:T(8,128)(2,1)}, f32[4,128,128]{2,1,0:T(8,128)}, bf16[64,128,128]{2,1,0:T(8,128)(2,1)}) custom-call(s32[64]{0:T(128)} %gather_fusion.2, s32[64]{0:T(128)} %copy-done.1, bf16[64,128,128]{2,1,0:T(8,128)(2,1)} %all_to_all.42.arrived_ref, ...), custom_call_target="tpu_custom_call", output_to_operand_aliasing={{1}: (4, {})} | custom-call | tf_op jit(solution)/shard_map/pallas_call | solution.py:76
  250.1 34.4 %all_to_all.43.arrived_ref = bf16[64,128,128]{2,1,0:T(8,128)(2,1)} all-to-all(bf16[64,128,128]{2,1,0:T(8,128)(2,1)} %get-tuple-element.24), channel_id=1, replica_groups=mesh['zh'=4,'zl'=2,'y'=4,'c'=2,'x'=4] {'zl','y','c','x'}, dimensions={0} | all-to-all | bytes 4194304 | tf_op jit(solution)/shard_map/all_to_all | solution.py:173
  284.5 5.6 %shard_map.86 = (bf16[4,128,128]{2,1,0:T(8,128)(2,1)}, f32[4,128,128]{2,1,0:T(8,128)}, bf16[64,128,128]{2,1,0:T(8,128)(2,1)}) custom-call(s32[64]{0:T(128)} %gather_fusion.2, s32[64]{0:T(128)} %copy-done.1, bf16[64,128,128]{2,1,0:T(8,128)(2,1)} %all_to_all.43.arrived_ref, ...), custom_call_target="tpu_custom_call", output_to_operand_aliasing={{1}: (4, {})} | custom-call | tf_op jit(solution)/shard_map/pallas_call | solution.py:76
  290.2 34.4 %all_to_all.44.arrived_ref = bf16[64,128,128]{2,1,0:T(8,128)(2,1)} all-to-all(bf16[64,128,128]{2,1,0:T(8,128)(2,1)} %get-tuple-element.26), channel_id=1, replica_groups=mesh['zh'=4,'zl'=2,'y'=4,'c'=2,'x'=4] {'zl','y','c','x'}, dimensions={0} | all-to-all | bytes 4194304 | tf_op jit(solution)/shard_map/all_to_all | solution.py:173
  324.6 5.6 %shard_map.87 = (bf16[4,128,128]{2,1,0:T(8,128)(2,1)}, f32[4,128,128]{2,1,0:T(8,128)}, bf16[64,128,128]{2,1,0:T(8,128)(2,1)}) custom-call(s32[64]{0:T(128)} %gather_fusion.2, s32[64]{0:T(128)} %copy-done.1, bf16[64,128,128]{2,1,0:T(8,128)(2,1)} %all_to_all.44.arrived_ref, ...), custom_call_target="tpu_custom_call", output_to_operand_aliasing={{1}: (4, {})} | custom-call | tf_op jit(solution)/shard_map/pallas_call | solution.py:76
  330.2 2.3 collective-permute-start.6
  332.5 1.1 reduce_sum.32
  333.6 2.3 collective-permute-start.7
  336.0 6.8 %collective-permute-done.7 = f32[4,128]{1,0:T(4,128)S(1)} collective-permute-done((f32[4,128]{1,0:T(4,128)S(1)}, f32[4,128]{1,0:T(4,128)S(1)}, u32[]{:S(2)}, u32[]{:S(2)}) %collective-permute-start.7) | collective-permute-done | bytes 2080 | tf_op jit(solution)/shard_map/ppermute | solution.py:178
  342.8 10.1 %psum.7 = f32[4,128]{1,0:T(4,128)S(1)} all-reduce(f32[4,128]{1,0:T(4,128)S(1)} %collective-permute-done.7), channel_id=1, replica_groups=mesh['zh'=4,'zl'=2,'y'=4,'c'=2,'x'=4] {'x'}, use_global_device_ids=true, to_apply=%region_7.8 | all-reduce | flops 512 | bytes 4096 | tf_op jit(solution)/shard_map/psum | solution.py:179
  352.9 0.8 multiply_divide_fusion
  (29 shorter events, 0.4 us)
Async XLA Ops:
  0.0 13.8 %collective-permute-start = (s32[128]{0:T(128)}, s32[128]{0:T(128)S(1)}, u32[]{:S(2)}, u32[]{:S(2)}) collective-permute-start(s32[128]{0:T(128)} %param.12), channel_id=1, source_target_pairs={{0,1},{1,2},{2,3},{3,0},{4,5},{5,6},{6,7},{7,4},{8,9},{9,10},{10,1... | collective-permute-start | bytes 1544 | tf_op jit(solution)/shard_map/ppermute | solution.py:130
  1.5 12.4 %collective-permute-start.2 = (s32[128]{0:T(128)}, s32[128]{0:T(128)S(1)}, u32[]{:S(2)}, u32[]{:S(2)}) collective-permute-start(s32[128]{0:T(128)} %param.12), channel_id=1, source_target_pairs={{0,3},{1,0},{2,1},{3,2},{4,7},{5,4},{6,5},{7,6},{8,11},{9,8},{10,9... | collective-permute-start | bytes 1544 | tf_op jit(solution)/shard_map/ppermute | solution.py:130
  3.2 10.6 %collective-permute-start.1 = (s32[128]{0:T(128)}, s32[128]{0:T(128)S(1)}, u32[]{:S(2)}, u32[]{:S(2)}) collective-permute-start(s32[128]{0:T(128)} %param.12), channel_id=1, source_target_pairs={{0,2},{1,3},{2,0},{3,1},{4,6},{5,7},{6,4},{7,5},{8,10},{9,11},{10,... | collective-permute-start | bytes 1544 | tf_op jit(solution)/shard_map/ppermute | solution.py:130
  5.1 9.5 %collective-permute-start.4 = (f32[512]{0:T(512)}, f32[512]{0:T(512)S(1)}, u32[]{:S(2)}, u32[]{:S(2)}) collective-permute-start(f32[512]{0:T(512)} %param.11), channel_id=1, source_target_pairs={{0,0},{225,1},{194,2},{163,3},{164,4},{197,5},{230,6},{7,7},{8,8},... | collective-permute-start | bytes 6152 | tf_op jit(solution)/shard_map/ppermute | solution.py:114
  6.4 8.6 %collective-permute-start.3 = (f32[512,128]{1,0:T(8,128)}, f32[512,128]{1,0:T(8,128)S(1)}, u32[]{:S(2)}, u32[]{:S(2)}) collective-permute-start(f32[512,128]{1,0:T(8,128)} %param.10), channel_id=1, source_target_pairs={{0,0},{225,1},{194,2},{163,3},{164,4},{197,5},{230,6},{7,7},{8,8},... | collective-permute-start | bytes 786440 | tf_op jit(solution)/shard_map/ppermute | solution.py:114
  13.8 42.5 %copy-start.1 = (s32[64]{0:T(128)}, s32[64]{0:T(128)S(1)}, u32[]{:S(2)}) copy-start(s32[64]{0:T(128)S(1)} %get-tuple-element.17.send_ref) | copy-start | bytes 772
  16.0 24.2 %all-to-all-start = ((f32[64,3,128]{2,1,0:T(4,128)}), f32[64,3,128]{2,1,0:T(4,128)S(1)}, u32[]{:S(2)}, u32[]{:S(2)}) async-start(f32[64,3,128]{2,1,0:T(4,128)} %pad_maximum_fusion), calls=%async_computation | async-start | bytes 262144 | tf_op jit(solution)/shard_map/all_to_all | solution.py:103
  41.0 13.2 %all-to-all-start.1 = ((f32[64,3,128]{2,1,0:T(4,128)}), f32[64,3,128]{2,1,0:T(4,128)S(1)}, u32[]{:S(2)}, u32[]{:S(2)}) async-start(f32[64,3,128]{2,1,0:T(4,128)} %broadcast_in_dim.12), calls=%async_computation.1 | async-start | bytes 262144 | tf_op jit(solution)/shard_map/all_to_all | solution.py:106
  57.9 51.0 %all-to-all-start.2 = ((bf16[64,128,128]{2,1,0:T(8,128)(2,1)}), bf16[64,128,128]{2,1,0:T(8,128)(2,1)S(1)}, u32[]{:S(2)}, u32[]{:S(2)}) async-start(bf16[64,128,128]{2,1,0:T(8,128)(2,1)} %broadcast_select_fusion), calls=%async_computation.2 | async-start | bytes 4194304 | tf_op jit(solution)/shard_map/all_to_all | solution.py:173
  63.9 21.9 %collective-permute-start.5 = (bf16[4,16,128,128]{3,2,1,0:T(8,128)(2,1)}, bf16[4,16,128,128]{3,2,1,0:T(8,128)(2,1)}, u32[]{:S(2)}, u32[]{:S(2)}) collective-permute-start(bf16[4,16,128,128]{3,2,1,0:T(8,128)(2,1)} %param.8), channel_id=1, source_target_pairs={{0,0},{225,1},{194,2},{163,3},{164,4},{197,5},{230,6},{7,7},{8,8},... | collective-permute-start | bytes 6291464 | tf_op jit(solution)/shard_map/ppermute | solution.py:115
  108.9 1.3 copy-start
  330.2 22.7 %collective-permute-start.6 = (f32[4,128,128]{2,1,0:T(8,128)}, f32[4,128,128]{2,1,0:T(8,128)S(1)}, u32[]{:S(2)}, u32[]{:S(2)}) collective-permute-start(f32[4,128,128]{2,1,0:T(8,128)} %get-tuple-element.28), channel_id=1, source_target_pairs={{0,0},{1,224},{2,192},{3,160},{4,164},{5,196},{6,228},{7,4},{8,8},... | collective-permute-start | bytes 786440 | tf_op jit(solution)/shard_map/ppermute | solution.py:178
  333.6 9.1 %collective-permute-start.7 = (f32[4,128]{1,0:T(4,128)S(1)}, f32[4,128]{1,0:T(4,128)S(1)}, u32[]{:S(2)}, u32[]{:S(2)}) collective-permute-start(f32[4,128]{1,0:T(4,128)S(1)} %reduce_sum.32), channel_id=1, source_target_pairs={{0,0},{1,224},{2,192},{3,160},{4,164},{5,196},{6,228},{7,4},{8,8},... | collective-permute-start | bytes 6152 | tf_op jit(solution)/shard_map/ppermute | solution.py:178

commit v7 on v6

--- a/solution.py
+++ b/solution.py
@@ -112,10 +112,11 @@
 
     def on_device(coefs, lag_pattern, loadings, idiosyncratic, shocked):
         loadings, idiosyncratic = lax.ppermute((loadings, idiosyncratic), ALL, perm_in)
-        coefs = lax.ppermute(coefs, ALL, perm_in)
         blk_dev = coefs.shape[0]
         lags = coefs.shape[1]
         block_size = coefs.shape[2]
+        coefs_wide = coefs.transpose(0, 2, 1, 3).reshape(blk_dev, block_size, lags * block_size)
+        coefs_wide = lax.ppermute(coefs_wide, ALL, perm_in)
         k = lax.axis_index("zh")
         zl = lax.axis_index("zl")
         y = lax.axis_index("y")
@@ -168,7 +169,6 @@
         )
         send_idx = jnp.argmax(send_need, axis=1).astype(jnp.int32)
         outgoing = jnp.take(present_response, send_idx, axis=0)
-        coefs_wide = coefs.transpose(0, 2, 1, 3).reshape(blk_dev, block_size, lags * block_size)
         for step_no in range(HORIZONS - 1):
             arriving_response = lax.all_to_all(outgoing, BOX, split_axis=0, concat_axis=0, tiled=True)
             present_response, squared_terms, outgoing = step(

time: 359 us -> 360 us (level)
  no operation moved by 1% of the time
where the time goes in v7:
time: 360 us; the launch traced here: 355 us
  blocking collectives  198 us (55%)
  starting transfers between devices  59.4 us (16%)
  waiting for transfers between devices  39.9 us (11%)
  Pallas kernels  33.7 us (9%)
  local copies, waits for them, and re-layouts  12.7 us (4%)
  other arithmetic  9.21 us (3%)
    all_to_all x5, blocking collectives, on_device(): lax.all_to_all(outgoing, BOX, split_axis=0, concat_axis=0, tiled=True)  188 us
    pallas_call x6, Pallas kernels, step(): pl.pallas_call(step_kernel, out_shape=(jax.ShapeDtypeStruct((blk_dev, bs,...  33.7 us
    all_to_all x1, waiting for transfers between devices, on_device(): lax.all_to_all(outgoing, BOX, split_axis=0, concat_axis=0, tiled=True)  18.6 us
    ppermute x1, starting transfers between devices, on_device(): coefs_wide = lax.ppermute(coefs_wide, ALL, perm_in)  17.1 us
    all_to_all x1, starting transfers between devices, gather_rows(): arrived = lax.all_to_all(packed, BOX, 0, 0, tiled=True)  17 us
    psum x1, blocking collectives, on_device(): totals = lax.psum(partial, 'x')  10.1 us
    all_to_all x1, waiting for transfers between devices, gather_rows(): full = lax.all_to_all(spread, BOX, 0, 0, tiled=True)  7.21 us
    all_to_all x1, waiting for transfers between devices, gather_rows(): arrived = lax.all_to_all(packed, BOX, 0, 0, tiled=True)  7.2 us
  transfers between devices with their start and end apart: 11, of which 4 were waited for; matrix products, arithmetic and copies ran while one was open for 4% of the time, Pallas kernels for 0%

profile of v7, /device:TPU:96, one launch (start us, length us, event | category | flops | bytes accessed | tf_op | source)
XLA Modules:
  0.0 354.6 jit_solution(2430217930671290665)
XLA Ops:
  0.0 1.5 collective-permute-start
  1.5 1.7 collective-permute-start.2
  3.2 1.8 collective-permute-start.1
  5.1 1.3 collective-permute-start.4
  6.4 1.6 collective-permute-start.3
  8.0 1.3 dynamic_slice.15
  9.9 0.8 copy.46
  10.7 0.8 constant_dynamic-slice_fusion.3
  11.5 0.1 copy.44
  11.6 0.1 reshape.228
  11.7 0.7 fusion.16
  12.4 0.1 reshape.229
  12.5 0.6 gather_fusion.3
  13.1 0.2 compare_reduce_fusion
  13.3 0.5 iota_reduce_fusion
  13.9 0.7 pad_add_fusion
  14.6 0.2 convolution_bitcast_fusion.1
  14.8 0.2 reshape.231
  15.0 0.3 fusion.4
  15.3 0.7 pad_maximum_fusion
  16.0 17.0 %all-to-all-start = ((f32[64,3,128]{2,1,0:T(4,128)}), f32[64,3,128]{2,1,0:T(4,128)S(1)}, u32[]{:S(2)}, u32[]{:S(2)}) async-start(f32[64,3,128]{2,1,0:T(4,128)} %pad_maximum_fusion), calls=%async_computation | async-start | bytes 262144 | tf_op jit(solution)/shard_map/all_to_all | solution.py:103
  33.1 7.2 %all-to-all-done = f32[64,3,128]{2,1,0:T(4,128)S(1)} async-done(((f32[64,3,128]{2,1,0:T(4,128)}), f32[64,3,128]{2,1,0:T(4,128)S(1)}, u32[]{:S(2)}, u32[]{:S(2)}) %all-to-all-start) | async-done | bytes 98336 | tf_op jit(solution)/shard_map/all_to_all | solution.py:103
  40.3 0.7 broadcast_in_dim.12
  41.0 5.9 %all-to-all-start.1 = ((f32[64,3,128]{2,1,0:T(4,128)}), f32[64,3,128]{2,1,0:T(4,128)S(1)}, u32[]{:S(2)}, u32[]{:S(2)}) async-start(f32[64,3,128]{2,1,0:T(4,128)} %broadcast_in_dim.12), calls=%async_computation.1 | async-start | bytes 262144 | tf_op jit(solution)/shard_map/all_to_all | solution.py:106
  47.0 7.2 %all-to-all-done.1 = f32[64,3,128]{2,1,0:T(4,128)S(1)} async-done(((f32[64,3,128]{2,1,0:T(4,128)}), f32[64,3,128]{2,1,0:T(4,128)S(1)}, u32[]{:S(2)}, u32[]{:S(2)}) %all-to-all-start.1) | async-done | bytes 98336 | tf_op jit(solution)/shard_map/all_to_all | solution.py:106
  54.2 0.1 slice_reduce_fusion
  54.3 0.1 reshape_squeeze.3
  54.5 0.1 fusion.10
  54.6 0.1 copy.50
  54.7 0.1 reduce_sum.31
  54.8 0.4 fusion.2
  55.2 0.1 copy.51
  55.3 2.2 gather_fusion.4
  57.5 3.2 broadcast_select_fusion
  60.7 6.8 %all-to-all-start.2 = ((bf16[64,128,128]{2,1,0:T(8,128)(2,1)}), bf16[64,128,128]{2,1,0:T(8,128)(2,1)}, u32[]{:S(2)}, u32[]{:S(2)}) async-start(bf16[64,128,128]{2,1,0:T(8,128)(2,1)} %broadcast_select_fusion), calls=%async_computation.2 | async-start | bytes 4194304 | tf_op jit(solution)/shard_map/all_to_all | solution.py:173
  67.5 1.6 copy_bitcast_fusion
  69.2 17.1 %collective-permute-start.5 = (bf16[4,128,2048]{2,1,0:T(8,128)(2,1)}, bf16[4,128,2048]{2,1,0:T(8,128)(2,1)}, u32[]{:S(2)}, u32[]{:S(2)}) collective-permute-start(bf16[4,128,2048]{2,1,0:T(8,128)(2,1)} %copy_bitcast_fusion), channel_id=1, source_target_pairs={{0,0},{225,1},{194,2},{163,3},{164,4},{197,5},{230,6},{7,7},{8,8},... | collective-permute-start | bytes 6291464 | tf_op jit(solution)/shard_map/ppermute | solution.py:119
  86.4 0.1 fusion.11
  86.5 0.1 reshape.236
  86.6 0.6 gather_fusion
  87.2 0.2 reduce_window_sum.11
  87.4 0.1 add.168
  87.5 0.7 fusion.14
  88.2 0.8 gather_fusion.1
  89.0 1.3 gather_fusion.2
  90.3 0.7 convert_multiply_fusion.sq_ref
  91.0 18.6 %all-to-all-done.2.arrived_ref = bf16[64,128,128]{2,1,0:T(8,128)(2,1)} async-done(((bf16[64,128,128]{2,1,0:T(8,128)(2,1)}), bf16[64,128,128]{2,1,0:T(8,128)(2,1)}, u32[]{:S(2)}, u32[]{:S(2)}) %all-to-all-start.2) | async-done | bytes 2097184 | tf_op jit(solution)/shard_map/all_to_all | solution.py:173
  109.7 5.6 %shard_map.82 = (bf16[4,128,128]{2,1,0:T(8,128)(2,1)}, f32[4,128,128]{2,1,0:T(8,128)}, bf16[64,128,128]{2,1,0:T(8,128)(2,1)}) custom-call(s32[64]{0:T(128)} %gather_fusion.2, s32[64]{0:T(128)} %copy-done.1, bf16[64,128,128]{2,1,0:T(8,128)(2,1)} %all-to-all-done.2.arrived_ref, ...), custom_call_target="tpu_custom_call", output_to_operand_aliasing={{1}: (4, {})} | custom-call | tf_op jit(solution)/shard_map/pallas_call | solution.py:76
  115.3 49.7 %all_to_all.40.arrived_ref = bf16[64,128,128]{2,1,0:T(8,128)(2,1)} all-to-all(bf16[64,128,128]{2,1,0:T(8,128)(2,1)} %get-tuple-element.18), channel_id=1, replica_groups=mesh['zh'=4,'zl'=2,'y'=4,'c'=2,'x'=4] {'zl','y','c','x'}, dimensions={0} | all-to-all | bytes 4194304 | tf_op jit(solution)/shard_map/all_to_all | solution.py:173
  165.0 5.6 %shard_map.83 = (bf16[4,128,128]{2,1,0:T(8,128)(2,1)}, f32[4,128,128]{2,1,0:T(8,128)}, bf16[64,128,128]{2,1,0:T(8,128)(2,1)}) custom-call(s32[64]{0:T(128)} %gather_fusion.2, s32[64]{0:T(128)} %copy-done.1, bf16[64,128,128]{2,1,0:T(8,128)(2,1)} %all_to_all.40.arrived_ref, ...), custom_call_target="tpu_custom_call", output_to_operand_aliasing={{1}: (4, {})} | custom-call | tf_op jit(solution)/shard_map/pallas_call | solution.py:76
  170.7 34.6 %all_to_all.41.arrived_ref = bf16[64,128,128]{2,1,0:T(8,128)(2,1)} all-to-all(bf16[64,128,128]{2,1,0:T(8,128)(2,1)} %get-tuple-element.20), channel_id=1, replica_groups=mesh['zh'=4,'zl'=2,'y'=4,'c'=2,'x'=4] {'zl','y','c','x'}, dimensions={0} | all-to-all | bytes 4194304 | tf_op jit(solution)/shard_map/all_to_all | solution.py:173
  205.3 5.6 %shard_map.84 = (bf16[4,128,128]{2,1,0:T(8,128)(2,1)}, f32[4,128,128]{2,1,0:T(8,128)}, bf16[64,128,128]{2,1,0:T(8,128)(2,1)}) custom-call(s32[64]{0:T(128)} %gather_fusion.2, s32[64]{0:T(128)} %copy-done.1, bf16[64,128,128]{2,1,0:T(8,128)(2,1)} %all_to_all.41.arrived_ref, ...), custom_call_target="tpu_custom_call", output_to_operand_aliasing={{1}: (4, {})} | custom-call | tf_op jit(solution)/shard_map/pallas_call | solution.py:76
  210.9 34.4 %all_to_all.42.arrived_ref = bf16[64,128,128]{2,1,0:T(8,128)(2,1)} all-to-all(bf16[64,128,128]{2,1,0:T(8,128)(2,1)} %get-tuple-element.22), channel_id=1, replica_groups=mesh['zh'=4,'zl'=2,'y'=4,'c'=2,'x'=4] {'zl','y','c','x'}, dimensions={0} | all-to-all | bytes 4194304 | tf_op jit(solution)/shard_map/all_to_all | solution.py:173
  245.3 5.6 %shard_map.85 = (bf16[4,128,128]{2,1,0:T(8,128)(2,1)}, f32[4,128,128]{2,1,0:T(8,128)}, bf16[64,128,128]{2,1,0:T(8,128)(2,1)}) custom-call(s32[64]{0:T(128)} %gather_fusion.2, s32[64]{0:T(128)} %copy-done.1, bf16[64,128,128]{2,1,0:T(8,128)(2,1)} %all_to_all.42.arrived_ref, ...), custom_call_target="tpu_custom_call", output_to_operand_aliasing={{1}: (4, {})} | custom-call | tf_op jit(solution)/shard_map/pallas_call | solution.py:76
  250.9 34.4 %all_to_all.43.arrived_ref = bf16[64,128,128]{2,1,0:T(8,128)(2,1)} all-to-all(bf16[64,128,128]{2,1,0:T(8,128)(2,1)} %get-tuple-element.24), channel_id=1, replica_groups=mesh['zh'=4,'zl'=2,'y'=4,'c'=2,'x'=4] {'zl','y','c','x'}, dimensions={0} | all-to-all | bytes 4194304 | tf_op jit(solution)/shard_map/all_to_all | solution.py:173
  285.4 5.6 %shard_map.86 = (bf16[4,128,128]{2,1,0:T(8,128)(2,1)}, f32[4,128,128]{2,1,0:T(8,128)}, bf16[64,128,128]{2,1,0:T(8,128)(2,1)}) custom-call(s32[64]{0:T(128)} %gather_fusion.2, s32[64]{0:T(128)} %copy-done.1, bf16[64,128,128]{2,1,0:T(8,128)(2,1)} %all_to_all.43.arrived_ref, ...), custom_call_target="tpu_custom_call", output_to_operand_aliasing={{1}: (4, {})} | custom-call | tf_op jit(solution)/shard_map/pallas_call | solution.py:76
  291.0 34.4 %all_to_all.44.arrived_ref = bf16[64,128,128]{2,1,0:T(8,128)(2,1)} all-to-all(bf16[64,128,128]{2,1,0:T(8,128)(2,1)} %get-tuple-element.26), channel_id=1, replica_groups=mesh['zh'=4,'zl'=2,'y'=4,'c'=2,'x'=4] {'zl','y','c','x'}, dimensions={0} | all-to-all | bytes 4194304 | tf_op jit(solution)/shard_map/all_to_all | solution.py:173
  325.4 5.6 %shard_map.87 = (bf16[4,128,128]{2,1,0:T(8,128)(2,1)}, f32[4,128,128]{2,1,0:T(8,128)}, bf16[64,128,128]{2,1,0:T(8,128)(2,1)}) custom-call(s32[64]{0:T(128)} %gather_fusion.2, s32[64]{0:T(128)} %copy-done.1, bf16[64,128,128]{2,1,0:T(8,128)(2,1)} %all_to_all.44.arrived_ref, ...), custom_call_target="tpu_custom_call", output_to_operand_aliasing={{1}: (4, {})} | custom-call | tf_op jit(solution)/shard_map/pallas_call | solution.py:76
  331.1 2.3 collective-permute-start.6
  333.3 1.1 reduce_sum.32
  334.5 2.3 collective-permute-start.7
  336.8 6.8 %collective-permute-done.7 = f32[4,128]{1,0:T(4,128)S(1)} collective-permute-done((f32[4,128]{1,0:T(4,128)S(1)}, f32[4,128]{1,0:T(4,128)S(1)}, u32[]{:S(2)}, u32[]{:S(2)}) %collective-permute-start.7) | collective-permute-done | bytes 2080 | tf_op jit(solution)/shard_map/ppermute | solution.py:178
  343.6 10.1 %psum.7 = f32[4,128]{1,0:T(4,128)S(1)} all-reduce(f32[4,128]{1,0:T(4,128)S(1)} %collective-permute-done.7), channel_id=1, replica_groups=mesh['zh'=4,'zl'=2,'y'=4,'c'=2,'x'=4] {'x'}, use_global_device_ids=true, to_apply=%region_7.8 | all-reduce | flops 512 | bytes 4096 | tf_op jit(solution)/shard_map/psum | solution.py:179
  353.7 0.8 multiply_divide_fusion
  (29 shorter events, 0.3 us)
Async XLA Ops:
  0.0 67.5 %copy-start = (bf16[4,16,128,128]{3,2,1,0:T(8,128)(2,1)S(1)}, bf16[4,16,128,128]{3,2,1,0:T(8,128)(2,1)}, u32[]{:S(2)}) copy-start(bf16[4,16,128,128]{3,2,1,0:T(8,128)(2,1)} %param.8) | copy-start | bytes 6291460
  0.0 13.8 %collective-permute-start = (s32[128]{0:T(128)}, s32[128]{0:T(128)S(1)}, u32[]{:S(2)}, u32[]{:S(2)}) collective-permute-start(s32[128]{0:T(128)} %param.12), channel_id=1, source_target_pairs={{0,1},{1,2},{2,3},{3,0},{4,5},{5,6},{6,7},{7,4},{8,9},{9,10},{10,1... | collective-permute-start | bytes 1544 | tf_op jit(solution)/shard_map/ppermute | solution.py:131
  1.5 12.4 %collective-permute-start.2 = (s32[128]{0:T(128)}, s32[128]{0:T(128)S(1)}, u32[]{:S(2)}, u32[]{:S(2)}) collective-permute-start(s32[128]{0:T(128)} %param.12), channel_id=1, source_target_pairs={{0,3},{1,0},{2,1},{3,2},{4,7},{5,4},{6,5},{7,6},{8,11},{9,8},{10,9... | collective-permute-start | bytes 1544 | tf_op jit(solution)/shard_map/ppermute | solution.py:131
  3.2 10.6 %collective-permute-start.1 = (s32[128]{0:T(128)}, s32[128]{0:T(128)S(1)}, u32[]{:S(2)}, u32[]{:S(2)}) collective-permute-start(s32[128]{0:T(128)} %param.12), channel_id=1, source_target_pairs={{0,2},{1,3},{2,0},{3,1},{4,6},{5,7},{6,4},{7,5},{8,10},{9,11},{10,... | collective-permute-start | bytes 1544 | tf_op jit(solution)/shard_map/ppermute | solution.py:131
  5.1 9.5 %collective-permute-start.4 = (f32[512]{0:T(512)}, f32[512]{0:T(512)S(1)}, u32[]{:S(2)}, u32[]{:S(2)}) collective-permute-start(f32[512]{0:T(512)} %param.11), channel_id=1, source_target_pairs={{0,0},{225,1},{194,2},{163,3},{164,4},{197,5},{230,6},{7,7},{8,8},... | collective-permute-start | bytes 6152 | tf_op jit(solution)/shard_map/ppermute | solution.py:114
  6.4 8.6 %collective-permute-start.3 = (f32[512,128]{1,0:T(8,128)}, f32[512,128]{1,0:T(8,128)S(1)}, u32[]{:S(2)}, u32[]{:S(2)}) collective-permute-start(f32[512,128]{1,0:T(8,128)} %param.10), channel_id=1, source_target_pairs={{0,0},{225,1},{194,2},{163,3},{164,4},{197,5},{230,6},{7,7},{8,8},... | collective-permute-start | bytes 786440 | tf_op jit(solution)/shard_map/ppermute | solution.py:114
  13.8 43.7 %copy-start.1 = (s32[64]{0:T(128)}, s32[64]{0:T(128)S(1)}, u32[]{:S(2)}) copy-start(s32[64]{0:T(128)S(1)} %get-tuple-element.17.send_ref) | copy-start | bytes 772
  16.0 24.2 %all-to-all-start = ((f32[64,3,128]{2,1,0:T(4,128)}), f32[64,3,128]{2,1,0:T(4,128)S(1)}, u32[]{:S(2)}, u32[]{:S(2)}) async-start(f32[64,3,128]{2,1,0:T(4,128)} %pad_maximum_fusion), calls=%async_computation | async-start | bytes 262144 | tf_op jit(solution)/shard_map/all_to_all | solution.py:103
  41.0 13.2 %all-to-all-start.1 = ((f32[64,3,128]{2,1,0:T(4,128)}), f32[64,3,128]{2,1,0:T(4,128)S(1)}, u32[]{:S(2)}, u32[]{:S(2)}) async-start(f32[64,3,128]{2,1,0:T(4,128)} %broadcast_in_dim.12), calls=%async_computation.1 | async-start | bytes 262144 | tf_op jit(solution)/shard_map/all_to_all | solution.py:106
  60.7 49.0 %all-to-all-start.2 = ((bf16[64,128,128]{2,1,0:T(8,128)(2,1)}), bf16[64,128,128]{2,1,0:T(8,128)(2,1)}, u32[]{:S(2)}, u32[]{:S(2)}) async-start(bf16[64,128,128]{2,1,0:T(8,128)(2,1)} %broadcast_select_fusion), calls=%async_computation.2 | async-start | bytes 4194304 | tf_op jit(solution)/shard_map/all_to_all | solution.py:173
  69.2 21.8 %collective-permute-start.5 = (bf16[4,128,2048]{2,1,0:T(8,128)(2,1)}, bf16[4,128,2048]{2,1,0:T(8,128)(2,1)}, u32[]{:S(2)}, u32[]{:S(2)}) collective-permute-start(bf16[4,128,2048]{2,1,0:T(8,128)(2,1)} %copy_bitcast_fusion), channel_id=1, source_target_pairs={{0,0},{225,1},{194,2},{163,3},{164,4},{197,5},{230,6},{7,7},{8,8},... | collective-permute-start | bytes 6291464 | tf_op jit(solution)/shard_map/ppermute | solution.py:119
  331.1 22.7 %collective-permute-start.6 = (f32[4,128,128]{2,1,0:T(8,128)}, f32[4,128,128]{2,1,0:T(8,128)S(1)}, u32[]{:S(2)}, u32[]{:S(2)}) collective-permute-start(f32[4,128,128]{2,1,0:T(8,128)} %get-tuple-element.28), channel_id=1, source_target_pairs={{0,0},{1,224},{2,192},{3,160},{4,164},{5,196},{6,228},{7,4},{8,8},... | collective-permute-start | bytes 786440 | tf_op jit(solution)/shard_map/ppermute | solution.py:178
  334.5 9.1 %collective-permute-start.7 = (f32[4,128]{1,0:T(4,128)S(1)}, f32[4,128]{1,0:T(4,128)S(1)}, u32[]{:S(2)}, u32[]{:S(2)}) collective-permute-start(f32[4,128]{1,0:T(4,128)S(1)} %reduce_sum.32), channel_id=1, source_target_pairs={{0,0},{1,224},{2,192},{3,160},{4,164},{5,196},{6,228},{7,4},{8,8},... | collective-permute-start | bytes 6152 | tf_op jit(solution)/shard_map/ppermute | solution.py:178

commit v8 on v6

--- a/solution.py
+++ b/solution.py
@@ -169,13 +169,20 @@
         send_idx = jnp.argmax(send_need, axis=1).astype(jnp.int32)
         outgoing = jnp.take(present_response, send_idx, axis=0)
         coefs_wide = coefs.transpose(0, 2, 1, 3).reshape(blk_dev, block_size, lags * block_size)
-        for step_no in range(HORIZONS - 1):
+        for step_no in range(HORIZONS - 2):
             arriving_response = lax.all_to_all(outgoing, BOX, split_axis=0, concat_axis=0, tiled=True)
             present_response, squared_terms, outgoing = step(
                 take_index, send_idx, arriving_response, coefs_wide, squared_terms
             )
+        earlier_squares = lax.ppermute(squared_terms, ALL, perm_out)
+        arriving_response = lax.all_to_all(outgoing, BOX, split_axis=0, concat_axis=0, tiled=True)
+        present_response, squared_terms, _ = step(
+            take_index, send_idx, arriving_response, coefs_wide, squared_terms
+        )
         partial = jnp.sum(squared_terms, axis=2)
-        squared_terms, partial = lax.ppermute((squared_terms, partial), ALL, perm_out)
+        last_response, partial = lax.ppermute((present_response, partial), ALL, perm_out)
+        wide_last = last_response.astype(jnp.float32)
+        squared_terms = earlier_squares + wide_last * wide_last
         totals = lax.psum(partial, "x")
         total_shocks = shock_columns * xs
         shares = total_shocks * squared_terms / (totals[:, :, None] + 1e-06)

time: 359 us -> 360 us (level)
  blocking collectives: 196 us -> 161 us
  waiting for transfers between devices: 41.1 us -> 67.3 us
  starting transfers between devices: 58.6 us -> 67.7 us
    all_to_all x5 -> x4, blocking collectives: 186 us -> 152 us  [on_device(): lax.all_to_all(outgoing, BOX, split_axis=0, concat_axis=0, tiled=True)]
    ppermute x2 -> x3, waiting for transfers between devices: 6.81 us -> 27.5 us  [the longest x1 22.6 us: on_device(): earlier_squares = lax.ppermute(squared_terms, ALL, perm_out)]
    all_to_all x1 -> x2, starting transfers between devices: 6.02 us -> 12.5 us  [on_device(): lax.all_to_all(outgoing, BOX, split_axis=0, concat_axis=0, tiled=True)]
    all_to_all x1 -> x2, waiting for transfers between devices: 19.9 us -> 25.4 us  [on_device(): lax.all_to_all(outgoing, BOX, split_axis=0, concat_axis=0, tiled=True)]
    ppermute x2 -> x3, starting transfers between devices: 4.6 us -> 7.23 us  [the longest x2 3.85 us: on_device(): lax.ppermute((present_response, partial), ALL, perm_out)]
  transfers between devices with their start and end apart: 11 -> 13, of which waited for: 4 -> 6; matrix products, arithmetic and copies ran while one was open for 4% -> 4% of each run, Pallas kernels for 0% -> 0%
where the time goes in v8:
time: 360 us; the launch traced here: 355 us
  blocking collectives  161 us (45%)
  starting transfers between devices  67.7 us (19%)
  waiting for transfers between devices  67.3 us (19%)
  Pallas kernels  33.6 us (9%)
  local copies, waits for them, and re-layouts  15.7 us (4%)
  other arithmetic  7.57 us (2%)
    all_to_all x4, blocking collectives, on_device(): lax.all_to_all(outgoing, BOX, split_axis=0, concat_axis=0, tiled=True)  152 us
    pallas_call x6, Pallas kernels, step(): pl.pallas_call(step_kernel, out_shape=(jax.ShapeDtypeStruct((blk_dev, bs,...  33.6 us
    all_to_all x2, waiting for transfers between devices, on_device(): lax.all_to_all(outgoing, BOX, split_axis=0, concat_axis=0, tiled=True)  25.4 us
    ppermute x1, waiting for transfers between devices, on_device(): earlier_squares = lax.ppermute(squared_terms, ALL, perm_out)  22.6 us
    ppermute x1, starting transfers between devices, on_device(): coefs = lax.ppermute(coefs, ALL, perm_in)  17.1 us
    all_to_all x1, starting transfers between devices, gather_rows(): arrived = lax.all_to_all(packed, BOX, 0, 0, tiled=True)  17 us
    all_to_all x2, starting transfers between devices, on_device(): lax.all_to_all(outgoing, BOX, split_axis=0, concat_axis=0, tiled=True)  12.5 us
    psum x1, blocking collectives, on_device(): totals = lax.psum(partial, 'x')  8.73 us
  transfers between devices with their start and end apart: 13, of which 6 were waited for; matrix products, arithmetic and copies ran while one was open for 4% of the time, Pallas kernels for 0%

profile of v8, /device:TPU:96, one launch (start us, length us, event | category | flops | bytes accessed | tf_op | source)
XLA Modules:
  0.0 354.5 jit_solution(10678820244912941925)
XLA Ops:
  0.0 1.5 collective-permute-start
  1.5 1.7 collective-permute-start.2
  3.2 1.8 collective-permute-start.1
  5.1 1.3 collective-permute-start.4
  6.4 1.6 collective-permute-start.3
  8.0 1.3 dynamic_slice.15
  9.9 0.8 copy.46
  10.7 0.8 constant_dynamic-slice_fusion.3
  11.7 0.7 fusion.16
  12.5 0.6 gather_fusion.3
  13.1 0.2 compare_reduce_fusion
  13.3 0.5 iota_reduce_fusion
  13.9 0.7 pad_add_fusion
  14.6 0.2 convolution_bitcast_fusion.1
  14.8 0.2 reshape.231
  15.0 0.3 fusion.4
  15.3 0.7 pad_maximum_fusion
  16.0 17.0 %all-to-all-start = ((f32[64,3,128]{2,1,0:T(4,128)}), f32[64,3,128]{2,1,0:T(4,128)S(1)}, u32[]{:S(2)}, u32[]{:S(2)}) async-start(f32[64,3,128]{2,1,0:T(4,128)} %pad_maximum_fusion), calls=%async_computation | async-start | bytes 262144 | tf_op jit(solution)/shard_map/all_to_all | solution.py:103
  33.1 7.2 %all-to-all-done = f32[64,3,128]{2,1,0:T(4,128)S(1)} async-done(((f32[64,3,128]{2,1,0:T(4,128)}), f32[64,3,128]{2,1,0:T(4,128)S(1)}, u32[]{:S(2)}, u32[]{:S(2)}) %all-to-all-start) | async-done | bytes 98336 | tf_op jit(solution)/shard_map/all_to_all | solution.py:103
  40.3 0.7 broadcast_in_dim.12
  41.0 5.9 %all-to-all-start.1 = ((f32[64,3,128]{2,1,0:T(4,128)}), f32[64,3,128]{2,1,0:T(4,128)S(1)}, u32[]{:S(2)}, u32[]{:S(2)}) async-start(f32[64,3,128]{2,1,0:T(4,128)} %broadcast_in_dim.12), calls=%async_computation.1 | async-start | bytes 262144 | tf_op jit(solution)/shard_map/all_to_all | solution.py:106
  47.0 7.2 %all-to-all-done.1 = f32[64,3,128]{2,1,0:T(4,128)S(1)} async-done(((f32[64,3,128]{2,1,0:T(4,128)}), f32[64,3,128]{2,1,0:T(4,128)S(1)}, u32[]{:S(2)}, u32[]{:S(2)}) %all-to-all-start.1) | async-done | bytes 98336 | tf_op jit(solution)/shard_map/all_to_all | solution.py:106
  54.2 0.1 slice_reduce_fusion
  54.3 0.1 reshape_squeeze.3
  54.6 0.1 copy.50
  54.7 0.1 reduce_sum.31
  54.8 0.4 fusion.2
  55.2 0.1 copy.51
  55.3 1.0 gather_fusion.4
  56.3 1.6 broadcast_select_fusion
  57.9 6.0 %all-to-all-start.2 = ((bf16[64,128,128]{2,1,0:T(8,128)(2,1)}), bf16[64,128,128]{2,1,0:T(8,128)(2,1)S(1)}, u32[]{:S(2)}, u32[]{:S(2)}) async-start(bf16[64,128,128]{2,1,0:T(8,128)(2,1)} %broadcast_select_fusion), calls=%async_computation.2 | async-start | bytes 4194304 | tf_op jit(solution)/shard_map/all_to_all | solution.py:173
  63.9 17.1 %collective-permute-start.5 = (bf16[4,16,128,128]{3,2,1,0:T(8,128)(2,1)}, bf16[4,16,128,128]{3,2,1,0:T(8,128)(2,1)}, u32[]{:S(2)}, u32[]{:S(2)}) collective-permute-start(bf16[4,16,128,128]{3,2,1,0:T(8,128)(2,1)} %param.8), channel_id=1, source_target_pairs={{0,0},{225,1},{194,2},{163,3},{164,4},{197,5},{230,6},{7,7},{8,8},... | collective-permute-start | bytes 6291464 | tf_op jit(solution)/shard_map/ppermute | solution.py:115
  81.2 0.1 reshape.236
  81.3 0.6 gather_fusion
  81.9 0.2 reduce_window_sum.11
  82.1 0.1 add.171
  82.2 0.7 fusion.14
  82.9 0.8 gather_fusion.1
  83.7 1.3 gather_fusion.2
  85.0 0.7 convert_multiply_fusion.sq_ref
  85.7 3.3 copy_bitcast_fusion.coefs_ref
  89.0 19.9 %all-to-all-done.2.arrived_ref = bf16[64,128,128]{2,1,0:T(8,128)(2,1)S(1)} async-done(((bf16[64,128,128]{2,1,0:T(8,128)(2,1)}), bf16[64,128,128]{2,1,0:T(8,128)(2,1)S(1)}, u32[]{:S(2)}, u32[]{:S(2)}) %all-to-all-start.2) | async-done | bytes 2097184 | tf_op jit(solution)/shard_map/all_to_all | solution.py:173
  108.9 1.3 copy-done.1
  110.2 5.6 %shard_map.82 = (bf16[4,128,128]{2,1,0:T(8,128)(2,1)}, f32[4,128,128]{2,1,0:T(8,128)}, bf16[64,128,128]{2,1,0:T(8,128)(2,1)}) custom-call(s32[64]{0:T(128)} %gather_fusion.2, s32[64]{0:T(128)} %copy-done.3, bf16[64,128,128]{2,1,0:T(8,128)(2,1)} %copy-done.1, bf16[4,128,2048]{2,1,0:T(8,128)(2,1)} %copy_bitcast_fusion.coefs_ref, ...), custom_call_target="tpu_custom_call", output_to_operand_aliasing={{1}: (4, {})} | custom-call | tf_op jit(solution)/shard_map/pallas_call | solution.py:76
  115.8 48.5 %all_to_all.40.arrived_ref = bf16[64,128,128]{2,1,0:T(8,128)(2,1)} all-to-all(bf16[64,128,128]{2,1,0:T(8,128)(2,1)} %get-tuple-element.19), channel_id=1, replica_groups=mesh['zh'=4,'zl'=2,'y'=4,'c'=2,'x'=4] {'zl','y','c','x'}, dimensions={0} | all-to-all | bytes 4194304 | tf_op jit(solution)/shard_map/all_to_all | solution.py:173
  164.3 5.6 %shard_map.83 = (bf16[4,128,128]{2,1,0:T(8,128)(2,1)}, f32[4,128,128]{2,1,0:T(8,128)}, bf16[64,128,128]{2,1,0:T(8,128)(2,1)}) custom-call(s32[64]{0:T(128)} %gather_fusion.2, s32[64]{0:T(128)} %copy-done.3, bf16[64,128,128]{2,1,0:T(8,128)(2,1)} %all_to_all.40.arrived_ref, ...), custom_call_target="tpu_custom_call", output_to_operand_aliasing={{1}: (4, {})} | custom-call | tf_op jit(solution)/shard_map/pallas_call | solution.py:76
  169.9 34.6 %all_to_all.41.arrived_ref = bf16[64,128,128]{2,1,0:T(8,128)(2,1)} all-to-all(bf16[64,128,128]{2,1,0:T(8,128)(2,1)} %get-tuple-element.21), channel_id=1, replica_groups=mesh['zh'=4,'zl'=2,'y'=4,'c'=2,'x'=4] {'zl','y','c','x'}, dimensions={0} | all-to-all | bytes 4194304 | tf_op jit(solution)/shard_map/all_to_all | solution.py:173
  204.5 5.6 %shard_map.84 = (bf16[4,128,128]{2,1,0:T(8,128)(2,1)}, f32[4,128,128]{2,1,0:T(8,128)}, bf16[64,128,128]{2,1,0:T(8,128)(2,1)}) custom-call(s32[64]{0:T(128)} %gather_fusion.2, s32[64]{0:T(128)} %copy-done.3, bf16[64,128,128]{2,1,0:T(8,128)(2,1)} %all_to_all.41.arrived_ref, ...), custom_call_target="tpu_custom_call", output_to_operand_aliasing={{1}: (4, {})} | custom-call | tf_op jit(solution)/shard_map/pallas_call | solution.py:76
  210.1 34.4 %all_to_all.42.arrived_ref = bf16[64,128,128]{2,1,0:T(8,128)(2,1)} all-to-all(bf16[64,128,128]{2,1,0:T(8,128)(2,1)} %get-tuple-element.23), channel_id=1, replica_groups=mesh['zh'=4,'zl'=2,'y'=4,'c'=2,'x'=4] {'zl','y','c','x'}, dimensions={0} | all-to-all | bytes 4194304 | tf_op jit(solution)/shard_map/all_to_all | solution.py:173
  244.5 5.6 %shard_map.85 = (bf16[4,128,128]{2,1,0:T(8,128)(2,1)}, f32[4,128,128]{2,1,0:T(8,128)}, bf16[64,128,128]{2,1,0:T(8,128)(2,1)}) custom-call(s32[64]{0:T(128)} %gather_fusion.2, s32[64]{0:T(128)} %copy-done.3, bf16[64,128,128]{2,1,0:T(8,128)(2,1)} %all_to_all.42.arrived_ref, ...), custom_call_target="tpu_custom_call", output_to_operand_aliasing={{1}: (4, {})} | custom-call | tf_op jit(solution)/shard_map/pallas_call | solution.py:76
  250.1 34.4 %all_to_all.43.arrived_ref = bf16[64,128,128]{2,1,0:T(8,128)(2,1)} all-to-all(bf16[64,128,128]{2,1,0:T(8,128)(2,1)} %get-tuple-element.25), channel_id=1, replica_groups=mesh['zh'=4,'zl'=2,'y'=4,'c'=2,'x'=4] {'zl','y','c','x'}, dimensions={0} | all-to-all | bytes 4194304 | tf_op jit(solution)/shard_map/all_to_all | solution.py:173
  284.5 5.6 %shard_map.86 = (bf16[4,128,128]{2,1,0:T(8,128)(2,1)}, f32[4,128,128]{2,1,0:T(8,128)}, bf16[64,128,128]{2,1,0:T(8,128)(2,1)}) custom-call(s32[64]{0:T(128)} %gather_fusion.2, s32[64]{0:T(128)} %copy-done.3, bf16[64,128,128]{2,1,0:T(8,128)(2,1)} %all_to_all.43.arrived_ref, ...), custom_call_target="tpu_custom_call", output_to_operand_aliasing={{1}: (4, {})} | custom-call | tf_op jit(solution)/shard_map/pallas_call | solution.py:76
  290.2 6.5 %all-to-all-start.7 = ((bf16[64,128,128]{2,1,0:T(8,128)(2,1)}), bf16[64,128,128]{2,1,0:T(8,128)(2,1)S(1)}, u32[]{:S(2)}, u32[]{:S(2)}) async-start(bf16[64,128,128]{2,1,0:T(8,128)(2,1)} %get-tuple-element.28), calls=%async_computation.7 | async-start | bytes 4194304 | tf_op jit(solution)/shard_map/all_to_all | solution.py:178
  296.6 3.4 collective-permute-start.6
  300.0 22.6 %collective-permute-done.6 = f32[4,128,128]{2,1,0:T(8,128)S(1)} collective-permute-done((f32[4,128,128]{2,1,0:T(8,128)S(1)}, f32[4,128,128]{2,1,0:T(8,128)S(1)}, u32[]{:S(2)}, u32[]{:S(2)}) %collective-permute-start.6) | collective-permute-done | bytes 262176 | tf_op jit(solution)/shard_map/ppermute | solution.py:177
  322.6 5.5 %all-to-all-done.7.arrived_ref = bf16[64,128,128]{2,1,0:T(8,128)(2,1)S(1)} async-done(((bf16[64,128,128]{2,1,0:T(8,128)(2,1)}), bf16[64,128,128]{2,1,0:T(8,128)(2,1)S(1)}, u32[]{:S(2)}, u32[]{:S(2)}) %all-to-all-start.7) | async-done | bytes 2097184 | tf_op jit(solution)/shard_map/all_to_all | solution.py:178
  328.1 1.3 copy-done.2
  329.4 5.6 %shard_map.87 = (bf16[4,128,128]{2,1,0:T(8,128)(2,1)}, f32[4,128,128]{2,1,0:T(8,128)}, bf16[64,128,128]{2,1,0:T(8,128)(2,1)}) custom-call(s32[64]{0:T(128)} %gather_fusion.2, s32[64]{0:T(128)} %copy-done.3, bf16[64,128,128]{2,1,0:T(8,128)(2,1)} %copy-done.2, bf16[4,128,2048]{2,1,0:T(8,128)(2,1)} %copy_bitcast_fusion.coefs_ref, ...), custom_call_target="tpu_custom_call", output_to_operand_aliasing={{1}: (4, {})} | custom-call | tf_op jit(solution)/shard_map/pallas_call | solution.py:76
  335.0 1.1 reduce_sum.32
  336.1 1.9 collective-permute-start.8
  338.1 1.9 collective-permute-start.7
  340.0 4.9 %collective-permute-done.8 = f32[4,128]{1,0:T(4,128)S(1)} collective-permute-done((f32[4,128]{1,0:T(4,128)S(1)}, f32[4,128]{1,0:T(4,128)S(1)}, u32[]{:S(2)}, u32[]{:S(2)}) %collective-permute-start.8) | collective-permute-done | bytes 2080 | tf_op jit(solution)/shard_map/ppermute | solution.py:183
  344.9 8.7 %psum.7 = f32[4,128]{1,0:T(4,128)S(1)} all-reduce(f32[4,128]{1,0:T(4,128)S(1)} %collective-permute-done.8), channel_id=1, replica_groups=mesh['zh'=4,'zl'=2,'y'=4,'c'=2,'x'=4] {'x'}, use_global_device_ids=true, to_apply=%region_7.8 | all-reduce | flops 512 | bytes 4096 | tf_op jit(solution)/shard_map/psum | solution.py:186
  353.7 0.8 multiply_divide_fusion
  (36 shorter events, 0.8 us)
Async XLA Ops:
  0.0 13.8 %collective-permute-start = (s32[128]{0:T(128)}, s32[128]{0:T(128)S(1)}, u32[]{:S(2)}, u32[]{:S(2)}) collective-permute-start(s32[128]{0:T(128)} %param.12), channel_id=1, source_target_pairs={{0,1},{1,2},{2,3},{3,0},{4,5},{5,6},{6,7},{7,4},{8,9},{9,10},{10,1... | collective-permute-start | bytes 1544 | tf_op jit(solution)/shard_map/ppermute | solution.py:130
  1.5 12.4 %collective-permute-start.2 = (s32[128]{0:T(128)}, s32[128]{0:T(128)S(1)}, u32[]{:S(2)}, u32[]{:S(2)}) collective-permute-start(s32[128]{0:T(128)} %param.12), channel_id=1, source_target_pairs={{0,3},{1,0},{2,1},{3,2},{4,7},{5,4},{6,5},{7,6},{8,11},{9,8},{10,9... | collective-permute-start | bytes 1544 | tf_op jit(solution)/shard_map/ppermute | solution.py:130
  3.2 10.6 %collective-permute-start.1 = (s32[128]{0:T(128)}, s32[128]{0:T(128)S(1)}, u32[]{:S(2)}, u32[]{:S(2)}) collective-permute-start(s32[128]{0:T(128)} %param.12), channel_id=1, source_target_pairs={{0,2},{1,3},{2,0},{3,1},{4,6},{5,7},{6,4},{7,5},{8,10},{9,11},{10,... | collective-permute-start | bytes 1544 | tf_op jit(solution)/shard_map/ppermute | solution.py:130
  5.1 9.5 %collective-permute-start.4 = (f32[512]{0:T(512)}, f32[512]{0:T(512)S(1)}, u32[]{:S(2)}, u32[]{:S(2)}) collective-permute-start(f32[512]{0:T(512)} %param.11), channel_id=1, source_target_pairs={{0,0},{225,1},{194,2},{163,3},{164,4},{197,5},{230,6},{7,7},{8,8},... | collective-permute-start | bytes 6152 | tf_op jit(solution)/shard_map/ppermute | solution.py:114
  6.4 8.6 %collective-permute-start.3 = (f32[512,128]{1,0:T(8,128)}, f32[512,128]{1,0:T(8,128)S(1)}, u32[]{:S(2)}, u32[]{:S(2)}) collective-permute-start(f32[512,128]{1,0:T(8,128)} %param.10), channel_id=1, source_target_pairs={{0,0},{225,1},{194,2},{163,3},{164,4},{197,5},{230,6},{7,7},{8,8},... | collective-permute-start | bytes 786440 | tf_op jit(solution)/shard_map/ppermute | solution.py:114
  13.8 42.5 %copy-start.3 = (s32[64]{0:T(128)}, s32[64]{0:T(128)S(1)}, u32[]{:S(2)}) copy-start(s32[64]{0:T(128)S(1)} %get-tuple-element.18.send_ref) | copy-start | bytes 772
  16.0 24.2 %all-to-all-start = ((f32[64,3,128]{2,1,0:T(4,128)}), f32[64,3,128]{2,1,0:T(4,128)S(1)}, u32[]{:S(2)}, u32[]{:S(2)}) async-start(f32[64,3,128]{2,1,0:T(4,128)} %pad_maximum_fusion), calls=%async_computation | async-start | bytes 262144 | tf_op jit(solution)/shard_map/all_to_all | solution.py:103
  41.0 13.2 %all-to-all-start.1 = ((f32[64,3,128]{2,1,0:T(4,128)}), f32[64,3,128]{2,1,0:T(4,128)S(1)}, u32[]{:S(2)}, u32[]{:S(2)}) async-start(f32[64,3,128]{2,1,0:T(4,128)} %broadcast_in_dim.12), calls=%async_computation.1 | async-start | bytes 262144 | tf_op jit(solution)/shard_map/all_to_all | solution.py:106
  57.9 51.0 %all-to-all-start.2 = ((bf16[64,128,128]{2,1,0:T(8,128)(2,1)}), bf16[64,128,128]{2,1,0:T(8,128)(2,1)S(1)}, u32[]{:S(2)}, u32[]{:S(2)}) async-start(bf16[64,128,128]{2,1,0:T(8,128)(2,1)} %broadcast_select_fusion), calls=%async_computation.2 | async-start | bytes 4194304 | tf_op jit(solution)/shard_map/all_to_all | solution.py:173
  63.9 21.8 %collective-permute-start.5 = (bf16[4,16,128,128]{3,2,1,0:T(8,128)(2,1)}, bf16[4,16,128,128]{3,2,1,0:T(8,128)(2,1)}, u32[]{:S(2)}, u32[]{:S(2)}) collective-permute-start(bf16[4,16,128,128]{3,2,1,0:T(8,128)(2,1)} %param.8), channel_id=1, source_target_pairs={{0,0},{225,1},{194,2},{163,3},{164,4},{197,5},{230,6},{7,7},{8,8},... | collective-permute-start | bytes 6291464 | tf_op jit(solution)/shard_map/ppermute | solution.py:115
  108.9 1.3 copy-start.1
  290.1 6.5 %copy-start = (f32[4,128,128]{2,1,0:T(8,128)S(1)}, f32[4,128,128]{2,1,0:T(8,128)}, u32[]{:S(2)}) copy-start(f32[4,128,128]{2,1,0:T(8,128)} %get-tuple-element.27.sq_ref) | copy-start | bytes 786436
  290.2 37.9 %all-to-all-start.7 = ((bf16[64,128,128]{2,1,0:T(8,128)(2,1)}), bf16[64,128,128]{2,1,0:T(8,128)(2,1)S(1)}, u32[]{:S(2)}, u32[]{:S(2)}) async-start(bf16[64,128,128]{2,1,0:T(8,128)(2,1)} %get-tuple-element.28), calls=%async_computation.7 | async-start | bytes 4194304 | tf_op jit(solution)/shard_map/all_to_all | solution.py:178
  296.6 26.0 %collective-permute-start.6 = (f32[4,128,128]{2,1,0:T(8,128)S(1)}, f32[4,128,128]{2,1,0:T(8,128)S(1)}, u32[]{:S(2)}, u32[]{:S(2)}) collective-permute-start(f32[4,128,128]{2,1,0:T(8,128)S(1)} %copy-done), channel_id=1, source_target_pairs={{0,0},{1,224},{2,192},{3,160},{4,164},{5,196},{6,228},{7,4},{8,8},... | collective-permute-start | bytes 786440 | tf_op jit(solution)/shard_map/ppermute | solution.py:177
  328.1 1.3 copy-start.2
  336.1 8.8 %collective-permute-start.8 = (f32[4,128]{1,0:T(4,128)S(1)}, f32[4,128]{1,0:T(4,128)S(1)}, u32[]{:S(2)}, u32[]{:S(2)}) collective-permute-start(f32[4,128]{1,0:T(4,128)S(1)} %reduce_sum.32), channel_id=1, source_target_pairs={{0,0},{1,224},{2,192},{3,160},{4,164},{5,196},{6,228},{7,4},{8,8},... | collective-permute-start | bytes 6152 | tf_op jit(solution)/shard_map/ppermute | solution.py:183
  338.1 15.6 %collective-permute-start.7 = (bf16[4,128,128]{2,1,0:T(8,128)(2,1)}, bf16[4,128,128]{2,1,0:T(8,128)(2,1)S(1)}, u32[]{:S(2)}, u32[]{:S(2)}) collective-permute-start(bf16[4,128,128]{2,1,0:T(8,128)(2,1)} %get-tuple-element.29), channel_id=1, source_target_pairs={{0,0},{1,224},{2,192},{3,160},{4,164},{5,196},{6,228},{7,4},{8,8},... | collective-permute-start | bytes 393224 | tf_op jit(solution)/shard_map/ppermute | solution.py:183

commit v9 on v8

--- a/solution.py
+++ b/solution.py
@@ -183,7 +183,10 @@
         last_response, partial = lax.ppermute((present_response, partial), ALL, perm_out)
         wide_last = last_response.astype(jnp.float32)
         squared_terms = earlier_squares + wide_last * wide_last
-        totals = lax.psum(partial, "x")
+        moved = jnp.stack([partial] + [lax.ppermute(partial, ALL, perm_x[j]) for j in range(1, xs)])
+        totals = moved[x % xs]
+        for source in range(1, xs):
+            totals = totals + moved[(x - source) % xs]
         total_shocks = shock_columns * xs
         shares = total_shocks * squared_terms / (totals[:, :, None] + 1e-06)
         return shares.reshape(local_rows, shock_columns)

time: 360 us -> 363 us (level)
  blocking collectives: 161 us -> 150 us
  waiting for transfers between devices: 67.3 us -> 75.7 us
    psum x1 -> x0, blocking collectives: 8.73 us -> none  [on_device(): totals = lax.psum(partial, 'x')]
    ppermute x2, waiting for transfers between devices: 4.94 us -> 13.3 us  [on_device(): lax.ppermute((present_response, partial), ALL, perm_out)]
    ppermute x0 -> x3, starting transfers between devices: none -> 4.97 us  [on_device(): lax.ppermute(partial, ALL, perm_x[j])]
    all_to_all x1, starting transfers between devices: 17 us -> 13.2 us  [gather_rows(): arrived = lax.all_to_all(packed, BOX, 0, 0, tiled=True)]
  transfers between devices with their start and end apart: 13 -> 16, of which waited for: 6 -> 7; matrix products, arithmetic and copies ran while one was open for 4% -> 4% of each run, Pallas kernels for 0% -> 0%
where the time goes in v9:
time: 363 us; the launch traced here: 355 us
  blocking collectives  150 us (41%)
  waiting for transfers between devices  75.7 us (21%)
  starting transfers between devices  70.8 us (20%)
  Pallas kernels  33.6 us (9%)
  local copies, waits for them, and re-layouts  15.7 us (4%)
  other arithmetic  7.58 us (2%)
    all_to_all x4, blocking collectives, on_device(): lax.all_to_all(outgoing, BOX, split_axis=0, concat_axis=0, tiled=True)  150 us
    pallas_call x6, Pallas kernels, step(): pl.pallas_call(step_kernel, out_shape=(jax.ShapeDtypeStruct((blk_dev, bs,...  33.6 us
    all_to_all x2, waiting for transfers between devices, on_device(): lax.all_to_all(outgoing, BOX, split_axis=0, concat_axis=0, tiled=True)  25.4 us
    ppermute x1, waiting for transfers between devices, on_device(): earlier_squares = lax.ppermute(squared_terms, ALL, perm_out)  22.5 us
    ppermute x1, starting transfers between devices, on_device(): coefs = lax.ppermute(coefs, ALL, perm_in)  17.1 us
    ppermute x2, waiting for transfers between devices, on_device(): lax.ppermute((present_response, partial), ALL, perm_out)  13.3 us
    all_to_all x1, starting transfers between devices, gather_rows(): arrived = lax.all_to_all(packed, BOX, 0, 0, tiled=True)  13.2 us
    all_to_all x2, starting transfers between devices, on_device(): lax.all_to_all(outgoing, BOX, split_axis=0, concat_axis=0, tiled=True)  12.5 us
  transfers between devices with their start and end apart: 16, of which 7 were waited for; matrix products, arithmetic and copies ran while one was open for 4% of the time, Pallas kernels for 0%

profile of v9, /device:TPU:96, one launch (start us, length us, event | category | flops | bytes accessed | tf_op | source)
XLA Modules:
  0.0 355.5 jit_solution(13008847180682008298)
XLA Ops:
  0.0 2.8 collective-permute-start.2
  2.8 2.3 collective-permute-start.1
  5.1 1.6 collective-permute-start.3
  6.6 1.3 collective-permute-start.4
  8.0 1.3 dynamic_slice.27
  9.9 0.8 copy.46
  10.7 0.8 constant_dynamic-slice_fusion.3
  11.7 0.7 fusion.16
  12.5 0.6 gather_fusion.3
  13.1 0.2 compare_reduce_fusion
  13.3 0.5 iota_reduce_fusion
  13.9 0.7 pad_add_fusion
  14.6 0.2 convolution_bitcast_fusion.1
  14.8 0.2 reshape.255
  15.0 0.3 fusion.4
  15.3 0.7 pad_maximum_fusion
  16.0 13.2 %all-to-all-start = ((f32[64,3,128]{2,1,0:T(4,128)}), f32[64,3,128]{2,1,0:T(4,128)S(1)}, u32[]{:S(2)}, u32[]{:S(2)}) async-start(f32[64,3,128]{2,1,0:T(4,128)} %pad_maximum_fusion), calls=%async_computation | async-start | bytes 262144 | tf_op jit(solution)/shard_map/all_to_all | solution.py:103
  29.3 7.2 %all-to-all-done = f32[64,3,128]{2,1,0:T(4,128)S(1)} async-done(((f32[64,3,128]{2,1,0:T(4,128)}), f32[64,3,128]{2,1,0:T(4,128)S(1)}, u32[]{:S(2)}, u32[]{:S(2)}) %all-to-all-start) | async-done | bytes 98336 | tf_op jit(solution)/shard_map/all_to_all | solution.py:103
  36.6 0.7 broadcast_in_dim.12
  37.3 5.9 %all-to-all-start.1 = ((f32[64,3,128]{2,1,0:T(4,128)}), f32[64,3,128]{2,1,0:T(4,128)S(1)}, u32[]{:S(2)}, u32[]{:S(2)}) async-start(f32[64,3,128]{2,1,0:T(4,128)} %broadcast_in_dim.12), calls=%async_computation.1 | async-start | bytes 262144 | tf_op jit(solution)/shard_map/all_to_all | solution.py:106
  43.3 7.2 %all-to-all-done.1 = f32[64,3,128]{2,1,0:T(4,128)S(1)} async-done(((f32[64,3,128]{2,1,0:T(4,128)}), f32[64,3,128]{2,1,0:T(4,128)S(1)}, u32[]{:S(2)}, u32[]{:S(2)}) %all-to-all-start.1) | async-done | bytes 98336 | tf_op jit(solution)/shard_map/all_to_all | solution.py:106
  50.7 0.1 reduce_sum.31
  50.9 0.1 reshape_squeeze.3
  51.1 0.4 fusion.2
  51.5 0.1 copy.51
  51.6 1.0 gather_fusion.4
  52.6 1.6 broadcast_select_fusion
  54.1 6.0 %all-to-all-start.2 = ((bf16[64,128,128]{2,1,0:T(8,128)(2,1)}), bf16[64,128,128]{2,1,0:T(8,128)(2,1)S(1)}, u32[]{:S(2)}, u32[]{:S(2)}) async-start(bf16[64,128,128]{2,1,0:T(8,128)(2,1)} %broadcast_select_fusion), calls=%async_computation.2 | async-start | bytes 4194304 | tf_op jit(solution)/shard_map/all_to_all | solution.py:173
  60.2 17.1 %collective-permute-start.5 = (bf16[4,16,128,128]{3,2,1,0:T(8,128)(2,1)}, bf16[4,16,128,128]{3,2,1,0:T(8,128)(2,1)}, u32[]{:S(2)}, u32[]{:S(2)}) collective-permute-start(bf16[4,16,128,128]{3,2,1,0:T(8,128)(2,1)} %param.8), channel_id=1, source_target_pairs={{0,0},{225,1},{194,2},{163,3},{164,4},{197,5},{230,6},{7,7},{8,8},... | collective-permute-start | bytes 6291464 | tf_op jit(solution)/shard_map/ppermute | solution.py:115
  77.5 0.1 reshape.260
  77.6 0.6 gather_fusion
  78.2 0.2 reduce_window_sum.11
  78.4 0.1 add.227
  78.5 0.7 fusion.14
  79.2 0.8 gather_fusion.1
  80.0 1.3 gather_fusion.2
  81.3 0.7 convert_multiply_fusion.sq_ref
  82.0 3.3 copy_bitcast_fusion.coefs_ref
  85.3 20.9 %all-to-all-done.2.arrived_ref = bf16[64,128,128]{2,1,0:T(8,128)(2,1)S(1)} async-done(((bf16[64,128,128]{2,1,0:T(8,128)(2,1)}), bf16[64,128,128]{2,1,0:T(8,128)(2,1)S(1)}, u32[]{:S(2)}, u32[]{:S(2)}) %all-to-all-start.2) | async-done | bytes 2097184 | tf_op jit(solution)/shard_map/all_to_all | solution.py:173
  106.1 1.3 copy-done.1
  107.5 5.6 %shard_map.82 = (bf16[4,128,128]{2,1,0:T(8,128)(2,1)}, f32[4,128,128]{2,1,0:T(8,128)}, bf16[64,128,128]{2,1,0:T(8,128)(2,1)}) custom-call(s32[64]{0:T(128)} %gather_fusion.2, s32[64]{0:T(128)} %copy-done.3, bf16[64,128,128]{2,1,0:T(8,128)(2,1)} %copy-done.1, bf16[4,128,2048]{2,1,0:T(8,128)(2,1)} %copy_bitcast_fusion.coefs_ref, ...), custom_call_target="tpu_custom_call", output_to_operand_aliasing={{1}: (4, {})} | custom-call | tf_op jit(solution)/shard_map/pallas_call | solution.py:76
  113.1 46.6 %all_to_all.40.arrived_ref = bf16[64,128,128]{2,1,0:T(8,128)(2,1)} all-to-all(bf16[64,128,128]{2,1,0:T(8,128)(2,1)} %get-tuple-element.19), channel_id=1, replica_groups=mesh['zh'=4,'zl'=2,'y'=4,'c'=2,'x'=4] {'zl','y','c','x'}, dimensions={0} | all-to-all | bytes 4194304 | tf_op jit(solution)/shard_map/all_to_all | solution.py:173
  159.7 5.6 %shard_map.83 = (bf16[4,128,128]{2,1,0:T(8,128)(2,1)}, f32[4,128,128]{2,1,0:T(8,128)}, bf16[64,128,128]{2,1,0:T(8,128)(2,1)}) custom-call(s32[64]{0:T(128)} %gather_fusion.2, s32[64]{0:T(128)} %copy-done.3, bf16[64,128,128]{2,1,0:T(8,128)(2,1)} %all_to_all.40.arrived_ref, ...), custom_call_target="tpu_custom_call", output_to_operand_aliasing={{1}: (4, {})} | custom-call | tf_op jit(solution)/shard_map/pallas_call | solution.py:76
  165.3 34.6 %all_to_all.41.arrived_ref = bf16[64,128,128]{2,1,0:T(8,128)(2,1)} all-to-all(bf16[64,128,128]{2,1,0:T(8,128)(2,1)} %get-tuple-element.21), channel_id=1, replica_groups=mesh['zh'=4,'zl'=2,'y'=4,'c'=2,'x'=4] {'zl','y','c','x'}, dimensions={0} | all-to-all | bytes 4194304 | tf_op jit(solution)/shard_map/all_to_all | solution.py:173
  199.9 5.6 %shard_map.84 = (bf16[4,128,128]{2,1,0:T(8,128)(2,1)}, f32[4,128,128]{2,1,0:T(8,128)}, bf16[64,128,128]{2,1,0:T(8,128)(2,1)}) custom-call(s32[64]{0:T(128)} %gather_fusion.2, s32[64]{0:T(128)} %copy-done.3, bf16[64,128,128]{2,1,0:T(8,128)(2,1)} %all_to_all.41.arrived_ref, ...), custom_call_target="tpu_custom_call", output_to_operand_aliasing={{1}: (4, {})} | custom-call | tf_op jit(solution)/shard_map/pallas_call | solution.py:76
  205.5 34.4 %all_to_all.42.arrived_ref = bf16[64,128,128]{2,1,0:T(8,128)(2,1)} all-to-all(bf16[64,128,128]{2,1,0:T(8,128)(2,1)} %get-tuple-element.23), channel_id=1, replica_groups=mesh['zh'=4,'zl'=2,'y'=4,'c'=2,'x'=4] {'zl','y','c','x'}, dimensions={0} | all-to-all | bytes 4194304 | tf_op jit(solution)/shard_map/all_to_all | solution.py:173
  239.9 5.6 %shard_map.85 = (bf16[4,128,128]{2,1,0:T(8,128)(2,1)}, f32[4,128,128]{2,1,0:T(8,128)}, bf16[64,128,128]{2,1,0:T(8,128)(2,1)}) custom-call(s32[64]{0:T(128)} %gather_fusion.2, s32[64]{0:T(128)} %copy-done.3, bf16[64,128,128]{2,1,0:T(8,128)(2,1)} %all_to_all.42.arrived_ref, ...), custom_call_target="tpu_custom_call", output_to_operand_aliasing={{1}: (4, {})} | custom-call | tf_op jit(solution)/shard_map/pallas_call | solution.py:76
  245.5 34.4 %all_to_all.43.arrived_ref = bf16[64,128,128]{2,1,0:T(8,128)(2,1)} all-to-all(bf16[64,128,128]{2,1,0:T(8,128)(2,1)} %get-tuple-element.25), channel_id=1, replica_groups=mesh['zh'=4,'zl'=2,'y'=4,'c'=2,'x'=4] {'zl','y','c','x'}, dimensions={0} | all-to-all | bytes 4194304 | tf_op jit(solution)/shard_map/all_to_all | solution.py:173
  279.9 5.6 %shard_map.86 = (bf16[4,128,128]{2,1,0:T(8,128)(2,1)}, f32[4,128,128]{2,1,0:T(8,128)}, bf16[64,128,128]{2,1,0:T(8,128)(2,1)}) custom-call(s32[64]{0:T(128)} %gather_fusion.2, s32[64]{0:T(128)} %copy-done.3, bf16[64,128,128]{2,1,0:T(8,128)(2,1)} %all_to_all.43.arrived_ref, ...), custom_call_target="tpu_custom_call", output_to_operand_aliasing={{1}: (4, {})} | custom-call | tf_op jit(solution)/shard_map/pallas_call | solution.py:76
  285.5 6.5 %all-to-all-start.7 = ((bf16[64,128,128]{2,1,0:T(8,128)(2,1)}), bf16[64,128,128]{2,1,0:T(8,128)(2,1)S(1)}, u32[]{:S(2)}, u32[]{:S(2)}) async-start(bf16[64,128,128]{2,1,0:T(8,128)(2,1)} %get-tuple-element.28), calls=%async_computation.7 | async-start | bytes 4194304 | tf_op jit(solution)/shard_map/all_to_all | solution.py:178
  292.0 3.4 collective-permute-start.6
  295.4 22.5 %collective-permute-done.6 = f32[4,128,128]{2,1,0:T(8,128)S(1)} collective-permute-done((f32[4,128,128]{2,1,0:T(8,128)S(1)}, f32[4,128,128]{2,1,0:T(8,128)S(1)}, u32[]{:S(2)}, u32[]{:S(2)}) %collective-permute-start.6) | collective-permute-done | bytes 262176 | tf_op jit(solution)/shard_map/ppermute | solution.py:177
  318.0 4.6 %all-to-all-done.7.arrived_ref = bf16[64,128,128]{2,1,0:T(8,128)(2,1)S(1)} async-done(((bf16[64,128,128]{2,1,0:T(8,128)(2,1)}), bf16[64,128,128]{2,1,0:T(8,128)(2,1)S(1)}, u32[]{:S(2)}, u32[]{:S(2)}) %all-to-all-start.7) | async-done | bytes 2097184 | tf_op jit(solution)/shard_map/all_to_all | solution.py:178
  322.5 1.3 copy-done.2
  323.8 5.6 %shard_map.87 = (bf16[4,128,128]{2,1,0:T(8,128)(2,1)}, f32[4,128,128]{2,1,0:T(8,128)}, bf16[64,128,128]{2,1,0:T(8,128)(2,1)}) custom-call(s32[64]{0:T(128)} %gather_fusion.2, s32[64]{0:T(128)} %copy-done.3, bf16[64,128,128]{2,1,0:T(8,128)(2,1)} %copy-done.2, bf16[4,128,2048]{2,1,0:T(8,128)(2,1)} %copy_bitcast_fusion.coefs_ref, ...), custom_call_target="tpu_custom_call", output_to_operand_aliasing={{1}: (4, {})} | custom-call | tf_op jit(solution)/shard_map/pallas_call | solution.py:76
  329.4 1.1 reduce_sum.32
  330.5 2.6 collective-permute-start.8
  333.2 6.1 %collective-permute-done.8 = f32[4,128]{1,0:T(4,128)S(1)} collective-permute-done((f32[4,128]{1,0:T(4,128)S(1)}, f32[4,128]{1,0:T(4,128)S(1)}, u32[]{:S(2)}, u32[]{:S(2)}) %collective-permute-start.8) | collective-permute-done | bytes 2080 | tf_op jit(solution)/shard_map/ppermute | solution.py:183
  339.3 0.6 collective-permute-start.9
  339.9 3.6 %collective-permute-start.10 = (f32[4,128]{1,0:T(4,128)S(1)}, f32[4,128]{1,0:T(4,128)S(1)}, u32[]{:S(2)}, u32[]{:S(2)}) collective-permute-start(f32[4,128]{1,0:T(4,128)S(1)} %collective-permute-done.8), channel_id=1, source_target_pairs={{0,2},{1,3},{2,0},{3,1},{4,6},{5,7},{6,4},{7,5},{8,10},{9,11},{10,... | collective-permute-start | bytes 6152 | tf_op jit(solution)/shard_map/ppermute | solution.py:186
  343.5 0.8 collective-permute-start.11
  344.3 3.1 collective-permute-start.7
  347.5 7.2 %collective-permute-done.7 = bf16[4,128,128]{2,1,0:T(8,128)(2,1)S(1)} collective-permute-done((bf16[4,128,128]{2,1,0:T(8,128)(2,1)}, bf16[4,128,128]{2,1,0:T(8,128)(2,1)S(1)}, u32[]{:S(2)}, u32[]{:S(2)}) %collective-permute-start.7) | collective-permute-done | bytes 131104 | tf_op jit(solution)/shard_map/ppermute | solution.py:183
  354.7 0.8 multiply_divide_fusion
  (42 shorter events, 1.0 us)
Async XLA Ops:
  0.0 13.8 %collective-permute-start.2 = (s32[128]{0:T(128)}, s32[128]{0:T(128)S(1)}, u32[]{:S(2)}, u32[]{:S(2)}) collective-permute-start(s32[128]{0:T(128)} %param.12), channel_id=1, source_target_pairs={{0,3},{1,0},{2,1},{3,2},{4,7},{5,4},{6,5},{7,6},{8,11},{9,8},{10,9... | collective-permute-start | bytes 1544 | tf_op jit(solution)/shard_map/ppermute | solution.py:130
  2.8 11.1 %collective-permute-start = (s32[128]{0:T(128)}, s32[128]{0:T(128)S(1)}, u32[]{:S(2)}, u32[]{:S(2)}) collective-permute-start(s32[128]{0:T(128)} %param.12), channel_id=1, source_target_pairs={{0,1},{1,2},{2,3},{3,0},{4,5},{5,6},{6,7},{7,4},{8,9},{9,10},{10,1... | collective-permute-start | bytes 1544 | tf_op jit(solution)/shard_map/ppermute | solution.py:130
  2.8 11.1 %collective-permute-start.1 = (s32[128]{0:T(128)}, s32[128]{0:T(128)S(1)}, u32[]{:S(2)}, u32[]{:S(2)}) collective-permute-start(s32[128]{0:T(128)} %param.12), channel_id=1, source_target_pairs={{0,2},{1,3},{2,0},{3,1},{4,6},{5,7},{6,4},{7,5},{8,10},{9,11},{10,... | collective-permute-start | bytes 1544 | tf_op jit(solution)/shard_map/ppermute | solution.py:130
  5.1 10.0 %collective-permute-start.3 = (f32[512,128]{1,0:T(8,128)}, f32[512,128]{1,0:T(8,128)S(1)}, u32[]{:S(2)}, u32[]{:S(2)}) collective-permute-start(f32[512,128]{1,0:T(8,128)} %param.10), channel_id=1, source_target_pairs={{0,0},{225,1},{194,2},{163,3},{164,4},{197,5},{230,6},{7,7},{8,8},... | collective-permute-start | bytes 786440 | tf_op jit(solution)/shard_map/ppermute | solution.py:114
  6.6 7.9 %collective-permute-start.4 = (f32[512]{0:T(512)}, f32[512]{0:T(512)S(1)}, u32[]{:S(2)}, u32[]{:S(2)}) collective-permute-start(f32[512]{0:T(512)} %param.11), channel_id=1, source_target_pairs={{0,0},{225,1},{194,2},{163,3},{164,4},{197,5},{230,6},{7,7},{8,8},... | collective-permute-start | bytes 6152 | tf_op jit(solution)/shard_map/ppermute | solution.py:114
  13.8 38.7 %copy-start.3 = (s32[64]{0:T(128)}, s32[64]{0:T(128)S(1)}, u32[]{:S(2)}) copy-start(s32[64]{0:T(128)S(1)} %get-tuple-element.18.send_ref) | copy-start | bytes 772
  16.0 20.5 %all-to-all-start = ((f32[64,3,128]{2,1,0:T(4,128)}), f32[64,3,128]{2,1,0:T(4,128)S(1)}, u32[]{:S(2)}, u32[]{:S(2)}) async-start(f32[64,3,128]{2,1,0:T(4,128)} %pad_maximum_fusion), calls=%async_computation | async-start | bytes 262144 | tf_op jit(solution)/shard_map/all_to_all | solution.py:103
  37.3 13.2 %all-to-all-start.1 = ((f32[64,3,128]{2,1,0:T(4,128)}), f32[64,3,128]{2,1,0:T(4,128)S(1)}, u32[]{:S(2)}, u32[]{:S(2)}) async-start(f32[64,3,128]{2,1,0:T(4,128)} %broadcast_in_dim.12), calls=%async_computation.1 | async-start | bytes 262144 | tf_op jit(solution)/shard_map/all_to_all | solution.py:106
  54.1 52.0 %all-to-all-start.2 = ((bf16[64,128,128]{2,1,0:T(8,128)(2,1)}), bf16[64,128,128]{2,1,0:T(8,128)(2,1)S(1)}, u32[]{:S(2)}, u32[]{:S(2)}) async-start(bf16[64,128,128]{2,1,0:T(8,128)(2,1)} %broadcast_select_fusion), calls=%async_computation.2 | async-start | bytes 4194304 | tf_op jit(solution)/shard_map/all_to_all | solution.py:173
  60.2 21.8 %collective-permute-start.5 = (bf16[4,16,128,128]{3,2,1,0:T(8,128)(2,1)}, bf16[4,16,128,128]{3,2,1,0:T(8,128)(2,1)}, u32[]{:S(2)}, u32[]{:S(2)}) collective-permute-start(bf16[4,16,128,128]{3,2,1,0:T(8,128)(2,1)} %param.8), channel_id=1, source_target_pairs={{0,0},{225,1},{194,2},{163,3},{164,4},{197,5},{230,6},{7,7},{8,8},... | collective-permute-start | bytes 6291464 | tf_op jit(solution)/shard_map/ppermute | solution.py:115
  106.1 1.3 copy-start.1
  285.5 6.5 %copy-start = (f32[4,128,128]{2,1,0:T(8,128)S(1)}, f32[4,128,128]{2,1,0:T(8,128)}, u32[]{:S(2)}) copy-start(f32[4,128,128]{2,1,0:T(8,128)} %get-tuple-element.27.sq_ref) | copy-start | bytes 786436
  285.5 37.0 %all-to-all-start.7 = ((bf16[64,128,128]{2,1,0:T(8,128)(2,1)}), bf16[64,128,128]{2,1,0:T(8,128)(2,1)S(1)}, u32[]{:S(2)}, u32[]{:S(2)}) async-start(bf16[64,128,128]{2,1,0:T(8,128)(2,1)} %get-tuple-element.28), calls=%async_computation.7 | async-start | bytes 4194304 | tf_op jit(solution)/shard_map/all_to_all | solution.py:178
  292.0 25.9 %collective-permute-start.6 = (f32[4,128,128]{2,1,0:T(8,128)S(1)}, f32[4,128,128]{2,1,0:T(8,128)S(1)}, u32[]{:S(2)}, u32[]{:S(2)}) collective-permute-start(f32[4,128,128]{2,1,0:T(8,128)S(1)} %copy-done), channel_id=1, source_target_pairs={{0,0},{1,224},{2,192},{3,160},{4,164},{5,196},{6,228},{7,4},{8,8},... | collective-permute-start | bytes 786440 | tf_op jit(solution)/shard_map/ppermute | solution.py:177
  322.5 1.3 copy-start.2
  330.5 8.8 %collective-permute-start.8 = (f32[4,128]{1,0:T(4,128)S(1)}, f32[4,128]{1,0:T(4,128)S(1)}, u32[]{:S(2)}, u32[]{:S(2)}) collective-permute-start(f32[4,128]{1,0:T(4,128)S(1)} %reduce_sum.32), channel_id=1, source_target_pairs={{0,0},{1,224},{2,192},{3,160},{4,164},{5,196},{6,228},{7,4},{8,8},... | collective-permute-start | bytes 6152 | tf_op jit(solution)/shard_map/ppermute | solution.py:183
  339.3 8.1 %collective-permute-start.9 = (f32[4,128]{1,0:T(4,128)S(1)}, f32[4,128]{1,0:T(4,128)S(1)}, u32[]{:S(2)}, u32[]{:S(2)}) collective-permute-start(f32[4,128]{1,0:T(4,128)S(1)} %collective-permute-done.8), channel_id=1, source_target_pairs={{0,1},{1,2},{2,3},{3,0},{4,5},{5,6},{6,7},{7,4},{8,9},{9,10},{10,1... | collective-permute-start | bytes 6152 | tf_op jit(solution)/shard_map/ppermute | solution.py:186
  339.9 7.5 %collective-permute-start.10 = (f32[4,128]{1,0:T(4,128)S(1)}, f32[4,128]{1,0:T(4,128)S(1)}, u32[]{:S(2)}, u32[]{:S(2)}) collective-permute-start(f32[4,128]{1,0:T(4,128)S(1)} %collective-permute-done.8), channel_id=1, source_target_pairs={{0,2},{1,3},{2,0},{3,1},{4,6},{5,7},{6,4},{7,5},{8,10},{9,11},{10,... | collective-permute-start | bytes 6152 | tf_op jit(solution)/shard_map/ppermute | solution.py:186
  343.5 4.0 %collective-permute-start.11 = (f32[4,128]{1,0:T(4,128)S(1)}, f32[4,128]{1,0:T(4,128)S(1)}, u32[]{:S(2)}, u32[]{:S(2)}) collective-permute-start(f32[4,128]{1,0:T(4,128)S(1)} %collective-permute-done.8), channel_id=1, source_target_pairs={{0,3},{1,0},{2,1},{3,2},{4,7},{5,4},{6,5},{7,6},{8,11},{9,8},{10,9... | collective-permute-start | bytes 6152 | tf_op jit(solution)/shard_map/ppermute | solution.py:186
  344.3 10.4 %collective-permute-start.7 = (bf16[4,128,128]{2,1,0:T(8,128)(2,1)}, bf16[4,128,128]{2,1,0:T(8,128)(2,1)S(1)}, u32[]{:S(2)}, u32[]{:S(2)}) collective-permute-start(bf16[4,128,128]{2,1,0:T(8,128)(2,1)} %get-tuple-element.29), channel_id=1, source_target_pairs={{0,0},{1,224},{2,192},{3,160},{4,164},{5,196},{6,228},{7,4},{8,8},... | collective-permute-start | bytes 393224 | tf_op jit(solution)/shard_map/ppermute | solution.py:183

commit v10 on v6

--- a/solution.py
+++ b/solution.py
@@ -57,6 +57,8 @@
         present_ref[r] = rounded
         wide = rounded.astype(jnp.float32)
         sq_out_ref[r] = sq_ref[r] + wide * wide
+    if out_hbm is None:
+        return
     copies = []
     for v in range(out_hbm.shape[0]):
         cp = pltpu.make_async_copy(present_ref.at[send_ref[v]], out_hbm.at[v], sems.at[v])
@@ -66,22 +68,27 @@
         cp.wait()
 
 
-def step(take, send, arrived, coefs_wide, squares):
+def last_kernel(take_ref, send_ref, arrived_ref, coefs_ref, sq_ref, present_ref, sq_out_ref, lag_buf, sems):
+    step_kernel(take_ref, send_ref, arrived_ref, coefs_ref, sq_ref, present_ref, sq_out_ref, None, lag_buf, sems)
+
+
+def step(take, send, arrived, coefs_wide, squares, last=False):
     blk_dev, bs, width = coefs_wide.shape
     cols = arrived.shape[2]
     n_out = send.shape[0]
     smem = pl.BlockSpec(memory_space=pltpu.SMEM)
     vmem = pl.BlockSpec(memory_space=pltpu.VMEM)
     hbm = pl.BlockSpec(memory_space=pl.ANY)
+    shapes = (
+        jax.ShapeDtypeStruct((blk_dev, bs, cols), jnp.bfloat16),
+        jax.ShapeDtypeStruct((blk_dev, bs, cols), jnp.float32),
+        jax.ShapeDtypeStruct((n_out, bs, cols), jnp.bfloat16),
+    )
     return pl.pallas_call(
-        step_kernel,
-        out_shape=(
-            jax.ShapeDtypeStruct((blk_dev, bs, cols), jnp.bfloat16),
-            jax.ShapeDtypeStruct((blk_dev, bs, cols), jnp.float32),
-            jax.ShapeDtypeStruct((n_out, bs, cols), jnp.bfloat16),
-        ),
+        last_kernel if last else step_kernel,
+        out_shape=shapes[:2] if last else shapes,
         in_specs=[smem, smem, vmem, vmem, vmem],
-        out_specs=(vmem, vmem, hbm),
+        out_specs=(vmem, vmem) if last else (vmem, vmem, hbm),
         scratch_shapes=[
             pltpu.VMEM((width, cols), jnp.bfloat16),
             pltpu.SemaphoreType.DMA((n_out,)),
@@ -171,9 +178,12 @@
         coefs_wide = coefs.transpose(0, 2, 1, 3).reshape(blk_dev, block_size, lags * block_size)
         for step_no in range(HORIZONS - 1):
             arriving_response = lax.all_to_all(outgoing, BOX, split_axis=0, concat_axis=0, tiled=True)
-            present_response, squared_terms, outgoing = step(
-                take_index, send_idx, arriving_response, coefs_wide, squared_terms
+            made = step(
+                take_index, send_idx, arriving_response, coefs_wide, squared_terms,
+                last=step_no == HORIZONS - 2,
             )
+            present_response, squared_terms = made[:2]
+            outgoing = made[-1]
         partial = jnp.sum(squared_terms, axis=2)
         squared_terms, partial = lax.ppermute((squared_terms, partial), ALL, perm_out)
         totals = lax.psum(partial, "x")

time: 359 us -> 358 us (level)
  no operation moved by 1% of the time
where the time goes in v10:
time: 358 us; the launch traced here: 352 us
  blocking collectives  196 us (55%)
  starting transfers between devices  58.6 us (16%)
  waiting for transfers between devices  41.1 us (11%)
  Pallas kernels  32.3 us (9%)
  local copies, waits for them, and re-layouts  14.4 us (4%)
  other arithmetic  7.57 us (2%)
    all_to_all x5, blocking collectives, on_device(): lax.all_to_all(outgoing, BOX, split_axis=0, concat_axis=0, tiled=True)  186 us
    pallas_call x6, Pallas kernels, step(): pl.pallas_call(last_kernel if last else step_kernel, out_shape=shapes[:2]...  32.3 us
    all_to_all x1, waiting for transfers between devices, on_device(): lax.all_to_all(outgoing, BOX, split_axis=0, concat_axis=0, tiled=True)  19.9 us
    ppermute x1, starting transfers between devices, on_device(): coefs = lax.ppermute(coefs, ALL, perm_in)  17.1 us
    all_to_all x1, starting transfers between devices, gather_rows(): arrived = lax.all_to_all(packed, BOX, 0, 0, tiled=True)  17 us
    psum x1, blocking collectives, on_device(): totals = lax.psum(partial, 'x')  10.1 us
    all_to_all x1, waiting for transfers between devices, gather_rows(): full = lax.all_to_all(spread, BOX, 0, 0, tiled=True)  7.21 us
    all_to_all x1, waiting for transfers between devices, gather_rows(): arrived = lax.all_to_all(packed, BOX, 0, 0, tiled=True)  7.2 us
  transfers between devices with their start and end apart: 11, of which 4 were waited for; matrix products, arithmetic and copies ran while one was open for 4% of the time, Pallas kernels for 0%

profile of v10, /device:TPU:96, one launch (start us, length us, event | category | flops | bytes accessed | tf_op | source)
XLA Modules:
  0.0 352.4 jit_solution(4550381972439263832)
XLA Ops:
  0.0 1.5 collective-permute-start
  1.5 1.7 collective-permute-start.2
  3.2 1.8 collective-permute-start.1
  5.1 1.3 collective-permute-start.4
  6.4 1.6 collective-permute-start.3
  8.0 1.3 dynamic_slice.15
  9.9 0.8 copy.46
  10.7 0.8 constant_dynamic-slice_fusion.3
  11.6 0.1 reshape.228
  11.7 0.7 fusion.16
  12.4 0.1 reshape.229
  12.5 0.6 gather_fusion.3
  13.1 0.2 compare_reduce_fusion
  13.3 0.5 iota_reduce_fusion
  13.9 0.7 pad_add_fusion
  14.6 0.2 convolution_bitcast_fusion.1
  14.8 0.2 reshape.231
  15.0 0.3 fusion.4
  15.3 0.7 pad_maximum_fusion
  16.0 17.0 %all-to-all-start = ((f32[64,3,128]{2,1,0:T(4,128)}), f32[64,3,128]{2,1,0:T(4,128)S(1)}, u32[]{:S(2)}, u32[]{:S(2)}) async-start(f32[64,3,128]{2,1,0:T(4,128)} %pad_maximum_fusion), calls=%async_computation | async-start | bytes 262144 | tf_op jit(solution)/shard_map/all_to_all | solution.py:110
  33.1 7.2 %all-to-all-done = f32[64,3,128]{2,1,0:T(4,128)S(1)} async-done(((f32[64,3,128]{2,1,0:T(4,128)}), f32[64,3,128]{2,1,0:T(4,128)S(1)}, u32[]{:S(2)}, u32[]{:S(2)}) %all-to-all-start) | async-done | bytes 98336 | tf_op jit(solution)/shard_map/all_to_all | solution.py:110
  40.3 0.7 broadcast_in_dim.12
  41.0 5.9 %all-to-all-start.1 = ((f32[64,3,128]{2,1,0:T(4,128)}), f32[64,3,128]{2,1,0:T(4,128)S(1)}, u32[]{:S(2)}, u32[]{:S(2)}) async-start(f32[64,3,128]{2,1,0:T(4,128)} %broadcast_in_dim.12), calls=%async_computation.1 | async-start | bytes 262144 | tf_op jit(solution)/shard_map/all_to_all | solution.py:113
  47.0 7.2 %all-to-all-done.1 = f32[64,3,128]{2,1,0:T(4,128)S(1)} async-done(((f32[64,3,128]{2,1,0:T(4,128)}), f32[64,3,128]{2,1,0:T(4,128)S(1)}, u32[]{:S(2)}, u32[]{:S(2)}) %all-to-all-start.1) | async-done | bytes 98336 | tf_op jit(solution)/shard_map/all_to_all | solution.py:113
  54.2 0.1 slice_reduce_fusion
  54.3 0.1 reshape_squeeze.3
  54.5 0.1 fusion.10
  54.6 0.1 copy.50
  54.7 0.1 reduce_sum.31
  54.8 0.4 fusion.2
  55.2 0.1 copy.51
  55.3 1.0 gather_fusion.4
  56.3 1.6 broadcast_select_fusion
  57.9 6.0 %all-to-all-start.2 = ((bf16[64,128,128]{2,1,0:T(8,128)(2,1)}), bf16[64,128,128]{2,1,0:T(8,128)(2,1)S(1)}, u32[]{:S(2)}, u32[]{:S(2)}) async-start(bf16[64,128,128]{2,1,0:T(8,128)(2,1)} %broadcast_select_fusion), calls=%async_computation.2 | async-start | bytes 4194304 | tf_op jit(solution)/shard_map/all_to_all | solution.py:180
  63.9 17.1 %collective-permute-start.5 = (bf16[4,16,128,128]{3,2,1,0:T(8,128)(2,1)}, bf16[4,16,128,128]{3,2,1,0:T(8,128)(2,1)}, u32[]{:S(2)}, u32[]{:S(2)}) collective-permute-start(bf16[4,16,128,128]{3,2,1,0:T(8,128)(2,1)} %param.8), channel_id=1, source_target_pairs={{0,0},{225,1},{194,2},{163,3},{164,4},{197,5},{230,6},{7,7},{8,8},... | collective-permute-start | bytes 6291464 | tf_op jit(solution)/shard_map/ppermute | solution.py:122
  81.1 0.1 fusion.11
  81.2 0.1 reshape.236
  81.3 0.6 gather_fusion
  81.9 0.2 reduce_window_sum.11
  82.1 0.1 add.168
  82.2 0.7 fusion.14
  82.9 0.8 gather_fusion.1
  83.7 1.3 gather_fusion.2
  85.0 0.7 convert_multiply_fusion.sq_ref
  85.7 3.3 copy_bitcast_fusion.coefs_ref
  89.0 19.9 %all-to-all-done.2.arrived_ref = bf16[64,128,128]{2,1,0:T(8,128)(2,1)S(1)} async-done(((bf16[64,128,128]{2,1,0:T(8,128)(2,1)}), bf16[64,128,128]{2,1,0:T(8,128)(2,1)S(1)}, u32[]{:S(2)}, u32[]{:S(2)}) %all-to-all-start.2) | async-done | bytes 2097184 | tf_op jit(solution)/shard_map/all_to_all | solution.py:180
  108.9 1.3 copy-done
  110.2 5.6 %shard_map.82 = (bf16[4,128,128]{2,1,0:T(8,128)(2,1)}, f32[4,128,128]{2,1,0:T(8,128)}, bf16[64,128,128]{2,1,0:T(8,128)(2,1)}) custom-call(s32[64]{0:T(128)} %gather_fusion.2, s32[64]{0:T(128)} %copy-done.1, bf16[64,128,128]{2,1,0:T(8,128)(2,1)} %copy-done, bf16[4,128,2048]{2,1,0:T(8,128)(2,1)} %copy_bitcast_fusion.coefs_ref, ...), custom_call_target="tpu_custom_call", output_to_operand_aliasing={{1}: (4, {})} | custom-call | tf_op jit(solution)/shard_map/pallas_call | solution.py:87
  115.8 48.5 %all_to_all.40.arrived_ref = bf16[64,128,128]{2,1,0:T(8,128)(2,1)} all-to-all(bf16[64,128,128]{2,1,0:T(8,128)(2,1)} %get-tuple-element.18), channel_id=1, replica_groups=mesh['zh'=4,'zl'=2,'y'=4,'c'=2,'x'=4] {'zl','y','c','x'}, dimensions={0} | all-to-all | bytes 4194304 | tf_op jit(solution)/shard_map/all_to_all | solution.py:180
  164.3 5.6 %shard_map.83 = (bf16[4,128,128]{2,1,0:T(8,128)(2,1)}, f32[4,128,128]{2,1,0:T(8,128)}, bf16[64,128,128]{2,1,0:T(8,128)(2,1)}) custom-call(s32[64]{0:T(128)} %gather_fusion.2, s32[64]{0:T(128)} %copy-done.1, bf16[64,128,128]{2,1,0:T(8,128)(2,1)} %all_to_all.40.arrived_ref, ...), custom_call_target="tpu_custom_call", output_to_operand_aliasing={{1}: (4, {})} | custom-call | tf_op jit(solution)/shard_map/pallas_call | solution.py:87
  169.9 34.6 %all_to_all.41.arrived_ref = bf16[64,128,128]{2,1,0:T(8,128)(2,1)} all-to-all(bf16[64,128,128]{2,1,0:T(8,128)(2,1)} %get-tuple-element.20), channel_id=1, replica_groups=mesh['zh'=4,'zl'=2,'y'=4,'c'=2,'x'=4] {'zl','y','c','x'}, dimensions={0} | all-to-all | bytes 4194304 | tf_op jit(solution)/shard_map/all_to_all | solution.py:180
  204.5 5.6 %shard_map.84 = (bf16[4,128,128]{2,1,0:T(8,128)(2,1)}, f32[4,128,128]{2,1,0:T(8,128)}, bf16[64,128,128]{2,1,0:T(8,128)(2,1)}) custom-call(s32[64]{0:T(128)} %gather_fusion.2, s32[64]{0:T(128)} %copy-done.1, bf16[64,128,128]{2,1,0:T(8,128)(2,1)} %all_to_all.41.arrived_ref, ...), custom_call_target="tpu_custom_call", output_to_operand_aliasing={{1}: (4, {})} | custom-call | tf_op jit(solution)/shard_map/pallas_call | solution.py:87
  210.1 34.4 %all_to_all.42.arrived_ref = bf16[64,128,128]{2,1,0:T(8,128)(2,1)} all-to-all(bf16[64,128,128]{2,1,0:T(8,128)(2,1)} %get-tuple-element.22), channel_id=1, replica_groups=mesh['zh'=4,'zl'=2,'y'=4,'c'=2,'x'=4] {'zl','y','c','x'}, dimensions={0} | all-to-all | bytes 4194304 | tf_op jit(solution)/shard_map/all_to_all | solution.py:180
  244.5 5.6 %shard_map.85 = (bf16[4,128,128]{2,1,0:T(8,128)(2,1)}, f32[4,128,128]{2,1,0:T(8,128)}, bf16[64,128,128]{2,1,0:T(8,128)(2,1)}) custom-call(s32[64]{0:T(128)} %gather_fusion.2, s32[64]{0:T(128)} %copy-done.1, bf16[64,128,128]{2,1,0:T(8,128)(2,1)} %all_to_all.42.arrived_ref, ...), custom_call_target="tpu_custom_call", output_to_operand_aliasing={{1}: (4, {})} | custom-call | tf_op jit(solution)/shard_map/pallas_call | solution.py:87
  250.1 34.4 %all_to_all.43.arrived_ref = bf16[64,128,128]{2,1,0:T(8,128)(2,1)} all-to-all(bf16[64,128,128]{2,1,0:T(8,128)(2,1)} %get-tuple-element.24), channel_id=1, replica_groups=mesh['zh'=4,'zl'=2,'y'=4,'c'=2,'x'=4] {'zl','y','c','x'}, dimensions={0} | all-to-all | bytes 4194304 | tf_op jit(solution)/shard_map/all_to_all | solution.py:180
  284.5 5.6 %shard_map.86 = (bf16[4,128,128]{2,1,0:T(8,128)(2,1)}, f32[4,128,128]{2,1,0:T(8,128)}, bf16[64,128,128]{2,1,0:T(8,128)(2,1)}) custom-call(s32[64]{0:T(128)} %gather_fusion.2, s32[64]{0:T(128)} %copy-done.1, bf16[64,128,128]{2,1,0:T(8,128)(2,1)} %all_to_all.43.arrived_ref, ...), custom_call_target="tpu_custom_call", output_to_operand_aliasing={{1}: (4, {})} | custom-call | tf_op jit(solution)/shard_map/pallas_call | solution.py:87
  290.2 34.4 %all_to_all.44.arrived_ref = bf16[64,128,128]{2,1,0:T(8,128)(2,1)} all-to-all(bf16[64,128,128]{2,1,0:T(8,128)(2,1)} %get-tuple-element.26), channel_id=1, replica_groups=mesh['zh'=4,'zl'=2,'y'=4,'c'=2,'x'=4] {'zl','y','c','x'}, dimensions={0} | all-to-all | bytes 4194304 | tf_op jit(solution)/shard_map/all_to_all | solution.py:180
  324.6 4.3 %shard_map.87 = (bf16[4,128,128]{2,1,0:T(8,128)(2,1)}, f32[4,128,128]{2,1,0:T(8,128)}) custom-call(s32[64]{0:T(128)} %gather_fusion.2, s32[64]{0:T(128)} %copy-done.1, bf16[64,128,128]{2,1,0:T(8,128)(2,1)} %all_to_all.44.arrived_ref, bf16[4,128,2048]{2,1,0:T(8,128)(2,1)} %copy_bitcast_fusion.coefs_ref, ...), custom_call_target="tpu_custom_call", output_to_operand_aliasing={{1}: (4, {})} | custom-call | tf_op jit(solution)/shard_map/pallas_call | solution.py:87
  328.9 2.3 collective-permute-start.6
  331.2 1.1 reduce_sum.32
  332.3 2.3 collective-permute-start.7
  334.6 6.8 %collective-permute-done.7 = f32[4,128]{1,0:T(4,128)S(1)} collective-permute-done((f32[4,128]{1,0:T(4,128)S(1)}, f32[4,128]{1,0:T(4,128)S(1)}, u32[]{:S(2)}, u32[]{:S(2)}) %collective-permute-start.7) | collective-permute-done | bytes 2080 | tf_op jit(solution)/shard_map/ppermute | solution.py:188
  341.5 10.1 %psum.7 = f32[4,128]{1,0:T(4,128)S(1)} all-reduce(f32[4,128]{1,0:T(4,128)S(1)} %collective-permute-done.7), channel_id=1, replica_groups=mesh['zh'=4,'zl'=2,'y'=4,'c'=2,'x'=4] {'x'}, use_global_device_ids=true, to_apply=%region_7.8 | all-reduce | flops 512 | bytes 4096 | tf_op jit(solution)/shard_map/psum | solution.py:189
  351.6 0.8 multiply_divide_fusion
  (29 shorter events, 0.4 us)
Async XLA Ops:
  0.0 13.8 %collective-permute-start = (s32[128]{0:T(128)}, s32[128]{0:T(128)S(1)}, u32[]{:S(2)}, u32[]{:S(2)}) collective-permute-start(s32[128]{0:T(128)} %param.12), channel_id=1, source_target_pairs={{0,1},{1,2},{2,3},{3,0},{4,5},{5,6},{6,7},{7,4},{8,9},{9,10},{10,1... | collective-permute-start | bytes 1544 | tf_op jit(solution)/shard_map/ppermute | solution.py:137
  1.5 12.4 %collective-permute-start.2 = (s32[128]{0:T(128)}, s32[128]{0:T(128)S(1)}, u32[]{:S(2)}, u32[]{:S(2)}) collective-permute-start(s32[128]{0:T(128)} %param.12), channel_id=1, source_target_pairs={{0,3},{1,0},{2,1},{3,2},{4,7},{5,4},{6,5},{7,6},{8,11},{9,8},{10,9... | collective-permute-start | bytes 1544 | tf_op jit(solution)/shard_map/ppermute | solution.py:137
  3.2 10.6 %collective-permute-start.1 = (s32[128]{0:T(128)}, s32[128]{0:T(128)S(1)}, u32[]{:S(2)}, u32[]{:S(2)}) collective-permute-start(s32[128]{0:T(128)} %param.12), channel_id=1, source_target_pairs={{0,2},{1,3},{2,0},{3,1},{4,6},{5,7},{6,4},{7,5},{8,10},{9,11},{10,... | collective-permute-start | bytes 1544 | tf_op jit(solution)/shard_map/ppermute | solution.py:137
  5.1 9.5 %collective-permute-start.4 = (f32[512]{0:T(512)}, f32[512]{0:T(512)S(1)}, u32[]{:S(2)}, u32[]{:S(2)}) collective-permute-start(f32[512]{0:T(512)} %param.11), channel_id=1, source_target_pairs={{0,0},{225,1},{194,2},{163,3},{164,4},{197,5},{230,6},{7,7},{8,8},... | collective-permute-start | bytes 6152 | tf_op jit(solution)/shard_map/ppermute | solution.py:121
  6.4 8.6 %collective-permute-start.3 = (f32[512,128]{1,0:T(8,128)}, f32[512,128]{1,0:T(8,128)S(1)}, u32[]{:S(2)}, u32[]{:S(2)}) collective-permute-start(f32[512,128]{1,0:T(8,128)} %param.10), channel_id=1, source_target_pairs={{0,0},{225,1},{194,2},{163,3},{164,4},{197,5},{230,6},{7,7},{8,8},... | collective-permute-start | bytes 786440 | tf_op jit(solution)/shard_map/ppermute | solution.py:121
  13.8 42.5 %copy-start.1 = (s32[64]{0:T(128)}, s32[64]{0:T(128)S(1)}, u32[]{:S(2)}) copy-start(s32[64]{0:T(128)S(1)} %get-tuple-element.17.send_ref) | copy-start | bytes 772
  16.0 24.2 %all-to-all-start = ((f32[64,3,128]{2,1,0:T(4,128)}), f32[64,3,128]{2,1,0:T(4,128)S(1)}, u32[]{:S(2)}, u32[]{:S(2)}) async-start(f32[64,3,128]{2,1,0:T(4,128)} %pad_maximum_fusion), calls=%async_computation | async-start | bytes 262144 | tf_op jit(solution)/shard_map/all_to_all | solution.py:110
  41.0 13.2 %all-to-all-start.1 = ((f32[64,3,128]{2,1,0:T(4,128)}), f32[64,3,128]{2,1,0:T(4,128)S(1)}, u32[]{:S(2)}, u32[]{:S(2)}) async-start(f32[64,3,128]{2,1,0:T(4,128)} %broadcast_in_dim.12), calls=%async_computation.1 | async-start | bytes 262144 | tf_op jit(solution)/shard_map/all_to_all | solution.py:113
  57.9 51.0 %all-to-all-start.2 = ((bf16[64,128,128]{2,1,0:T(8,128)(2,1)}), bf16[64,128,128]{2,1,0:T(8,128)(2,1)S(1)}, u32[]{:S(2)}, u32[]{:S(2)}) async-start(bf16[64,128,128]{2,1,0:T(8,128)(2,1)} %broadcast_select_fusion), calls=%async_computation.2 | async-start | bytes 4194304 | tf_op jit(solution)/shard_map/all_to_all | solution.py:180
  63.9 21.9 %collective-permute-start.5 = (bf16[4,16,128,128]{3,2,1,0:T(8,128)(2,1)}, bf16[4,16,128,128]{3,2,1,0:T(8,128)(2,1)}, u32[]{:S(2)}, u32[]{:S(2)}) collective-permute-start(bf16[4,16,128,128]{3,2,1,0:T(8,128)(2,1)} %param.8), channel_id=1, source_target_pairs={{0,0},{225,1},{194,2},{163,3},{164,4},{197,5},{230,6},{7,7},{8,8},... | collective-permute-start | bytes 6291464 | tf_op jit(solution)/shard_map/ppermute | solution.py:122
  108.9 1.3 copy-start
  328.9 22.7 %collective-permute-start.6 = (f32[4,128,128]{2,1,0:T(8,128)}, f32[4,128,128]{2,1,0:T(8,128)S(1)}, u32[]{:S(2)}, u32[]{:S(2)}) collective-permute-start(f32[4,128,128]{2,1,0:T(8,128)} %get-tuple-element.28), channel_id=1, source_target_pairs={{0,0},{1,224},{2,192},{3,160},{4,164},{5,196},{6,228},{7,4},{8,8},... | collective-permute-start | bytes 786440 | tf_op jit(solution)/shard_map/ppermute | solution.py:188
  332.3 9.1 %collective-permute-start.7 = (f32[4,128]{1,0:T(4,128)S(1)}, f32[4,128]{1,0:T(4,128)S(1)}, u32[]{:S(2)}, u32[]{:S(2)}) collective-permute-start(f32[4,128]{1,0:T(4,128)S(1)} %reduce_sum.32), channel_id=1, source_target_pairs={{0,0},{1,224},{2,192},{3,160},{4,164},{5,196},{6,228},{7,4},{8,8},... | collective-permute-start | bytes 6152 | tf_op jit(solution)/shard_map/ppermute | solution.py:188

commit v11 on v10

--- a/solution.py
+++ b/solution.py
@@ -68,8 +68,10 @@
         cp.wait()
 
 
-def last_kernel(take_ref, send_ref, arrived_ref, coefs_ref, sq_ref, present_ref, sq_out_ref, lag_buf, sems):
+def last_kernel(take_ref, send_ref, arrived_ref, coefs_ref, sq_ref, present_ref, sq_out_ref, part_ref, lag_buf, sems):
     step_kernel(take_ref, send_ref, arrived_ref, coefs_ref, sq_ref, present_ref, sq_out_ref, None, lag_buf, sems)
+    for r in range(part_ref.shape[0]):
+        part_ref[r] = jnp.sum(sq_out_ref[r], axis=1)
 
 
 def step(take, send, arrived, coefs_wide, squares, last=False):
@@ -84,11 +86,12 @@
         jax.ShapeDtypeStruct((blk_dev, bs, cols), jnp.float32),
         jax.ShapeDtypeStruct((n_out, bs, cols), jnp.bfloat16),
     )
+    part = jax.ShapeDtypeStruct((blk_dev, bs), jnp.float32)
     return pl.pallas_call(
         last_kernel if last else step_kernel,
-        out_shape=shapes[:2] if last else shapes,
+        out_shape=shapes[:2] + (part,) if last else shapes,
         in_specs=[smem, smem, vmem, vmem, vmem],
-        out_specs=(vmem, vmem) if last else (vmem, vmem, hbm),
+        out_specs=(vmem, vmem, vmem) if last else (vmem, vmem, hbm),
         scratch_shapes=[
             pltpu.VMEM((width, cols), jnp.bfloat16),
             pltpu.SemaphoreType.DMA((n_out,)),
@@ -184,7 +187,7 @@
             )
             present_response, squared_terms = made[:2]
             outgoing = made[-1]
-        partial = jnp.sum(squared_terms, axis=2)
+        partial = made[-1]
         squared_terms, partial = lax.ppermute((squared_terms, partial), ALL, perm_out)
         totals = lax.psum(partial, "x")
         total_shocks = shock_columns * xs

time: 358 us -> 358 us (level)
  no operation moved by 1% of the time
where the time goes in v11:
time: 358 us; the launch traced here: 351 us
  blocking collectives  196 us (55%)
  starting transfers between devices  58.6 us (16%)
  waiting for transfers between devices  42.2 us (12%)
  Pallas kernels  32.3 us (9%)
  local copies, waits for them, and re-layouts  14.4 us (4%)
  other arithmetic  6.47 us (2%)
    all_to_all x5, blocking collectives, on_device(): lax.all_to_all(outgoing, BOX, split_axis=0, concat_axis=0, tiled=True)  186 us
    pallas_call x6, Pallas kernels, step(): pl.pallas_call(last_kernel if last else step_kernel, out_shape=shapes[:2]...  32.3 us
    all_to_all x1, waiting for transfers between devices, on_device(): lax.all_to_all(outgoing, BOX, split_axis=0, concat_axis=0, tiled=True)  19.9 us
    ppermute x1, starting transfers between devices, on_device(): coefs = lax.ppermute(coefs, ALL, perm_in)  17.1 us
    all_to_all x1, starting transfers between devices, gather_rows(): arrived = lax.all_to_all(packed, BOX, 0, 0, tiled=True)  17 us
    psum x1, blocking collectives, on_device(): totals = lax.psum(partial, 'x')  9.16 us
    ppermute x2, waiting for transfers between devices, on_device(): lax.ppermute((squared_terms, partial), ALL, perm_out)  7.92 us
    all_to_all x1, waiting for transfers between devices, gather_rows(): full = lax.all_to_all(spread, BOX, 0, 0, tiled=True)  7.21 us
  transfers between devices with their start and end apart: 11, of which 4 were waited for; matrix products, arithmetic and copies ran while one was open for 4% of the time, Pallas kernels for 0%

profile of v11, /device:TPU:96, one launch (start us, length us, event | category | flops | bytes accessed | tf_op | source)
XLA Modules:
  0.0 351.5 jit_solution(7340865827271119935)
XLA Ops:
  0.0 1.5 collective-permute-start
  1.5 1.7 collective-permute-start.2
  3.2 1.8 collective-permute-start.1
  5.1 1.3 collective-permute-start.4
  6.4 1.6 collective-permute-start.3
  8.0 1.3 dynamic_slice.15
  9.9 0.8 copy.46
  10.7 0.8 constant_dynamic-slice_fusion.3
  11.5 0.1 copy.44
  11.6 0.1 reshape.228
  11.7 0.7 fusion.16
  12.4 0.1 reshape.229
  12.5 0.6 gather_fusion.3
  13.1 0.2 compare_reduce_fusion
  13.3 0.5 iota_reduce_fusion
  13.9 0.7 pad_add_fusion
  14.6 0.2 convolution_bitcast_fusion.1
  14.8 0.2 reshape.231
  15.0 0.3 fusion.4
  15.3 0.7 pad_maximum_fusion
  16.0 17.0 %all-to-all-start = ((f32[64,3,128]{2,1,0:T(4,128)}), f32[64,3,128]{2,1,0:T(4,128)S(1)}, u32[]{:S(2)}, u32[]{:S(2)}) async-start(f32[64,3,128]{2,1,0:T(4,128)} %pad_maximum_fusion), calls=%async_computation | async-start | bytes 262144 | tf_op jit(solution)/shard_map/all_to_all | solution.py:113
  33.1 7.2 %all-to-all-done = f32[64,3,128]{2,1,0:T(4,128)S(1)} async-done(((f32[64,3,128]{2,1,0:T(4,128)}), f32[64,3,128]{2,1,0:T(4,128)S(1)}, u32[]{:S(2)}, u32[]{:S(2)}) %all-to-all-start) | async-done | bytes 98336 | tf_op jit(solution)/shard_map/all_to_all | solution.py:113
  40.3 0.7 broadcast_in_dim.12
  41.0 5.9 %all-to-all-start.1 = ((f32[64,3,128]{2,1,0:T(4,128)}), f32[64,3,128]{2,1,0:T(4,128)S(1)}, u32[]{:S(2)}, u32[]{:S(2)}) async-start(f32[64,3,128]{2,1,0:T(4,128)} %broadcast_in_dim.12), calls=%async_computation.1 | async-start | bytes 262144 | tf_op jit(solution)/shard_map/all_to_all | solution.py:116
  47.0 7.2 %all-to-all-done.1 = f32[64,3,128]{2,1,0:T(4,128)S(1)} async-done(((f32[64,3,128]{2,1,0:T(4,128)}), f32[64,3,128]{2,1,0:T(4,128)S(1)}, u32[]{:S(2)}, u32[]{:S(2)}) %all-to-all-start.1) | async-done | bytes 98336 | tf_op jit(solution)/shard_map/all_to_all | solution.py:116
  54.2 0.1 slice_reduce_fusion
  54.3 0.1 reshape_squeeze.3
  54.5 0.1 fusion.10
  54.6 0.1 copy.50
  54.7 0.1 reduce_sum.22
  54.8 0.4 fusion.2
  55.2 0.1 copy.51
  55.3 1.0 gather_fusion.4
  56.3 1.6 broadcast_select_fusion
  57.9 6.0 %all-to-all-start.2 = ((bf16[64,128,128]{2,1,0:T(8,128)(2,1)}), bf16[64,128,128]{2,1,0:T(8,128)(2,1)S(1)}, u32[]{:S(2)}, u32[]{:S(2)}) async-start(bf16[64,128,128]{2,1,0:T(8,128)(2,1)} %broadcast_select_fusion), calls=%async_computation.2 | async-start | bytes 4194304 | tf_op jit(solution)/shard_map/all_to_all | solution.py:183
  63.9 17.1 %collective-permute-start.5 = (bf16[4,16,128,128]{3,2,1,0:T(8,128)(2,1)}, bf16[4,16,128,128]{3,2,1,0:T(8,128)(2,1)}, u32[]{:S(2)}, u32[]{:S(2)}) collective-permute-start(bf16[4,16,128,128]{3,2,1,0:T(8,128)(2,1)} %param.8), channel_id=1, source_target_pairs={{0,0},{225,1},{194,2},{163,3},{164,4},{197,5},{230,6},{7,7},{8,8},... | collective-permute-start | bytes 6291464 | tf_op jit(solution)/shard_map/ppermute | solution.py:125
  81.1 0.1 fusion.11
  81.2 0.1 reshape.236
  81.3 0.6 gather_fusion
  81.9 0.2 reduce_window_sum.11
  82.1 0.1 add.168
  82.2 0.7 fusion.14
  82.9 0.8 gather_fusion.1
  83.7 1.3 gather_fusion.2
  85.0 0.7 convert_multiply_fusion.sq_ref
  85.7 3.3 copy_bitcast_fusion.coefs_ref
  89.0 19.9 %all-to-all-done.2.arrived_ref = bf16[64,128,128]{2,1,0:T(8,128)(2,1)S(1)} async-done(((bf16[64,128,128]{2,1,0:T(8,128)(2,1)}), bf16[64,128,128]{2,1,0:T(8,128)(2,1)S(1)}, u32[]{:S(2)}, u32[]{:S(2)}) %all-to-all-start.2) | async-done | bytes 2097184 | tf_op jit(solution)/shard_map/all_to_all | solution.py:183
  108.9 1.3 copy-done
  110.2 5.6 %shard_map.82 = (bf16[4,128,128]{2,1,0:T(8,128)(2,1)}, f32[4,128,128]{2,1,0:T(8,128)}, bf16[64,128,128]{2,1,0:T(8,128)(2,1)}) custom-call(s32[64]{0:T(128)} %gather_fusion.2, s32[64]{0:T(128)} %copy-done.1, bf16[64,128,128]{2,1,0:T(8,128)(2,1)} %copy-done, bf16[4,128,2048]{2,1,0:T(8,128)(2,1)} %copy_bitcast_fusion.coefs_ref, ...), custom_call_target="tpu_custom_call", output_to_operand_aliasing={{1}: (4, {})} | custom-call | tf_op jit(solution)/shard_map/pallas_call | solution.py:90
  115.8 48.5 %all_to_all.40.arrived_ref = bf16[64,128,128]{2,1,0:T(8,128)(2,1)} all-to-all(bf16[64,128,128]{2,1,0:T(8,128)(2,1)} %get-tuple-element.19), channel_id=1, replica_groups=mesh['zh'=4,'zl'=2,'y'=4,'c'=2,'x'=4] {'zl','y','c','x'}, dimensions={0} | all-to-all | bytes 4194304 | tf_op jit(solution)/shard_map/all_to_all | solution.py:183
  164.3 5.6 %shard_map.83 = (bf16[4,128,128]{2,1,0:T(8,128)(2,1)}, f32[4,128,128]{2,1,0:T(8,128)}, bf16[64,128,128]{2,1,0:T(8,128)(2,1)}) custom-call(s32[64]{0:T(128)} %gather_fusion.2, s32[64]{0:T(128)} %copy-done.1, bf16[64,128,128]{2,1,0:T(8,128)(2,1)} %all_to_all.40.arrived_ref, ...), custom_call_target="tpu_custom_call", output_to_operand_aliasing={{1}: (4, {})} | custom-call | tf_op jit(solution)/shard_map/pallas_call | solution.py:90
  169.9 34.6 %all_to_all.41.arrived_ref = bf16[64,128,128]{2,1,0:T(8,128)(2,1)} all-to-all(bf16[64,128,128]{2,1,0:T(8,128)(2,1)} %get-tuple-element.21), channel_id=1, replica_groups=mesh['zh'=4,'zl'=2,'y'=4,'c'=2,'x'=4] {'zl','y','c','x'}, dimensions={0} | all-to-all | bytes 4194304 | tf_op jit(solution)/shard_map/all_to_all | solution.py:183
  204.5 5.6 %shard_map.84 = (bf16[4,128,128]{2,1,0:T(8,128)(2,1)}, f32[4,128,128]{2,1,0:T(8,128)}, bf16[64,128,128]{2,1,0:T(8,128)(2,1)}) custom-call(s32[64]{0:T(128)} %gather_fusion.2, s32[64]{0:T(128)} %copy-done.1, bf16[64,128,128]{2,1,0:T(8,128)(2,1)} %all_to_all.41.arrived_ref, ...), custom_call_target="tpu_custom_call", output_to_operand_aliasing={{1}: (4, {})} | custom-call | tf_op jit(solution)/shard_map/pallas_call | solution.py:90
  210.1 34.4 %all_to_all.42.arrived_ref = bf16[64,128,128]{2,1,0:T(8,128)(2,1)} all-to-all(bf16[64,128,128]{2,1,0:T(8,128)(2,1)} %get-tuple-element.23), channel_id=1, replica_groups=mesh['zh'=4,'zl'=2,'y'=4,'c'=2,'x'=4] {'zl','y','c','x'}, dimensions={0} | all-to-all | bytes 4194304 | tf_op jit(solution)/shard_map/all_to_all | solution.py:183
  244.5 5.6 %shard_map.85 = (bf16[4,128,128]{2,1,0:T(8,128)(2,1)}, f32[4,128,128]{2,1,0:T(8,128)}, bf16[64,128,128]{2,1,0:T(8,128)(2,1)}) custom-call(s32[64]{0:T(128)} %gather_fusion.2, s32[64]{0:T(128)} %copy-done.1, bf16[64,128,128]{2,1,0:T(8,128)(2,1)} %all_to_all.42.arrived_ref, ...), custom_call_target="tpu_custom_call", output_to_operand_aliasing={{1}: (4, {})} | custom-call | tf_op jit(solution)/shard_map/pallas_call | solution.py:90
  250.1 34.4 %all_to_all.43.arrived_ref = bf16[64,128,128]{2,1,0:T(8,128)(2,1)} all-to-all(bf16[64,128,128]{2,1,0:T(8,128)(2,1)} %get-tuple-element.25), channel_id=1, replica_groups=mesh['zh'=4,'zl'=2,'y'=4,'c'=2,'x'=4] {'zl','y','c','x'}, dimensions={0} | all-to-all | bytes 4194304 | tf_op jit(solution)/shard_map/all_to_all | solution.py:183
  284.5 5.6 %shard_map.86 = (bf16[4,128,128]{2,1,0:T(8,128)(2,1)}, f32[4,128,128]{2,1,0:T(8,128)}, bf16[64,128,128]{2,1,0:T(8,128)(2,1)}) custom-call(s32[64]{0:T(128)} %gather_fusion.2, s32[64]{0:T(128)} %copy-done.1, bf16[64,128,128]{2,1,0:T(8,128)(2,1)} %all_to_all.43.arrived_ref, ...), custom_call_target="tpu_custom_call", output_to_operand_aliasing={{1}: (4, {})} | custom-call | tf_op jit(solution)/shard_map/pallas_call | solution.py:90
  290.2 34.4 %all_to_all.44.arrived_ref = bf16[64,128,128]{2,1,0:T(8,128)(2,1)} all-to-all(bf16[64,128,128]{2,1,0:T(8,128)(2,1)} %get-tuple-element.27), channel_id=1, replica_groups=mesh['zh'=4,'zl'=2,'y'=4,'c'=2,'x'=4] {'zl','y','c','x'}, dimensions={0} | all-to-all | bytes 4194304 | tf_op jit(solution)/shard_map/all_to_all | solution.py:183
  324.6 4.3 %shard_map.87 = (bf16[4,128,128]{2,1,0:T(8,128)(2,1)}, f32[4,128,128]{2,1,0:T(8,128)}, f32[4,128]{1,0:T(4,128)}) custom-call(s32[64]{0:T(128)} %gather_fusion.2, s32[64]{0:T(128)} %copy-done.1, bf16[64,128,128]{2,1,0:T(8,128)(2,1)} %all_to_all.44.arrived_ref, bf16[4,128,2048]{2,1,0:T(8,128)(2,1)} %copy_bitcast_fusion.coefs_ref, ...), custom_call_target="tpu_custom_call", output_to_operand_aliasing={{1}: (4, {})} | custom-call | tf_op jit(solution)/shard_map/pallas_call | solution.py:90
  328.9 2.3 collective-permute-start.6
  331.2 2.3 collective-permute-start.7
  333.5 7.9 %collective-permute-done.7 = f32[4,128]{1,0:T(4,128)S(1)} collective-permute-done((f32[4,128]{1,0:T(4,128)}, f32[4,128]{1,0:T(4,128)S(1)}, u32[]{:S(2)}, u32[]{:S(2)}) %collective-permute-start.7) | collective-permute-done | bytes 2080 | tf_op jit(solution)/shard_map/ppermute | solution.py:191
  341.5 9.2 %psum.7 = f32[4,128]{1,0:T(4,128)S(1)} all-reduce(f32[4,128]{1,0:T(4,128)S(1)} %collective-permute-done.7), channel_id=1, replica_groups=mesh['zh'=4,'zl'=2,'y'=4,'c'=2,'x'=4] {'x'}, use_global_device_ids=true, to_apply=%region_6.7 | all-reduce | flops 512 | bytes 4096 | tf_op jit(solution)/shard_map/psum | solution.py:192
  350.6 0.8 multiply_divide_fusion
  (28 shorter events, 0.3 us)
Async XLA Ops:
  0.0 13.8 %collective-permute-start = (s32[128]{0:T(128)}, s32[128]{0:T(128)S(1)}, u32[]{:S(2)}, u32[]{:S(2)}) collective-permute-start(s32[128]{0:T(128)} %param.12), channel_id=1, source_target_pairs={{0,1},{1,2},{2,3},{3,0},{4,5},{5,6},{6,7},{7,4},{8,9},{9,10},{10,1... | collective-permute-start | bytes 1544 | tf_op jit(solution)/shard_map/ppermute | solution.py:140
  1.5 12.4 %collective-permute-start.2 = (s32[128]{0:T(128)}, s32[128]{0:T(128)S(1)}, u32[]{:S(2)}, u32[]{:S(2)}) collective-permute-start(s32[128]{0:T(128)} %param.12), channel_id=1, source_target_pairs={{0,3},{1,0},{2,1},{3,2},{4,7},{5,4},{6,5},{7,6},{8,11},{9,8},{10,9... | collective-permute-start | bytes 1544 | tf_op jit(solution)/shard_map/ppermute | solution.py:140
  3.2 10.6 %collective-permute-start.1 = (s32[128]{0:T(128)}, s32[128]{0:T(128)S(1)}, u32[]{:S(2)}, u32[]{:S(2)}) collective-permute-start(s32[128]{0:T(128)} %param.12), channel_id=1, source_target_pairs={{0,2},{1,3},{2,0},{3,1},{4,6},{5,7},{6,4},{7,5},{8,10},{9,11},{10,... | collective-permute-start | bytes 1544 | tf_op jit(solution)/shard_map/ppermute | solution.py:140
  5.1 9.5 %collective-permute-start.4 = (f32[512]{0:T(512)}, f32[512]{0:T(512)S(1)}, u32[]{:S(2)}, u32[]{:S(2)}) collective-permute-start(f32[512]{0:T(512)} %param.11), channel_id=1, source_target_pairs={{0,0},{225,1},{194,2},{163,3},{164,4},{197,5},{230,6},{7,7},{8,8},... | collective-permute-start | bytes 6152 | tf_op jit(solution)/shard_map/ppermute | solution.py:124
  6.4 8.6 %collective-permute-start.3 = (f32[512,128]{1,0:T(8,128)}, f32[512,128]{1,0:T(8,128)S(1)}, u32[]{:S(2)}, u32[]{:S(2)}) collective-permute-start(f32[512,128]{1,0:T(8,128)} %param.10), channel_id=1, source_target_pairs={{0,0},{225,1},{194,2},{163,3},{164,4},{197,5},{230,6},{7,7},{8,8},... | collective-permute-start | bytes 786440 | tf_op jit(solution)/shard_map/ppermute | solution.py:124
  13.8 42.5 %copy-start.1 = (s32[64]{0:T(128)}, s32[64]{0:T(128)S(1)}, u32[]{:S(2)}) copy-start(s32[64]{0:T(128)S(1)} %get-tuple-element.18.send_ref) | copy-start | bytes 772
  16.0 24.2 %all-to-all-start = ((f32[64,3,128]{2,1,0:T(4,128)}), f32[64,3,128]{2,1,0:T(4,128)S(1)}, u32[]{:S(2)}, u32[]{:S(2)}) async-start(f32[64,3,128]{2,1,0:T(4,128)} %pad_maximum_fusion), calls=%async_computation | async-start | bytes 262144 | tf_op jit(solution)/shard_map/all_to_all | solution.py:113
  41.0 13.2 %all-to-all-start.1 = ((f32[64,3,128]{2,1,0:T(4,128)}), f32[64,3,128]{2,1,0:T(4,128)S(1)}, u32[]{:S(2)}, u32[]{:S(2)}) async-start(f32[64,3,128]{2,1,0:T(4,128)} %broadcast_in_dim.12), calls=%async_computation.1 | async-start | bytes 262144 | tf_op jit(solution)/shard_map/all_to_all | solution.py:116
  57.9 51.0 %all-to-all-start.2 = ((bf16[64,128,128]{2,1,0:T(8,128)(2,1)}), bf16[64,128,128]{2,1,0:T(8,128)(2,1)S(1)}, u32[]{:S(2)}, u32[]{:S(2)}) async-start(bf16[64,128,128]{2,1,0:T(8,128)(2,1)} %broadcast_select_fusion), calls=%async_computation.2 | async-start | bytes 4194304 | tf_op jit(solution)/shard_map/all_to_all | solution.py:183
  63.9 21.9 %collective-permute-start.5 = (bf16[4,16,128,128]{3,2,1,0:T(8,128)(2,1)}, bf16[4,16,128,128]{3,2,1,0:T(8,128)(2,1)}, u32[]{:S(2)}, u32[]{:S(2)}) collective-permute-start(bf16[4,16,128,128]{3,2,1,0:T(8,128)(2,1)} %param.8), channel_id=1, source_target_pairs={{0,0},{225,1},{194,2},{163,3},{164,4},{197,5},{230,6},{7,7},{8,8},... | collective-permute-start | bytes 6291464 | tf_op jit(solution)/shard_map/ppermute | solution.py:125
  108.9 1.3 copy-start
  328.9 21.7 %collective-permute-start.6 = (f32[4,128,128]{2,1,0:T(8,128)}, f32[4,128,128]{2,1,0:T(8,128)S(1)}, u32[]{:S(2)}, u32[]{:S(2)}) collective-permute-start(f32[4,128,128]{2,1,0:T(8,128)} %get-tuple-element.29), channel_id=1, source_target_pairs={{0,0},{1,224},{2,192},{3,160},{4,164},{5,196},{6,228},{7,4},{8,8},... | collective-permute-start | bytes 786440 | tf_op jit(solution)/shard_map/ppermute | solution.py:191
  331.2 10.3 %collective-permute-start.7 = (f32[4,128]{1,0:T(4,128)}, f32[4,128]{1,0:T(4,128)S(1)}, u32[]{:S(2)}, u32[]{:S(2)}) collective-permute-start(f32[4,128]{1,0:T(4,128)} %get-tuple-element.30), channel_id=1, source_target_pairs={{0,0},{1,224},{2,192},{3,160},{4,164},{5,196},{6,228},{7,4},{8,8},... | collective-permute-start | bytes 6152 | tf_op jit(solution)/shard_map/ppermute | solution.py:191

commit v12 on v10

--- a/solution.py
+++ b/solution.py
@@ -117,9 +117,19 @@
 def make_body(zh, xs):
     zsrc_t, group_t, pos_t, perm_in, perm_out, perm_x = layout(zh, xs)
 
+    moves_in = [(a, b) for a, b in perm_in if a != b]
+    moves_out = [(a, b) for a, b in perm_out if a != b]
+    stays_in = np.array([a == b for a, b in sorted(perm_in, key=lambda p: p[1])])
+    stays_out = np.array([a == b for a, b in sorted(perm_out, key=lambda p: p[1])])
+
+    def move(value, moves, stays, me):
+        moved = lax.ppermute(value, ALL, moves)
+        return jax.tree.map(lambda own, got: jnp.where(jnp.asarray(stays)[me], own, got), value, moved)
+
     def on_device(coefs, lag_pattern, loadings, idiosyncratic, shocked):
-        loadings, idiosyncratic = lax.ppermute((loadings, idiosyncratic), ALL, perm_in)
-        coefs = lax.ppermute(coefs, ALL, perm_in)
+        me = lax.axis_index(ALL)
+        loadings, idiosyncratic = move((loadings, idiosyncratic), moves_in, stays_in, me)
+        coefs = move(coefs, moves_in, stays_in, me)
         blk_dev = coefs.shape[0]
         lags = coefs.shape[1]
         block_size = coefs.shape[2]
@@ -185,7 +195,7 @@
             present_response, squared_terms = made[:2]
             outgoing = made[-1]
         partial = jnp.sum(squared_terms, axis=2)
-        squared_terms, partial = lax.ppermute((squared_terms, partial), ALL, perm_out)
+        squared_terms, partial = move((squared_terms, partial), moves_out, stays_out, me)
         totals = lax.psum(partial, "x")
         total_shocks = shock_columns * xs
         shares = total_shocks * squared_terms / (totals[:, :, None] + 1e-06)

time: 358 us -> 357 us (level)
  starting transfers between devices: 58.6 us -> 44.1 us
  other arithmetic: 7.57 us -> 14.3 us
  blocking collectives: 196 us -> 201 us
    ppermute x5, starting transfers between devices: 24.6 us -> 12 us  [move(): moved = lax.ppermute(value, ALL, moves)]
    all_to_all x1, waiting for transfers between devices: 19.9 us -> 29.5 us  [on_device(): lax.all_to_all(outgoing, BOX, split_axis=0, concat_axis=0, tiled=True)]
    ppermute x5, waiting for transfers between devices: 6.82 us -> 0.01 us  [move(): moved = lax.ppermute(value, ALL, moves)]
    reshape x0 -> x1, other arithmetic: none -> 4.04 us  [on_device(): coefs.transpose(0, 2, 1, 3).reshape(blk_dev, block_size, lags * block_size)]
  transfers between devices with their start and end apart: 11 -> 11, of which waited for: 4 -> 3; matrix products, arithmetic and copies ran while one was open for 4% -> 5% of each run, Pallas kernels for 0% -> 0%
where the time goes in v12:
time: 357 us; the launch traced here: 353 us
  blocking collectives  201 us (56%)
  starting transfers between devices  44.1 us (12%)
  waiting for transfers between devices  43.9 us (12%)
  Pallas kernels  32.3 us (9%)
  other arithmetic  14.3 us (4%)
  local copies, waits for them, and re-layouts  13 us (4%)
    all_to_all x5, blocking collectives, on_device(): lax.all_to_all(outgoing, BOX, split_axis=0, concat_axis=0, tiled=True)  189 us
    pallas_call x6, Pallas kernels, step(): pl.pallas_call(last_kernel if last else step_kernel, out_shape=shapes[:2]...  32.3 us
    all_to_all x1, waiting for transfers between devices, on_device(): lax.all_to_all(outgoing, BOX, split_axis=0, concat_axis=0, tiled=True)  29.5 us
    all_to_all x1, starting transfers between devices, gather_rows(): arrived = lax.all_to_all(packed, BOX, 0, 0, tiled=True)  15.1 us
    psum x1, blocking collectives, on_device(): totals = lax.psum(partial, 'x')  12.4 us
    ppermute x5, starting transfers between devices, move(): moved = lax.ppermute(value, ALL, moves)  12 us
    all_to_all x1, waiting for transfers between devices, gather_rows(): full = lax.all_to_all(spread, BOX, 0, 0, tiled=True)  7.21 us
    all_to_all x1, waiting for transfers between devices, gather_rows(): arrived = lax.all_to_all(packed, BOX, 0, 0, tiled=True)  7.2 us
  transfers between devices with their start and end apart: 11, of which 3 were waited for; matrix products, arithmetic and copies ran while one was open for 5% of the time, Pallas kernels for 0%

profile of v12, /device:TPU:96, one launch (start us, length us, event | category | flops | bytes accessed | tf_op | source)
XLA Modules:
  0.0 353.1 jit_solution(15156264752788668835)
XLA Ops:
  0.0 1.5 collective-permute-start.1
  1.5 1.7 collective-permute-start.3
  3.2 1.8 collective-permute-start.2
  5.1 0.6 collective-permute-start.4
  5.7 0.7 collective-permute-start
  6.4 1.3 dynamic_slice.25
  8.4 0.8 copy.44
  9.2 0.8 constant_dynamic-slice_fusion.3
  10.2 0.7 fusion.15
  11.0 0.6 gather_fusion.3
  11.6 0.2 compare_reduce_fusion
  11.8 0.5 iota_reduce_fusion
  12.3 1.2 dynamic_slice.29
  13.6 0.7 pad_add_fusion
  14.3 1.3 broadcast_select_fusion.5
  15.5 0.2 convolution_bitcast_fusion
  15.7 0.2 reshape.231
  16.0 1.8 fusion.3
  17.8 0.7 pad_maximum_fusion
  18.5 15.1 %all-to-all-start = ((f32[64,3,128]{2,1,0:T(4,128)}), f32[64,3,128]{2,1,0:T(4,128)S(1)}, u32[]{:S(2)}, u32[]{:S(2)}) async-start(f32[64,3,128]{2,1,0:T(4,128)} %pad_maximum_fusion), calls=%async_computation | async-start | bytes 262144 | tf_op jit(solution)/shard_map/all_to_all | solution.py:110
  33.7 7.2 %all-to-all-done = f32[64,3,128]{2,1,0:T(4,128)S(1)} async-done(((f32[64,3,128]{2,1,0:T(4,128)}), f32[64,3,128]{2,1,0:T(4,128)S(1)}, u32[]{:S(2)}, u32[]{:S(2)}) %all-to-all-start) | async-done | bytes 98336 | tf_op jit(solution)/shard_map/all_to_all | solution.py:110
  40.9 0.7 broadcast_in_dim.12
  41.6 5.9 %all-to-all-start.1 = ((f32[64,3,128]{2,1,0:T(4,128)}), f32[64,3,128]{2,1,0:T(4,128)S(1)}, u32[]{:S(2)}, u32[]{:S(2)}) async-start(f32[64,3,128]{2,1,0:T(4,128)} %broadcast_in_dim.12), calls=%async_computation.1 | async-start | bytes 262144 | tf_op jit(solution)/shard_map/all_to_all | solution.py:113
  47.6 7.2 %all-to-all-done.1 = f32[64,3,128]{2,1,0:T(4,128)S(1)} async-done(((f32[64,3,128]{2,1,0:T(4,128)}), f32[64,3,128]{2,1,0:T(4,128)S(1)}, u32[]{:S(2)}, u32[]{:S(2)}) %all-to-all-start.1) | async-done | bytes 98336 | tf_op jit(solution)/shard_map/all_to_all | solution.py:113
  54.8 0.1 slice_reduce_fusion
  54.9 0.1 reshape_squeeze.3
  55.1 0.1 fusion.9
  55.2 0.1 copy.48
  55.3 0.1 reduce_sum.31
  55.4 1.0 fusion.1
  56.4 1.0 gather_fusion.4
  57.4 1.6 broadcast_select_fusion
  58.9 6.0 %all-to-all-start.2 = ((bf16[64,128,128]{2,1,0:T(8,128)(2,1)}), bf16[64,128,128]{2,1,0:T(8,128)(2,1)S(1)}, u32[]{:S(2)}, u32[]{:S(2)}) async-start(bf16[64,128,128]{2,1,0:T(8,128)(2,1)} %broadcast_select_fusion), calls=%async_computation.2 | async-start | bytes 4194304 | tf_op jit(solution)/shard_map/all_to_all | solution.py:190
  64.9 2.0 collective-permute-start.5
  67.0 0.1 fusion.10
  67.1 0.1 reshape.236
  67.2 0.6 gather_fusion
  67.8 0.2 reduce_window_sum.11
  68.0 0.1 add.192
  68.1 0.7 fusion.13
  68.8 0.8 gather_fusion.1
  69.6 1.3 gather_fusion.2
  70.9 0.7 convert_multiply_fusion.sq_ref
  71.7 4.0 %copy_bitcast_fusion.coefs_ref = bf16[4,128,2048]{2,1,0:T(8,128)(2,1)} fusion(bf16[4,16,128,128]{3,2,1,0:T(8,128)(2,1)} %param.10, bf16[4,16,128,128]{3,2,1,0:T(8,128)(2,1)} %collective-permute-done.5, pred[]{:T(512)} %bitcast.8), kind=kLoop, calls=%fused_computation.5 | loop fusion | flops 1048576 | bytes 6291457 | tf_op jit(solution)/shard_map/reshape | solution.py:188
  75.7 29.5 %all-to-all-done.2.arrived_ref = bf16[64,128,128]{2,1,0:T(8,128)(2,1)S(1)} async-done(((bf16[64,128,128]{2,1,0:T(8,128)(2,1)}), bf16[64,128,128]{2,1,0:T(8,128)(2,1)S(1)}, u32[]{:S(2)}, u32[]{:S(2)}) %all-to-all-start.2) | async-done | bytes 2097184 | tf_op jit(solution)/shard_map/all_to_all | solution.py:190
  105.2 1.3 copy-done
  106.5 5.6 %shard_map.100 = (bf16[4,128,128]{2,1,0:T(8,128)(2,1)}, f32[4,128,128]{2,1,0:T(8,128)}, bf16[64,128,128]{2,1,0:T(8,128)(2,1)}) custom-call(s32[64]{0:T(128)} %gather_fusion.2, s32[64]{0:T(128)} %copy-done.2, bf16[64,128,128]{2,1,0:T(8,128)(2,1)} %copy-done, bf16[4,128,2048]{2,1,0:T(8,128)(2,1)} %copy_bitcast_fusion.coefs_ref, ...), custom_call_target="tpu_custom_call", output_to_operand_aliasing={{1}: (4, {})} | custom-call | tf_op jit(solution)/shard_map/pallas_call | solution.py:87
  112.1 51.3 %all_to_all.40.arrived_ref = bf16[64,128,128]{2,1,0:T(8,128)(2,1)} all-to-all(bf16[64,128,128]{2,1,0:T(8,128)(2,1)} %get-tuple-element.18), channel_id=1, replica_groups=mesh['zh'=4,'zl'=2,'y'=4,'c'=2,'x'=4] {'zl','y','c','x'}, dimensions={0} | all-to-all | bytes 4194304 | tf_op jit(solution)/shard_map/all_to_all | solution.py:190
  163.4 5.6 %shard_map.101 = (bf16[4,128,128]{2,1,0:T(8,128)(2,1)}, f32[4,128,128]{2,1,0:T(8,128)}, bf16[64,128,128]{2,1,0:T(8,128)(2,1)}) custom-call(s32[64]{0:T(128)} %gather_fusion.2, s32[64]{0:T(128)} %copy-done.2, bf16[64,128,128]{2,1,0:T(8,128)(2,1)} %all_to_all.40.arrived_ref, ...), custom_call_target="tpu_custom_call", output_to_operand_aliasing={{1}: (4, {})} | custom-call | tf_op jit(solution)/shard_map/pallas_call | solution.py:87
  169.0 34.4 %all_to_all.41.arrived_ref = bf16[64,128,128]{2,1,0:T(8,128)(2,1)} all-to-all(bf16[64,128,128]{2,1,0:T(8,128)(2,1)} %get-tuple-element.20), channel_id=1, replica_groups=mesh['zh'=4,'zl'=2,'y'=4,'c'=2,'x'=4] {'zl','y','c','x'}, dimensions={0} | all-to-all | bytes 4194304 | tf_op jit(solution)/shard_map/all_to_all | solution.py:190
  203.4 5.6 %shard_map.102 = (bf16[4,128,128]{2,1,0:T(8,128)(2,1)}, f32[4,128,128]{2,1,0:T(8,128)}, bf16[64,128,128]{2,1,0:T(8,128)(2,1)}) custom-call(s32[64]{0:T(128)} %gather_fusion.2, s32[64]{0:T(128)} %copy-done.2, bf16[64,128,128]{2,1,0:T(8,128)(2,1)} %all_to_all.41.arrived_ref, ...), custom_call_target="tpu_custom_call", output_to_operand_aliasing={{1}: (4, {})} | custom-call | tf_op jit(solution)/shard_map/pallas_call | solution.py:87
  209.0 34.4 %all_to_all.42.arrived_ref = bf16[64,128,128]{2,1,0:T(8,128)(2,1)} all-to-all(bf16[64,128,128]{2,1,0:T(8,128)(2,1)} %get-tuple-element.22), channel_id=1, replica_groups=mesh['zh'=4,'zl'=2,'y'=4,'c'=2,'x'=4] {'zl','y','c','x'}, dimensions={0} | all-to-all | bytes 4194304 | tf_op jit(solution)/shard_map/all_to_all | solution.py:190
  243.4 5.6 %shard_map.103 = (bf16[4,128,128]{2,1,0:T(8,128)(2,1)}, f32[4,128,128]{2,1,0:T(8,128)}, bf16[64,128,128]{2,1,0:T(8,128)(2,1)}) custom-call(s32[64]{0:T(128)} %gather_fusion.2, s32[64]{0:T(128)} %copy-done.2, bf16[64,128,128]{2,1,0:T(8,128)(2,1)} %all_to_all.42.arrived_ref, ...), custom_call_target="tpu_custom_call", output_to_operand_aliasing={{1}: (4, {})} | custom-call | tf_op jit(solution)/shard_map/pallas_call | solution.py:87
  249.0 34.4 %all_to_all.43.arrived_ref = bf16[64,128,128]{2,1,0:T(8,128)(2,1)} all-to-all(bf16[64,128,128]{2,1,0:T(8,128)(2,1)} %get-tuple-element.24), channel_id=1, replica_groups=mesh['zh'=4,'zl'=2,'y'=4,'c'=2,'x'=4] {'zl','y','c','x'}, dimensions={0} | all-to-all | bytes 4194304 | tf_op jit(solution)/shard_map/all_to_all | solution.py:190
  283.5 5.6 %shard_map.104 = (bf16[4,128,128]{2,1,0:T(8,128)(2,1)}, f32[4,128,128]{2,1,0:T(8,128)}, bf16[64,128,128]{2,1,0:T(8,128)(2,1)}) custom-call(s32[64]{0:T(128)} %gather_fusion.2, s32[64]{0:T(128)} %copy-done.2, bf16[64,128,128]{2,1,0:T(8,128)(2,1)} %all_to_all.43.arrived_ref, ...), custom_call_target="tpu_custom_call", output_to_operand_aliasing={{1}: (4, {})} | custom-call | tf_op jit(solution)/shard_map/pallas_call | solution.py:87
  289.1 34.4 %all_to_all.44.arrived_ref = bf16[64,128,128]{2,1,0:T(8,128)(2,1)} all-to-all(bf16[64,128,128]{2,1,0:T(8,128)(2,1)} %get-tuple-element.26), channel_id=1, replica_groups=mesh['zh'=4,'zl'=2,'y'=4,'c'=2,'x'=4] {'zl','y','c','x'}, dimensions={0} | all-to-all | bytes 4194304 | tf_op jit(solution)/shard_map/all_to_all | solution.py:190
  323.5 4.3 %shard_map.105 = (bf16[4,128,128]{2,1,0:T(8,128)(2,1)}, f32[4,128,128]{2,1,0:T(8,128)}) custom-call(s32[64]{0:T(128)} %gather_fusion.2, s32[64]{0:T(128)} %copy-done.2, bf16[64,128,128]{2,1,0:T(8,128)(2,1)} %all_to_all.44.arrived_ref, bf16[4,128,2048]{2,1,0:T(8,128)(2,1)} %copy_bitcast_fusion.coefs_ref, ...), custom_call_target="tpu_custom_call", output_to_operand_aliasing={{1}: (4, {})} | custom-call | tf_op jit(solution)/shard_map/pallas_call | solution.py:87
  327.8 1.1 reduce_sum.32
  328.9 2.3 collective-permute-start.7
  331.2 0.7 dynamic_slice.24
  331.9 6.4 %collective-permute-start.6 = (f32[4,128,128]{2,1,0:T(8,128)}, f32[4,128,128]{2,1,0:T(8,128)S(1)}, u32[]{:S(2)}, u32[]{:S(2)}) collective-permute-start(f32[4,128,128]{2,1,0:T(8,128)} %get-tuple-element.28), channel_id=1, source_target_pairs={{1,224},{2,192},{3,160},{4,164},{5,196},{6,228},{7,4},{9,232},{10,... | collective-permute-start | bytes 786440 | tf_op jit(solution)/shard_map/ppermute | solution.py:126
  338.4 0.7 broadcast_select_fusion.4
  339.1 12.4 %psum.7 = f32[4,128]{1,0:T(4,128)S(1)} all-reduce(f32[4,128]{1,0:T(4,128)S(1)} %broadcast_select_fusion.4), channel_id=1, replica_groups=mesh['zh'=4,'zl'=2,'y'=4,'c'=2,'x'=4] {'x'}, use_global_device_ids=true, to_apply=%region_7.8 | all-reduce | flops 512 | bytes 4096 | tf_op jit(solution)/shard_map/psum | solution.py:199
  351.5 1.5 multiply_divide_fusion
  (36 shorter events, 0.6 us)
Async XLA Ops:
  0.0 55.4 %copy-start.1 = (f32[512,128]{1,0:T(8,128)S(1)}, f32[512,128]{1,0:T(8,128)}, u32[]{:S(2)}) copy-start(f32[512,128]{1,0:T(8,128)} %param.12) | copy-start | bytes 786436
  0.0 13.6 %collective-permute-start.1 = (s32[128]{0:T(128)}, s32[128]{0:T(128)S(1)}, u32[]{:S(2)}, u32[]{:S(2)}) collective-permute-start(s32[128]{0:T(128)} %param.14), channel_id=1, source_target_pairs={{0,1},{1,2},{2,3},{3,0},{4,5},{5,6},{6,7},{7,4},{8,9},{9,10},{10,1... | collective-permute-start | bytes 1544 | tf_op jit(solution)/shard_map/ppermute | solution.py:147
  1.5 12.1 %collective-permute-start.3 = (s32[128]{0:T(128)}, s32[128]{0:T(128)S(1)}, u32[]{:S(2)}, u32[]{:S(2)}) collective-permute-start(s32[128]{0:T(128)} %param.14), channel_id=1, source_target_pairs={{0,3},{1,0},{2,1},{3,2},{4,7},{5,4},{6,5},{7,6},{8,11},{9,8},{10,9... | collective-permute-start | bytes 1544 | tf_op jit(solution)/shard_map/ppermute | solution.py:147
  3.2 10.3 %collective-permute-start.2 = (s32[128]{0:T(128)}, s32[128]{0:T(128)S(1)}, u32[]{:S(2)}, u32[]{:S(2)}) collective-permute-start(s32[128]{0:T(128)} %param.14), channel_id=1, source_target_pairs={{0,2},{1,3},{2,0},{3,1},{4,6},{5,7},{6,4},{7,5},{8,10},{9,11},{10,... | collective-permute-start | bytes 1544 | tf_op jit(solution)/shard_map/ppermute | solution.py:147
  5.1 9.2 %collective-permute-start.4 = (f32[512]{0:T(512)}, f32[512]{0:T(512)S(1)}, u32[]{:S(2)}, u32[]{:S(2)}) collective-permute-start(f32[512]{0:T(512)} %param.13), channel_id=1, source_target_pairs={{225,1},{194,2},{163,3},{164,4},{197,5},{230,6},{233,9},{202,10},{... | collective-permute-start | bytes 6152 | tf_op jit(solution)/shard_map/ppermute | solution.py:126
  5.7 10.3 %collective-permute-start = (f32[512,128]{1,0:T(8,128)}, f32[512,128]{1,0:T(8,128)S(1)}, u32[]{:S(2)}, u32[]{:S(2)}) collective-permute-start(f32[512,128]{1,0:T(8,128)} %param.12), channel_id=1, source_target_pairs={{225,1},{194,2},{163,3},{164,4},{197,5},{230,6},{233,9},{202,10},{... | collective-permute-start | bytes 786440 | tf_op jit(solution)/shard_map/ppermute | solution.py:126
  12.3 45.1 %copy-start.2 = (s32[64]{0:T(128)}, s32[64]{0:T(128)S(1)}, u32[]{:S(2)}) copy-start(s32[64]{0:T(128)S(1)} %get-tuple-element.17.send_ref) | copy-start | bytes 772
  18.5 22.3 %all-to-all-start = ((f32[64,3,128]{2,1,0:T(4,128)}), f32[64,3,128]{2,1,0:T(4,128)S(1)}, u32[]{:S(2)}, u32[]{:S(2)}) async-start(f32[64,3,128]{2,1,0:T(4,128)} %pad_maximum_fusion), calls=%async_computation | async-start | bytes 262144 | tf_op jit(solution)/shard_map/all_to_all | solution.py:110
  41.6 13.2 %all-to-all-start.1 = ((f32[64,3,128]{2,1,0:T(4,128)}), f32[64,3,128]{2,1,0:T(4,128)S(1)}, u32[]{:S(2)}, u32[]{:S(2)}) async-start(f32[64,3,128]{2,1,0:T(4,128)} %broadcast_in_dim.12), calls=%async_computation.1 | async-start | bytes 262144 | tf_op jit(solution)/shard_map/all_to_all | solution.py:113
  58.9 46.3 %all-to-all-start.2 = ((bf16[64,128,128]{2,1,0:T(8,128)(2,1)}), bf16[64,128,128]{2,1,0:T(8,128)(2,1)S(1)}, u32[]{:S(2)}, u32[]{:S(2)}) async-start(bf16[64,128,128]{2,1,0:T(8,128)(2,1)} %broadcast_select_fusion), calls=%async_computation.2 | async-start | bytes 4194304 | tf_op jit(solution)/shard_map/all_to_all | solution.py:190
  64.9 6.7 %collective-permute-start.5 = (bf16[4,16,128,128]{3,2,1,0:T(8,128)(2,1)}, bf16[4,16,128,128]{3,2,1,0:T(8,128)(2,1)}, u32[]{:S(2)}, u32[]{:S(2)}) collective-permute-start(bf16[4,16,128,128]{3,2,1,0:T(8,128)(2,1)} %param.10), channel_id=1, source_target_pairs={{225,1},{194,2},{163,3},{164,4},{197,5},{230,6},{233,9},{202,10},{... | collective-permute-start | bytes 6291464 | tf_op jit(solution)/shard_map/ppermute | solution.py:126
  105.2 1.3 copy-start
  323.5 7.7 %copy-start.3 = (pred[256]{0:T(512)(128)(4,1)S(1)}, pred[256]{0:T(512)(128)(4,1)}, u32[]{:S(2)}) copy-start(pred[256]{0:T(512)(128)(4,1)} %constant.117.clone) | copy-start | bytes 772
  328.9 9.4 %collective-permute-start.7 = (f32[4,128]{1,0:T(4,128)S(1)}, f32[4,128]{1,0:T(4,128)S(1)}, u32[]{:S(2)}, u32[]{:S(2)}) collective-permute-start(f32[4,128]{1,0:T(4,128)S(1)} %reduce_sum.32), channel_id=1, source_target_pairs={{1,224},{2,192},{3,160},{4,164},{5,196},{6,228},{7,4},{9,232},{10,... | collective-permute-start | bytes 6152 | tf_op jit(solution)/shard_map/ppermute | solution.py:126
  331.9 19.6 %collective-permute-start.6 = (f32[4,128,128]{2,1,0:T(8,128)}, f32[4,128,128]{2,1,0:T(8,128)S(1)}, u32[]{:S(2)}, u32[]{:S(2)}) collective-permute-start(f32[4,128,128]{2,1,0:T(8,128)} %get-tuple-element.28), channel_id=1, source_target_pairs={{1,224},{2,192},{3,160},{4,164},{5,196},{6,228},{7,4},{9,232},{10,... | collective-permute-start | bytes 786440 | tf_op jit(solution)/shard_map/ppermute | solution.py:126

commit v13 on v10

--- a/solution.py
+++ b/solution.py
@@ -119,7 +119,6 @@
 
     def on_device(coefs, lag_pattern, loadings, idiosyncratic, shocked):
         loadings, idiosyncratic = lax.ppermute((loadings, idiosyncratic), ALL, perm_in)
-        coefs = lax.ppermute(coefs, ALL, perm_in)
         blk_dev = coefs.shape[0]
         lags = coefs.shape[1]
         block_size = coefs.shape[2]
@@ -178,6 +177,9 @@
         coefs_wide = coefs.transpose(0, 2, 1, 3).reshape(blk_dev, block_size, lags * block_size)
         for step_no in range(HORIZONS - 1):
             arriving_response = lax.all_to_all(outgoing, BOX, split_axis=0, concat_axis=0, tiled=True)
+            if step_no == 0:
+                arriving_response, coefs_wide = lax.optimization_barrier((arriving_response, coefs_wide))
+                coefs_wide = lax.ppermute(coefs_wide, ALL, perm_in)
             made = step(
                 take_index, send_idx, arriving_response, coefs_wide, squared_terms,
                 last=step_no == HORIZONS - 2,

time: 358 us -> 383 us (1.070)
  blocking collectives: 196 us -> 213 us
  waiting for transfers between devices: 41.1 us -> 47 us
    all_to_all x5, blocking collectives: 186 us -> 203 us  [on_device(): lax.all_to_all(outgoing, BOX, split_axis=0, concat_axis=0, tiled=True)]
    all_to_all x1, waiting for transfers between devices: 19.9 us -> 26.3 us  [on_device(): lax.all_to_all(outgoing, BOX, split_axis=0, concat_axis=0, tiled=True)]
where the time goes in v13:
time: 383 us; the launch traced here: 377 us
  blocking collectives  213 us (56%)
  starting transfers between devices  60.6 us (16%)
  waiting for transfers between devices  47 us (12%)
  Pallas kernels  32.4 us (8%)
  local copies, waits for them, and re-layouts  12.7 us (3%)
  other arithmetic  9.22 us (2%)
    all_to_all x5, blocking collectives, on_device(): lax.all_to_all(outgoing, BOX, split_axis=0, concat_axis=0, tiled=True)  203 us
    pallas_call x6, Pallas kernels, step(): pl.pallas_call(last_kernel if last else step_kernel, out_shape=shapes[:2]...  32.4 us
    all_to_all x1, waiting for transfers between devices, on_device(): lax.all_to_all(outgoing, BOX, split_axis=0, concat_axis=0, tiled=True)  26.3 us
    ppermute x1, starting transfers between devices, on_device(): coefs_wide = lax.ppermute(coefs_wide, ALL, perm_in)  17.1 us
    all_to_all x1, starting transfers between devices, gather_rows(): arrived = lax.all_to_all(packed, BOX, 0, 0, tiled=True)  17 us
    psum x1, blocking collectives, on_device(): totals = lax.psum(partial, 'x')  10.1 us
  transfers between devices with their start and end apart: 11, of which 4 were waited for; matrix products, arithmetic and copies ran while one was open for 4% of the time, Pallas kernels for 0%

profile of v13, /device:TPU:96, one launch (start us, length us, event | category | flops | bytes accessed | tf_op | source)
XLA Modules:
  0.0 376.7 jit_solution(7518634786640767015)
XLA Ops:
  0.0 1.5 collective-permute-start
  1.5 1.7 collective-permute-start.2
  3.2 1.8 collective-permute-start.1
  5.1 1.3 collective-permute-start.4
  6.4 1.6 collective-permute-start.3
  8.0 1.3 dynamic_slice.15
  9.9 0.8 copy.46
  10.7 0.8 constant_dynamic-slice_fusion.3
  11.5 0.1 copy.44
  11.6 0.1 reshape.228
  11.7 0.7 fusion.16
  12.4 0.1 reshape.229
  12.5 0.6 gather_fusion.3
  13.1 0.2 compare_reduce_fusion
  13.3 0.5 iota_reduce_fusion
  13.9 0.7 pad_add_fusion
  14.6 0.2 convolution_bitcast_fusion.1
  14.8 0.2 reshape.231
  15.0 0.3 fusion.4
  15.3 0.7 pad_maximum_fusion
  16.0 17.0 %all-to-all-start = ((f32[64,3,128]{2,1,0:T(4,128)}), f32[64,3,128]{2,1,0:T(4,128)S(1)}, u32[]{:S(2)}, u32[]{:S(2)}) async-start(f32[64,3,128]{2,1,0:T(4,128)} %pad_maximum_fusion), calls=%async_computation | async-start | bytes 262144 | tf_op jit(solution)/shard_map/all_to_all | solution.py:110
  33.1 7.2 %all-to-all-done = f32[64,3,128]{2,1,0:T(4,128)S(1)} async-done(((f32[64,3,128]{2,1,0:T(4,128)}), f32[64,3,128]{2,1,0:T(4,128)S(1)}, u32[]{:S(2)}, u32[]{:S(2)}) %all-to-all-start) | async-done | bytes 98336 | tf_op jit(solution)/shard_map/all_to_all | solution.py:110
  40.3 0.7 broadcast_in_dim.12
  41.0 5.9 %all-to-all-start.1 = ((f32[64,3,128]{2,1,0:T(4,128)}), f32[64,3,128]{2,1,0:T(4,128)S(1)}, u32[]{:S(2)}, u32[]{:S(2)}) async-start(f32[64,3,128]{2,1,0:T(4,128)} %broadcast_in_dim.12), calls=%async_computation.1 | async-start | bytes 262144 | tf_op jit(solution)/shard_map/all_to_all | solution.py:113
  47.0 7.2 %all-to-all-done.1 = f32[64,3,128]{2,1,0:T(4,128)S(1)} async-done(((f32[64,3,128]{2,1,0:T(4,128)}), f32[64,3,128]{2,1,0:T(4,128)S(1)}, u32[]{:S(2)}, u32[]{:S(2)}) %all-to-all-start.1) | async-done | bytes 98336 | tf_op jit(solution)/shard_map/all_to_all | solution.py:113
  54.2 0.1 slice_reduce_fusion
  54.3 0.1 reshape_squeeze.3
  54.5 0.1 fusion.10
  54.6 0.1 copy.50
  54.7 0.1 reduce_sum.31
  54.8 0.4 fusion.2
  55.2 0.1 copy.51
  55.3 2.2 gather_fusion.4
  57.5 3.2 broadcast_select_fusion
  60.7 6.8 %all-to-all-start.2 = ((bf16[64,128,128]{2,1,0:T(8,128)(2,1)}), bf16[64,128,128]{2,1,0:T(8,128)(2,1)}, u32[]{:S(2)}, u32[]{:S(2)}) async-start(bf16[64,128,128]{2,1,0:T(8,128)(2,1)} %broadcast_select_fusion), calls=%async_computation.2 | async-start | bytes 4194304 | tf_op jit(solution)/shard_map/all_to_all | solution.py:179
  67.5 1.6 copy_bitcast_fusion
  69.2 26.3 %all-to-all-done.2.arrived_ref = bf16[64,128,128]{2,1,0:T(8,128)(2,1)} async-done(((bf16[64,128,128]{2,1,0:T(8,128)(2,1)}), bf16[64,128,128]{2,1,0:T(8,128)(2,1)}, u32[]{:S(2)}, u32[]{:S(2)}) %all-to-all-start.2) | async-done | bytes 2097184 | tf_op jit(solution)/shard_map/all_to_all | solution.py:179
  95.4 17.1 %collective-permute-start.5 = (bf16[4,128,2048]{2,1,0:T(8,128)(2,1)}, bf16[4,128,2048]{2,1,0:T(8,128)(2,1)}, u32[]{:S(2)}, u32[]{:S(2)}) collective-permute-start(bf16[4,128,2048]{2,1,0:T(8,128)(2,1)} %copy_bitcast_fusion), channel_id=1, source_target_pairs={{0,0},{225,1},{194,2},{163,3},{164,4},{197,5},{230,6},{7,7},{8,8},... | collective-permute-start | bytes 6291464 | tf_op jit(solution)/shard_map/ppermute | solution.py:182
  112.6 0.1 fusion.11
  112.7 0.1 reshape.236
  112.8 0.6 gather_fusion
  113.4 0.2 reduce_window_sum.11
  113.6 0.1 add.168
  113.7 0.7 fusion.14
  114.4 0.8 gather_fusion.1
  115.2 1.3 gather_fusion.2
  116.5 0.7 convert_multiply_fusion.sq_ref
  117.3 5.6 %shard_map.82 = (bf16[4,128,128]{2,1,0:T(8,128)(2,1)}, f32[4,128,128]{2,1,0:T(8,128)}, bf16[64,128,128]{2,1,0:T(8,128)(2,1)}) custom-call(s32[64]{0:T(128)} %gather_fusion.2, s32[64]{0:T(128)} %copy-done.1, bf16[64,128,128]{2,1,0:T(8,128)(2,1)} %all-to-all-done.2.arrived_ref, ...), custom_call_target="tpu_custom_call", output_to_operand_aliasing={{1}: (4, {})} | custom-call | tf_op jit(solution)/shard_map/pallas_call | solution.py:87
  122.9 64.8 %all_to_all.40.arrived_ref = bf16[64,128,128]{2,1,0:T(8,128)(2,1)} all-to-all(bf16[64,128,128]{2,1,0:T(8,128)(2,1)} %get-tuple-element.22), channel_id=1, replica_groups=mesh['zh'=4,'zl'=2,'y'=4,'c'=2,'x'=4] {'zl','y','c','x'}, dimensions={0} | all-to-all | bytes 4194304 | tf_op jit(solution)/shard_map/all_to_all | solution.py:179
  187.7 5.6 %shard_map.83 = (bf16[4,128,128]{2,1,0:T(8,128)(2,1)}, f32[4,128,128]{2,1,0:T(8,128)}, bf16[64,128,128]{2,1,0:T(8,128)(2,1)}) custom-call(s32[64]{0:T(128)} %gather_fusion.2, s32[64]{0:T(128)} %copy-done.1, bf16[64,128,128]{2,1,0:T(8,128)(2,1)} %all_to_all.40.arrived_ref, ...), custom_call_target="tpu_custom_call", output_to_operand_aliasing={{1}: (4, {})} | custom-call | tf_op jit(solution)/shard_map/pallas_call | solution.py:87
  193.4 34.6 %all_to_all.41.arrived_ref = bf16[64,128,128]{2,1,0:T(8,128)(2,1)} all-to-all(bf16[64,128,128]{2,1,0:T(8,128)(2,1)} %get-tuple-element.24), channel_id=1, replica_groups=mesh['zh'=4,'zl'=2,'y'=4,'c'=2,'x'=4] {'zl','y','c','x'}, dimensions={0} | all-to-all | bytes 4194304 | tf_op jit(solution)/shard_map/all_to_all | solution.py:179
  228.0 5.6 %shard_map.84 = (bf16[4,128,128]{2,1,0:T(8,128)(2,1)}, f32[4,128,128]{2,1,0:T(8,128)}, bf16[64,128,128]{2,1,0:T(8,128)(2,1)}) custom-call(s32[64]{0:T(128)} %gather_fusion.2, s32[64]{0:T(128)} %copy-done.1, bf16[64,128,128]{2,1,0:T(8,128)(2,1)} %all_to_all.41.arrived_ref, ...), custom_call_target="tpu_custom_call", output_to_operand_aliasing={{1}: (4, {})} | custom-call | tf_op jit(solution)/shard_map/pallas_call | solution.py:87
  233.6 34.4 %all_to_all.42.arrived_ref = bf16[64,128,128]{2,1,0:T(8,128)(2,1)} all-to-all(bf16[64,128,128]{2,1,0:T(8,128)(2,1)} %get-tuple-element.26), channel_id=1, replica_groups=mesh['zh'=4,'zl'=2,'y'=4,'c'=2,'x'=4] {'zl','y','c','x'}, dimensions={0} | all-to-all | bytes 4194304 | tf_op jit(solution)/shard_map/all_to_all | solution.py:179
  268.0 5.6 %shard_map.85 = (bf16[4,128,128]{2,1,0:T(8,128)(2,1)}, f32[4,128,128]{2,1,0:T(8,128)}, bf16[64,128,128]{2,1,0:T(8,128)(2,1)}) custom-call(s32[64]{0:T(128)} %gather_fusion.2, s32[64]{0:T(128)} %copy-done.1, bf16[64,128,128]{2,1,0:T(8,128)(2,1)} %all_to_all.42.arrived_ref, ...), custom_call_target="tpu_custom_call", output_to_operand_aliasing={{1}: (4, {})} | custom-call | tf_op jit(solution)/shard_map/pallas_call | solution.py:87
  273.7 34.4 %all_to_all.43.arrived_ref = bf16[64,128,128]{2,1,0:T(8,128)(2,1)} all-to-all(bf16[64,128,128]{2,1,0:T(8,128)(2,1)} %get-tuple-element.28), channel_id=1, replica_groups=mesh['zh'=4,'zl'=2,'y'=4,'c'=2,'x'=4] {'zl','y','c','x'}, dimensions={0} | all-to-all | bytes 4194304 | tf_op jit(solution)/shard_map/all_to_all | solution.py:179
  308.1 5.6 %shard_map.86 = (bf16[4,128,128]{2,1,0:T(8,128)(2,1)}, f32[4,128,128]{2,1,0:T(8,128)}, bf16[64,128,128]{2,1,0:T(8,128)(2,1)}) custom-call(s32[64]{0:T(128)} %gather_fusion.2, s32[64]{0:T(128)} %copy-done.1, bf16[64,128,128]{2,1,0:T(8,128)(2,1)} %all_to_all.43.arrived_ref, ...), custom_call_target="tpu_custom_call", output_to_operand_aliasing={{1}: (4, {})} | custom-call | tf_op jit(solution)/shard_map/pallas_call | solution.py:87
  313.7 34.4 %all_to_all.44.arrived_ref = bf16[64,128,128]{2,1,0:T(8,128)(2,1)} all-to-all(bf16[64,128,128]{2,1,0:T(8,128)(2,1)} %get-tuple-element.30), channel_id=1, replica_groups=mesh['zh'=4,'zl'=2,'y'=4,'c'=2,'x'=4] {'zl','y','c','x'}, dimensions={0} | all-to-all | bytes 4194304 | tf_op jit(solution)/shard_map/all_to_all | solution.py:179
  348.1 4.3 %shard_map.87 = (bf16[4,128,128]{2,1,0:T(8,128)(2,1)}, f32[4,128,128]{2,1,0:T(8,128)}) custom-call(s32[64]{0:T(128)} %gather_fusion.2, s32[64]{0:T(128)} %copy-done.1, bf16[64,128,128]{2,1,0:T(8,128)(2,1)} %all_to_all.44.arrived_ref, bf16[4,128,2048]{2,1,0:T(8,128)(2,1)} %collective-permute-done.5.coefs_ref, ...), custom_call_target="tpu_custom_call", output_to_operand_aliasing={{1}: (4, {})} | custom-call | tf_op jit(solution)/shard_map/pallas_call | solution.py:87
  352.4 2.3 collective-permute-start.6
  354.7 1.1 reduce_sum.32
  355.8 3.6 collective-permute-start.7
  359.4 6.4 %collective-permute-done.7 = f32[4,128]{1,0:T(4,128)S(1)} collective-permute-done((f32[4,128]{1,0:T(4,128)S(1)}, f32[4,128]{1,0:T(4,128)S(1)}, u32[]{:S(2)}, u32[]{:S(2)}) %collective-permute-start.7) | collective-permute-done | bytes 2080 | tf_op jit(solution)/shard_map/ppermute | solution.py:190
  365.8 10.1 %psum.7 = f32[4,128]{1,0:T(4,128)S(1)} all-reduce(f32[4,128]{1,0:T(4,128)S(1)} %collective-permute-done.7), channel_id=1, replica_groups=mesh['zh'=4,'zl'=2,'y'=4,'c'=2,'x'=4] {'x'}, use_global_device_ids=true, to_apply=%region_7.8 | all-reduce | flops 512 | bytes 4096 | tf_op jit(solution)/shard_map/psum | solution.py:191
  375.9 0.8 multiply_divide_fusion
  (29 shorter events, 0.3 us)
Async XLA Ops:
  0.0 67.5 %copy-start = (bf16[4,16,128,128]{3,2,1,0:T(8,128)(2,1)S(1)}, bf16[4,16,128,128]{3,2,1,0:T(8,128)(2,1)}, u32[]{:S(2)}) copy-start(bf16[4,16,128,128]{3,2,1,0:T(8,128)(2,1)} %param.8) | copy-start | bytes 6291460
  0.0 13.8 %collective-permute-start = (s32[128]{0:T(128)}, s32[128]{0:T(128)S(1)}, u32[]{:S(2)}, u32[]{:S(2)}) collective-permute-start(s32[128]{0:T(128)} %param.12), channel_id=1, source_target_pairs={{0,1},{1,2},{2,3},{3,0},{4,5},{5,6},{6,7},{7,4},{8,9},{9,10},{10,1... | collective-permute-start | bytes 1544 | tf_op jit(solution)/shard_map/ppermute | solution.py:136
  1.5 12.4 %collective-permute-start.2 = (s32[128]{0:T(128)}, s32[128]{0:T(128)S(1)}, u32[]{:S(2)}, u32[]{:S(2)}) collective-permute-start(s32[128]{0:T(128)} %param.12), channel_id=1, source_target_pairs={{0,3},{1,0},{2,1},{3,2},{4,7},{5,4},{6,5},{7,6},{8,11},{9,8},{10,9... | collective-permute-start | bytes 1544 | tf_op jit(solution)/shard_map/ppermute | solution.py:136
  3.2 10.6 %collective-permute-start.1 = (s32[128]{0:T(128)}, s32[128]{0:T(128)S(1)}, u32[]{:S(2)}, u32[]{:S(2)}) collective-permute-start(s32[128]{0:T(128)} %param.12), channel_id=1, source_target_pairs={{0,2},{1,3},{2,0},{3,1},{4,6},{5,7},{6,4},{7,5},{8,10},{9,11},{10,... | collective-permute-start | bytes 1544 | tf_op jit(solution)/shard_map/ppermute | solution.py:136
  5.1 9.5 %collective-permute-start.4 = (f32[512]{0:T(512)}, f32[512]{0:T(512)S(1)}, u32[]{:S(2)}, u32[]{:S(2)}) collective-permute-start(f32[512]{0:T(512)} %param.11), channel_id=1, source_target_pairs={{0,0},{225,1},{194,2},{163,3},{164,4},{197,5},{230,6},{7,7},{8,8},... | collective-permute-start | bytes 6152 | tf_op jit(solution)/shard_map/ppermute | solution.py:121
  6.4 8.6 %collective-permute-start.3 = (f32[512,128]{1,0:T(8,128)}, f32[512,128]{1,0:T(8,128)S(1)}, u32[]{:S(2)}, u32[]{:S(2)}) collective-permute-start(f32[512,128]{1,0:T(8,128)} %param.10), channel_id=1, source_target_pairs={{0,0},{225,1},{194,2},{163,3},{164,4},{197,5},{230,6},{7,7},{8,8},... | collective-permute-start | bytes 786440 | tf_op jit(solution)/shard_map/ppermute | solution.py:121
  13.8 43.7 %copy-start.1 = (s32[64]{0:T(128)}, s32[64]{0:T(128)S(1)}, u32[]{:S(2)}) copy-start(s32[64]{0:T(128)S(1)} %get-tuple-element.19.send_ref) | copy-start | bytes 772
  16.0 24.2 %all-to-all-start = ((f32[64,3,128]{2,1,0:T(4,128)}), f32[64,3,128]{2,1,0:T(4,128)S(1)}, u32[]{:S(2)}, u32[]{:S(2)}) async-start(f32[64,3,128]{2,1,0:T(4,128)} %pad_maximum_fusion), calls=%async_computation | async-start | bytes 262144 | tf_op jit(solution)/shard_map/all_to_all | solution.py:110
  41.0 13.2 %all-to-all-start.1 = ((f32[64,3,128]{2,1,0:T(4,128)}), f32[64,3,128]{2,1,0:T(4,128)S(1)}, u32[]{:S(2)}, u32[]{:S(2)}) async-start(f32[64,3,128]{2,1,0:T(4,128)} %broadcast_in_dim.12), calls=%async_computation.1 | async-start | bytes 262144 | tf_op jit(solution)/shard_map/all_to_all | solution.py:113
  60.7 34.7 %all-to-all-start.2 = ((bf16[64,128,128]{2,1,0:T(8,128)(2,1)}), bf16[64,128,128]{2,1,0:T(8,128)(2,1)}, u32[]{:S(2)}, u32[]{:S(2)}) async-start(bf16[64,128,128]{2,1,0:T(8,128)(2,1)} %broadcast_select_fusion), calls=%async_computation.2 | async-start | bytes 4194304 | tf_op jit(solution)/shard_map/all_to_all | solution.py:179
  95.4 21.8 %collective-permute-start.5 = (bf16[4,128,2048]{2,1,0:T(8,128)(2,1)}, bf16[4,128,2048]{2,1,0:T(8,128)(2,1)}, u32[]{:S(2)}, u32[]{:S(2)}) collective-permute-start(bf16[4,128,2048]{2,1,0:T(8,128)(2,1)} %copy_bitcast_fusion), channel_id=1, source_target_pairs={{0,0},{225,1},{194,2},{163,3},{164,4},{197,5},{230,6},{7,7},{8,8},... | collective-permute-start | bytes 6291464 | tf_op jit(solution)/shard_map/ppermute | solution.py:182
  352.4 23.4 %collective-permute-start.6 = (f32[4,128,128]{2,1,0:T(8,128)}, f32[4,128,128]{2,1,0:T(8,128)S(1)}, u32[]{:S(2)}, u32[]{:S(2)}) collective-permute-start(f32[4,128,128]{2,1,0:T(8,128)} %get-tuple-element.32), channel_id=1, source_target_pairs={{0,0},{1,224},{2,192},{3,160},{4,164},{5,196},{6,228},{7,4},{8,8},... | collective-permute-start | bytes 786440 | tf_op jit(solution)/shard_map/ppermute | solution.py:190
  355.8 9.9 %collective-permute-start.7 = (f32[4,128]{1,0:T(4,128)S(1)}, f32[4,128]{1,0:T(4,128)S(1)}, u32[]{:S(2)}, u32[]{:S(2)}) collective-permute-start(f32[4,128]{1,0:T(4,128)S(1)} %reduce_sum.32), channel_id=1, source_target_pairs={{0,0},{1,224},{2,192},{3,160},{4,164},{5,196},{6,228},{7,4},{8,8},... | collective-permute-start | bytes 6152 | tf_op jit(solution)/shard_map/ppermute | solution.py:190

commit v14 on v10

--- a/solution.py
+++ b/solution.py
@@ -120,6 +120,7 @@
     def on_device(coefs, lag_pattern, loadings, idiosyncratic, shocked):
         loadings, idiosyncratic = lax.ppermute((loadings, idiosyncratic), ALL, perm_in)
         coefs = lax.ppermute(coefs, ALL, perm_in)
+        loadings, coefs = lax.optimization_barrier((loadings, coefs))
         blk_dev = coefs.shape[0]
         lags = coefs.shape[1]
         block_size = coefs.shape[2]

time: 358 us -> 364 us (1.017)
  starting transfers between devices: 58.6 us -> 80.8 us
  blocking collectives: 196 us -> 187 us
  waiting for transfers between devices: 41.1 us -> 36.7 us
    all_to_all x1, starting transfers between devices: 17 us -> 46.5 us  [gather_rows(): arrived = lax.all_to_all(packed, BOX, 0, 0, tiled=True)]
    ppermute x1, starting transfers between devices: 17.1 us -> 2.24 us  [on_device(): coefs = lax.ppermute(coefs, ALL, perm_in)]
    all_to_all x5, blocking collectives: 186 us -> 172 us  [on_device(): lax.all_to_all(outgoing, BOX, split_axis=0, concat_axis=0, tiled=True)]
    psum x1, blocking collectives: 10.1 us -> 14.8 us  [on_device(): totals = lax.psum(partial, 'x')]
    ppermute x2, waiting for transfers between devices: 6.81 us -> 2.23 us  [on_device(): lax.ppermute((squared_terms, partial), ALL, perm_out)]
    ppermute x2, starting transfers between devices: 4.6 us -> 9.16 us  [on_device(): lax.ppermute((squared_terms, partial), ALL, perm_out)]
where the time goes in v14:
time: 364 us; the launch traced here: 361 us
  blocking collectives  187 us (51%)
  starting transfers between devices  80.8 us (22%)
  waiting for transfers between devices  36.7 us (10%)
  Pallas kernels  32.3 us (9%)
  local copies, waits for them, and re-layouts  14.3 us (4%)
  other arithmetic  7.9 us (2%)
    all_to_all x5, blocking collectives, on_device(): lax.all_to_all(outgoing, BOX, split_axis=0, concat_axis=0, tiled=True)  172 us
    all_to_all x1, starting transfers between devices, gather_rows(): arrived = lax.all_to_all(packed, BOX, 0, 0, tiled=True)  46.5 us
    pallas_call x6, Pallas kernels, step(): pl.pallas_call(last_kernel if last else step_kernel, out_shape=shapes[:2]...  32.3 us
    all_to_all x1, waiting for transfers between devices, on_device(): lax.all_to_all(outgoing, BOX, split_axis=0, concat_axis=0, tiled=True)  20 us
    psum x1, blocking collectives, on_device(): totals = lax.psum(partial, 'x')  14.8 us
    ppermute x2, starting transfers between devices, on_device(): lax.ppermute((squared_terms, partial), ALL, perm_out)  9.16 us
    ppermute x3, starting transfers between devices, on_device(): lax.ppermute(shocked, ALL, perm_x[j])  8 us
  transfers between devices with their start and end apart: 11, of which 4 were waited for; matrix products, arithmetic and copies ran while one was open for 4% of the time, Pallas kernels for 0%

profile of v14, /device:TPU:96, one launch (start us, length us, event | category | flops | bytes accessed | tf_op | source)
XLA Modules:
  0.0 361.0 jit_solution(2051474384428668606)
XLA Ops:
  0.0 2.2 collective-permute-start.1
  2.2 4.4 %collective-permute-start.2 = (s32[128]{0:T(128)}, s32[128]{0:T(128)S(1)}, u32[]{:S(2)}, u32[]{:S(2)}) collective-permute-start(s32[128]{0:T(128)} %param.12), channel_id=1, source_target_pairs={{0,1},{1,2},{2,3},{3,0},{4,5},{5,6},{6,7},{7,4},{8,9},{9,10},{10,1... | collective-permute-start | bytes 1544 | tf_op jit(solution)/shard_map/ppermute | solution.py:138
  6.6 2.3 collective-permute-start.4
  8.9 1.4 collective-permute-start.3
  10.2 1.3 collective-permute-start.5
  11.6 1.3 dynamic_slice.15
  13.5 0.8 copy.42
  14.3 0.8 constant_dynamic-slice_fusion.3
  15.2 0.1 reshape.228
  15.3 0.1 reshape.229
  15.4 0.7 fusion.15
  16.1 0.6 gather_fusion.3
  16.7 0.2 compare_reduce_fusion
  16.9 0.5 iota_reduce_fusion
  17.5 1.6 collective-permute-start
  19.1 0.7 pad_add_fusion
  19.7 0.2 convolution_bitcast_fusion
  20.0 0.2 reshape.231
  20.2 0.3 fusion.3
  20.5 1.0 pad_maximum_fusion
  21.6 46.5 %all-to-all-start = ((f32[64,3,128]{2,1,0:T(4,128)}), f32[64,3,128]{2,1,0:T(4,128)S(1)}, u32[]{:S(2)}, u32[]{:S(2)}) async-start(f32[64,3,128]{2,1,0:T(4,128)} %pad_maximum_fusion), calls=%async_computation | async-start | bytes 262144 | tf_op jit(solution)/shard_map/all_to_all | solution.py:110
  68.1 7.2 %all-to-all-done = f32[64,3,128]{2,1,0:T(4,128)S(1)} async-done(((f32[64,3,128]{2,1,0:T(4,128)}), f32[64,3,128]{2,1,0:T(4,128)S(1)}, u32[]{:S(2)}, u32[]{:S(2)}) %all-to-all-start) | async-done | bytes 98336 | tf_op jit(solution)/shard_map/all_to_all | solution.py:110
  75.4 0.7 broadcast_in_dim.12
  76.1 5.9 %all-to-all-start.1 = ((f32[64,3,128]{2,1,0:T(4,128)}), f32[64,3,128]{2,1,0:T(4,128)S(1)}, u32[]{:S(2)}, u32[]{:S(2)}) async-start(f32[64,3,128]{2,1,0:T(4,128)} %broadcast_in_dim.12), calls=%async_computation.1 | async-start | bytes 262144 | tf_op jit(solution)/shard_map/all_to_all | solution.py:113
  82.0 7.2 %all-to-all-done.1 = f32[64,3,128]{2,1,0:T(4,128)S(1)} async-done(((f32[64,3,128]{2,1,0:T(4,128)}), f32[64,3,128]{2,1,0:T(4,128)S(1)}, u32[]{:S(2)}, u32[]{:S(2)}) %all-to-all-start.1) | async-done | bytes 98336 | tf_op jit(solution)/shard_map/all_to_all | solution.py:113
  89.2 0.1 slice_reduce_fusion
  89.3 0.1 reshape_squeeze.3
  89.5 0.1 fusion.9
  89.6 0.1 copy.46
  89.7 0.1 reduce_sum.31
  89.9 0.4 fusion.1
  90.3 1.0 gather_fusion.4
  91.2 1.6 broadcast_select_fusion
  92.8 6.0 %all-to-all-start.2 = ((bf16[64,128,128]{2,1,0:T(8,128)(2,1)}), bf16[64,128,128]{2,1,0:T(8,128)(2,1)S(1)}, u32[]{:S(2)}, u32[]{:S(2)}) async-start(bf16[64,128,128]{2,1,0:T(8,128)(2,1)} %broadcast_select_fusion), calls=%async_computation.2 | async-start | bytes 4194304 | tf_op jit(solution)/shard_map/all_to_all | solution.py:181
  98.8 0.1 eq.56
  98.9 0.1 fusion.10
  99.0 0.1 reshape.236
  99.1 0.6 gather_fusion
  99.7 0.2 reduce_window_sum.11
  99.9 0.1 add.168
  100.0 0.7 fusion.13
  100.7 0.8 gather_fusion.1
  101.5 1.3 gather_fusion.2
  102.8 3.3 copy_bitcast_fusion.coefs_ref
  106.1 0.7 convert_multiply_fusion.sq_ref
  106.8 20.0 %all-to-all-done.2.arrived_ref = bf16[64,128,128]{2,1,0:T(8,128)(2,1)S(1)} async-done(((bf16[64,128,128]{2,1,0:T(8,128)(2,1)}), bf16[64,128,128]{2,1,0:T(8,128)(2,1)S(1)}, u32[]{:S(2)}, u32[]{:S(2)}) %all-to-all-start.2) | async-done | bytes 2097184 | tf_op jit(solution)/shard_map/all_to_all | solution.py:181
  126.8 1.3 copy-done
  128.1 5.6 %shard_map.82 = (bf16[4,128,128]{2,1,0:T(8,128)(2,1)}, f32[4,128,128]{2,1,0:T(8,128)}, bf16[64,128,128]{2,1,0:T(8,128)(2,1)}) custom-call(s32[64]{0:T(128)} %gather_fusion.2, s32[64]{0:T(128)} %copy-done.2, bf16[64,128,128]{2,1,0:T(8,128)(2,1)} %copy-done, bf16[4,128,2048]{2,1,0:T(8,128)(2,1)} %copy_bitcast_fusion.coefs_ref, ...), custom_call_target="tpu_custom_call", output_to_operand_aliasing={{1}: (4, {})} | custom-call | tf_op jit(solution)/shard_map/pallas_call | solution.py:87
  133.7 34.5 %all_to_all.40.arrived_ref = bf16[64,128,128]{2,1,0:T(8,128)(2,1)} all-to-all(bf16[64,128,128]{2,1,0:T(8,128)(2,1)} %get-tuple-element.22), channel_id=1, replica_groups=mesh['zh'=4,'zl'=2,'y'=4,'c'=2,'x'=4] {'zl','y','c','x'}, dimensions={0} | all-to-all | bytes 4194304 | tf_op jit(solution)/shard_map/all_to_all | solution.py:181
  168.2 5.6 %shard_map.83 = (bf16[4,128,128]{2,1,0:T(8,128)(2,1)}, f32[4,128,128]{2,1,0:T(8,128)}, bf16[64,128,128]{2,1,0:T(8,128)(2,1)}) custom-call(s32[64]{0:T(128)} %gather_fusion.2, s32[64]{0:T(128)} %copy-done.2, bf16[64,128,128]{2,1,0:T(8,128)(2,1)} %all_to_all.40.arrived_ref, ...), custom_call_target="tpu_custom_call", output_to_operand_aliasing={{1}: (4, {})} | custom-call | tf_op jit(solution)/shard_map/pallas_call | solution.py:87
  173.8 34.6 %all_to_all.41.arrived_ref = bf16[64,128,128]{2,1,0:T(8,128)(2,1)} all-to-all(bf16[64,128,128]{2,1,0:T(8,128)(2,1)} %get-tuple-element.24), channel_id=1, replica_groups=mesh['zh'=4,'zl'=2,'y'=4,'c'=2,'x'=4] {'zl','y','c','x'}, dimensions={0} | all-to-all | bytes 4194304 | tf_op jit(solution)/shard_map/all_to_all | solution.py:181
  208.4 5.6 %shard_map.84 = (bf16[4,128,128]{2,1,0:T(8,128)(2,1)}, f32[4,128,128]{2,1,0:T(8,128)}, bf16[64,128,128]{2,1,0:T(8,128)(2,1)}) custom-call(s32[64]{0:T(128)} %gather_fusion.2, s32[64]{0:T(128)} %copy-done.2, bf16[64,128,128]{2,1,0:T(8,128)(2,1)} %all_to_all.41.arrived_ref, ...), custom_call_target="tpu_custom_call", output_to_operand_aliasing={{1}: (4, {})} | custom-call | tf_op jit(solution)/shard_map/pallas_call | solution.py:87
  214.0 34.4 %all_to_all.42.arrived_ref = bf16[64,128,128]{2,1,0:T(8,128)(2,1)} all-to-all(bf16[64,128,128]{2,1,0:T(8,128)(2,1)} %get-tuple-element.26), channel_id=1, replica_groups=mesh['zh'=4,'zl'=2,'y'=4,'c'=2,'x'=4] {'zl','y','c','x'}, dimensions={0} | all-to-all | bytes 4194304 | tf_op jit(solution)/shard_map/all_to_all | solution.py:181
  248.4 5.6 %shard_map.85 = (bf16[4,128,128]{2,1,0:T(8,128)(2,1)}, f32[4,128,128]{2,1,0:T(8,128)}, bf16[64,128,128]{2,1,0:T(8,128)(2,1)}) custom-call(s32[64]{0:T(128)} %gather_fusion.2, s32[64]{0:T(128)} %copy-done.2, bf16[64,128,128]{2,1,0:T(8,128)(2,1)} %all_to_all.42.arrived_ref, ...), custom_call_target="tpu_custom_call", output_to_operand_aliasing={{1}: (4, {})} | custom-call | tf_op jit(solution)/shard_map/pallas_call | solution.py:87
  254.0 34.4 %all_to_all.43.arrived_ref = bf16[64,128,128]{2,1,0:T(8,128)(2,1)} all-to-all(bf16[64,128,128]{2,1,0:T(8,128)(2,1)} %get-tuple-element.28), channel_id=1, replica_groups=mesh['zh'=4,'zl'=2,'y'=4,'c'=2,'x'=4] {'zl','y','c','x'}, dimensions={0} | all-to-all | bytes 4194304 | tf_op jit(solution)/shard_map/all_to_all | solution.py:181
  288.4 5.6 %shard_map.86 = (bf16[4,128,128]{2,1,0:T(8,128)(2,1)}, f32[4,128,128]{2,1,0:T(8,128)}, bf16[64,128,128]{2,1,0:T(8,128)(2,1)}) custom-call(s32[64]{0:T(128)} %gather_fusion.2, s32[64]{0:T(128)} %copy-done.2, bf16[64,128,128]{2,1,0:T(8,128)(2,1)} %all_to_all.43.arrived_ref, ...), custom_call_target="tpu_custom_call", output_to_operand_aliasing={{1}: (4, {})} | custom-call | tf_op jit(solution)/shard_map/pallas_call | solution.py:87
  294.1 34.4 %all_to_all.44.arrived_ref = bf16[64,128,128]{2,1,0:T(8,128)(2,1)} all-to-all(bf16[64,128,128]{2,1,0:T(8,128)(2,1)} %get-tuple-element.30), channel_id=1, replica_groups=mesh['zh'=4,'zl'=2,'y'=4,'c'=2,'x'=4] {'zl','y','c','x'}, dimensions={0} | all-to-all | bytes 4194304 | tf_op jit(solution)/shard_map/all_to_all | solution.py:181
  328.5 4.3 %shard_map.87 = (bf16[4,128,128]{2,1,0:T(8,128)(2,1)}, f32[4,128,128]{2,1,0:T(8,128)}) custom-call(s32[64]{0:T(128)} %gather_fusion.2, s32[64]{0:T(128)} %copy-done.2, bf16[64,128,128]{2,1,0:T(8,128)(2,1)} %all_to_all.44.arrived_ref, bf16[4,128,2048]{2,1,0:T(8,128)(2,1)} %copy_bitcast_fusion.coefs_ref, ...), custom_call_target="tpu_custom_call", output_to_operand_aliasing={{1}: (4, {})} | custom-call | tf_op jit(solution)/shard_map/pallas_call | solution.py:87
  332.8 2.3 collective-permute-start.6
  335.1 1.1 reduce_sum.32
  336.2 6.9 %collective-permute-start.7 = (f32[4,128]{1,0:T(4,128)S(1)}, f32[4,128]{1,0:T(4,128)S(1)}, u32[]{:S(2)}, u32[]{:S(2)}) collective-permute-start(f32[4,128]{1,0:T(4,128)S(1)} %reduce_sum.32), channel_id=1, source_target_pairs={{0,0},{1,224},{2,192},{3,160},{4,164},{5,196},{6,228},{7,4},{8,8},... | collective-permute-start | bytes 6152 | tf_op jit(solution)/shard_map/ppermute | solution.py:189
  343.1 2.2 collective-permute-done.7
  345.3 14.8 %psum.7 = f32[4,128]{1,0:T(4,128)S(1)} all-reduce(f32[4,128]{1,0:T(4,128)S(1)} %collective-permute-done.7), channel_id=1, replica_groups=mesh['zh'=4,'zl'=2,'y'=4,'c'=2,'x'=4] {'x'}, use_global_device_ids=true, to_apply=%region_7.8 | all-reduce | flops 512 | bytes 4096 | tf_op jit(solution)/shard_map/psum | solution.py:190
  360.2 0.8 multiply_divide_fusion
  (30 shorter events, 0.3 us)
Async XLA Ops:
  0.0 20.2 %collective-permute-start.1 = (bf16[4,16,128,128]{3,2,1,0:T(8,128)(2,1)}, bf16[4,16,128,128]{3,2,1,0:T(8,128)(2,1)S(1)}, u32[]{:S(2)}, u32[]{:S(2)}) collective-permute-start(bf16[4,16,128,128]{3,2,1,0:T(8,128)(2,1)} %param.8), channel_id=1, source_target_pairs={{0,0},{225,1},{194,2},{163,3},{164,4},{197,5},{230,6},{7,7},{8,8},... | collective-permute-start | bytes 6291464 | tf_op jit(solution)/shard_map/ppermute | solution.py:122
  2.2 15.2 %collective-permute-start.2 = (s32[128]{0:T(128)}, s32[128]{0:T(128)S(1)}, u32[]{:S(2)}, u32[]{:S(2)}) collective-permute-start(s32[128]{0:T(128)} %param.12), channel_id=1, source_target_pairs={{0,1},{1,2},{2,3},{3,0},{4,5},{5,6},{6,7},{7,4},{8,9},{9,10},{10,1... | collective-permute-start | bytes 1544 | tf_op jit(solution)/shard_map/ppermute | solution.py:138
  6.6 12.5 %collective-permute-start.4 = (s32[128]{0:T(128)}, s32[128]{0:T(128)S(1)}, u32[]{:S(2)}, u32[]{:S(2)}) collective-permute-start(s32[128]{0:T(128)} %param.12), channel_id=1, source_target_pairs={{0,3},{1,0},{2,1},{3,2},{4,7},{5,4},{6,5},{7,6},{8,11},{9,8},{10,9... | collective-permute-start | bytes 1544 | tf_op jit(solution)/shard_map/ppermute | solution.py:138
  8.9 10.2 %collective-permute-start.3 = (s32[128]{0:T(128)}, s32[128]{0:T(128)S(1)}, u32[]{:S(2)}, u32[]{:S(2)}) collective-permute-start(s32[128]{0:T(128)} %param.12), channel_id=1, source_target_pairs={{0,2},{1,3},{2,0},{3,1},{4,6},{5,7},{6,4},{7,5},{8,10},{9,11},{10,... | collective-permute-start | bytes 1544 | tf_op jit(solution)/shard_map/ppermute | solution.py:138
  10.2 9.5 %collective-permute-start.5 = (f32[512]{0:T(512)}, f32[512]{0:T(512)S(1)}, u32[]{:S(2)}, u32[]{:S(2)}) collective-permute-start(f32[512]{0:T(512)} %param.11), channel_id=1, source_target_pairs={{0,0},{225,1},{194,2},{163,3},{164,4},{197,5},{230,6},{7,7},{8,8},... | collective-permute-start | bytes 6152 | tf_op jit(solution)/shard_map/ppermute | solution.py:121
  17.4 73.8 %copy-start.2 = (s32[64]{0:T(128)}, s32[64]{0:T(128)S(1)}, u32[]{:S(2)}) copy-start(s32[64]{0:T(128)S(1)} %get-tuple-element.19.send_ref) | copy-start | bytes 772
  17.5 2.7 collective-permute-start
  20.2 69.6 %copy-start.1 = (bf16[4,16,128,128]{3,2,1,0:T(8,128)(2,1)}, bf16[4,16,128,128]{3,2,1,0:T(8,128)(2,1)S(1)}, u32[]{:S(2)}) copy-start(bf16[4,16,128,128]{3,2,1,0:T(8,128)(2,1)S(1)} %collective-permute-done.1) | copy-start | bytes 6291460
  21.6 53.7 %all-to-all-start = ((f32[64,3,128]{2,1,0:T(4,128)}), f32[64,3,128]{2,1,0:T(4,128)S(1)}, u32[]{:S(2)}, u32[]{:S(2)}) async-start(f32[64,3,128]{2,1,0:T(4,128)} %pad_maximum_fusion), calls=%async_computation | async-start | bytes 262144 | tf_op jit(solution)/shard_map/all_to_all | solution.py:110
  76.1 13.2 %all-to-all-start.1 = ((f32[64,3,128]{2,1,0:T(4,128)}), f32[64,3,128]{2,1,0:T(4,128)S(1)}, u32[]{:S(2)}, u32[]{:S(2)}) async-start(f32[64,3,128]{2,1,0:T(4,128)} %broadcast_in_dim.12), calls=%async_computation.1 | async-start | bytes 262144 | tf_op jit(solution)/shard_map/all_to_all | solution.py:113
  92.8 34.0 %all-to-all-start.2 = ((bf16[64,128,128]{2,1,0:T(8,128)(2,1)}), bf16[64,128,128]{2,1,0:T(8,128)(2,1)S(1)}, u32[]{:S(2)}, u32[]{:S(2)}) async-start(bf16[64,128,128]{2,1,0:T(8,128)(2,1)} %broadcast_select_fusion), calls=%async_computation.2 | async-start | bytes 4194304 | tf_op jit(solution)/shard_map/all_to_all | solution.py:181
  126.8 1.3 copy-start
  332.8 27.3 %collective-permute-start.6 = (f32[4,128,128]{2,1,0:T(8,128)}, f32[4,128,128]{2,1,0:T(8,128)S(1)}, u32[]{:S(2)}, u32[]{:S(2)}) collective-permute-start(f32[4,128,128]{2,1,0:T(8,128)} %get-tuple-element.32), channel_id=1, source_target_pairs={{0,0},{1,224},{2,192},{3,160},{4,164},{5,196},{6,228},{7,4},{8,8},... | collective-permute-start | bytes 786440 | tf_op jit(solution)/shard_map/ppermute | solution.py:189
  336.2 9.1 %collective-permute-start.7 = (f32[4,128]{1,0:T(4,128)S(1)}, f32[4,128]{1,0:T(4,128)S(1)}, u32[]{:S(2)}, u32[]{:S(2)}) collective-permute-start(f32[4,128]{1,0:T(4,128)S(1)} %reduce_sum.32), channel_id=1, source_target_pairs={{0,0},{1,224},{2,192},{3,160},{4,164},{5,196},{6,228},{7,4},{8,8},... | collective-permute-start | bytes 6152 | tf_op jit(solution)/shard_map/ppermute | solution.py:189

commit v15 on v10

--- a/solution.py
+++ b/solution.py
@@ -97,6 +97,27 @@
     )(take, send, arrived, coefs_wide, squares)
 
 
+def send_kernel(send_ref, present_ref, out_hbm, sems):
+    copies = []
+    for v in range(out_hbm.shape[0]):
+        cp = pltpu.make_async_copy(present_ref.at[send_ref[v]], out_hbm.at[v], sems.at[v])
+        cp.start()
+        copies.append(cp)
+    for cp in copies:
+        cp.wait()
+
+
+def first_outgoing(send, present):
+    n_out = send.shape[0]
+    return pl.pallas_call(
+        send_kernel,
+        out_shape=jax.ShapeDtypeStruct((n_out,) + present.shape[1:], present.dtype),
+        in_specs=[pl.BlockSpec(memory_space=pltpu.SMEM), pl.BlockSpec(memory_space=pltpu.VMEM)],
+        out_specs=pl.BlockSpec(memory_space=pl.ANY),
+        scratch_shapes=[pltpu.SemaphoreType.DMA((n_out,))],
+    )(send, present)
+
+
 def gather_rows(chosen, chosen_idio, owners):
     shocks, factors = chosen.shape
     per = shocks // owners
@@ -174,7 +195,7 @@
             jnp.int32
         )
         send_idx = jnp.argmax(send_need, axis=1).astype(jnp.int32)
-        outgoing = jnp.take(present_response, send_idx, axis=0)
+        outgoing = first_outgoing(send_idx, present_response)
         coefs_wide = coefs.transpose(0, 2, 1, 3).reshape(blk_dev, block_size, lags * block_size)
         for step_no in range(HORIZONS - 1):
             arriving_response = lax.all_to_all(outgoing, BOX, split_axis=0, concat_axis=0, tiled=True)

time: 358 us -> 359 us (level)
  no operation moved by 1% of the time
where the time goes in v15:
time: 359 us; the launch traced here: 353 us
  blocking collectives  196 us (55%)
  starting transfers between devices  59.5 us (17%)
  waiting for transfers between devices  40.4 us (11%)
  Pallas kernels  35.1 us (10%)
  local copies, waits for them, and re-layouts  14.1 us (4%)
  other arithmetic  6.08 us (2%)
    all_to_all x5, blocking collectives, on_device(): lax.all_to_all(outgoing, BOX, split_axis=0, concat_axis=0, tiled=True)  186 us
    pallas_call x6, Pallas kernels, step(): pl.pallas_call(last_kernel if last else step_kernel, out_shape=shapes[:2]...  32.3 us
    all_to_all x1, waiting for transfers between devices, on_device(): lax.all_to_all(outgoing, BOX, split_axis=0, concat_axis=0, tiled=True)  19.9 us
    all_to_all x1, starting transfers between devices, gather_rows(): arrived = lax.all_to_all(packed, BOX, 0, 0, tiled=True)  17.7 us
    ppermute x1, starting transfers between devices, on_device(): coefs = lax.ppermute(coefs, ALL, perm_in)  17.1 us
    psum x1, blocking collectives, on_device(): totals = lax.psum(partial, 'x')  10.1 us
  transfers between devices with their start and end apart: 11, of which 4 were waited for; matrix products, arithmetic and copies ran while one was open for 4% of the time, Pallas kernels for 0%

profile of v15, /device:TPU:96, one launch (start us, length us, event | category | flops | bytes accessed | tf_op | source)
XLA Modules:
  0.0 353.5 jit_solution(15015197070160115432)
XLA Ops:
  0.0 1.5 collective-permute-start
  1.5 1.7 collective-permute-start.2
  3.2 1.8 collective-permute-start.1
  5.1 1.3 collective-permute-start.4
  6.4 1.6 collective-permute-start.3
  8.0 1.3 dynamic_slice.15
  9.9 0.8 constant_dynamic-slice_fusion.3
  10.8 0.1 reshape.223
  10.9 0.7 fusion.16
  11.6 0.8 copy.46
  12.4 0.1 reshape.224
  12.5 0.6 gather_fusion.3
  13.1 0.7 pad_add_fusion
  13.8 0.2 convolution_bitcast_fusion.1
  14.0 0.2 reshape.226
  14.3 0.3 fusion.4
  14.6 0.7 pad_maximum_fusion
  15.3 17.7 %all-to-all-start = ((f32[64,3,128]{2,1,0:T(4,128)}), f32[64,3,128]{2,1,0:T(4,128)S(1)}, u32[]{:S(2)}, u32[]{:S(2)}) async-start(f32[64,3,128]{2,1,0:T(4,128)} %pad_maximum_fusion), calls=%async_computation | async-start | bytes 262144 | tf_op jit(solution)/shard_map/all_to_all | solution.py:131
  33.0 0.2 compare_reduce_fusion
  33.3 7.0 %all-to-all-done = f32[64,3,128]{2,1,0:T(4,128)S(1)} async-done(((f32[64,3,128]{2,1,0:T(4,128)}), f32[64,3,128]{2,1,0:T(4,128)S(1)}, u32[]{:S(2)}, u32[]{:S(2)}) %all-to-all-start) | async-done | bytes 98336 | tf_op jit(solution)/shard_map/all_to_all | solution.py:131
  40.3 0.7 broadcast_in_dim.2
  41.0 5.9 %all-to-all-start.1 = ((f32[64,3,128]{2,1,0:T(4,128)}), f32[64,3,128]{2,1,0:T(4,128)S(1)}, u32[]{:S(2)}, u32[]{:S(2)}) async-start(f32[64,3,128]{2,1,0:T(4,128)} %broadcast_in_dim.2), calls=%async_computation.1 | async-start | bytes 262144 | tf_op jit(solution)/shard_map/all_to_all | solution.py:134
  47.0 0.6 iota_reduce_fusion
  47.6 6.6 %all-to-all-done.1 = f32[64,3,128]{2,1,0:T(4,128)S(1)} async-done(((f32[64,3,128]{2,1,0:T(4,128)}), f32[64,3,128]{2,1,0:T(4,128)S(1)}, u32[]{:S(2)}, u32[]{:S(2)}) %all-to-all-start.1) | async-done | bytes 98336 | tf_op jit(solution)/shard_map/all_to_all | solution.py:134
  54.2 0.1 slice_reduce_fusion
  54.3 0.1 reshape_squeeze.3
  54.5 0.1 fusion.10
  54.6 0.1 copy.50
  54.7 0.1 reduce_sum.31
  54.8 0.4 fusion.2
  55.2 0.8 copy.51
  56.0 2.8 shard_map.82
  58.8 6.2 %all-to-all-start.2 = ((bf16[64,128,128]{2,1,0:T(8,128)(2,1)}), bf16[64,128,128]{2,1,0:T(8,128)(2,1)S(1)}, u32[]{:S(2)}, u32[]{:S(2)}) async-start(bf16[64,128,128]{2,1,0:T(8,128)(2,1)} %shard_map.82), calls=%async_computation.2 | async-start | bytes 4194304 | tf_op jit(solution)/shard_map/all_to_all | solution.py:201
  64.9 17.1 %collective-permute-start.5 = (bf16[4,16,128,128]{3,2,1,0:T(8,128)(2,1)}, bf16[4,16,128,128]{3,2,1,0:T(8,128)(2,1)}, u32[]{:S(2)}, u32[]{:S(2)}) collective-permute-start(bf16[4,16,128,128]{3,2,1,0:T(8,128)(2,1)} %param.8), channel_id=1, source_target_pairs={{0,0},{225,1},{194,2},{163,3},{164,4},{197,5},{230,6},{7,7},{8,8},... | collective-permute-start | bytes 6291464 | tf_op jit(solution)/shard_map/ppermute | solution.py:143
  82.1 0.1 eq.56
  82.2 0.1 fusion.11
  82.3 0.1 reshape.231
  82.4 0.6 gather_fusion
  83.0 0.2 reduce_window_sum.11
  83.2 0.1 add.162
  83.3 0.7 fusion.14
  84.0 0.8 gather_fusion.1
  84.8 1.3 gather_fusion.2
  86.1 0.7 convert_multiply_fusion.sq_ref
  86.8 3.3 copy_bitcast_fusion.coefs_ref
  90.1 19.9 %all-to-all-done.2.arrived_ref = bf16[64,128,128]{2,1,0:T(8,128)(2,1)S(1)} async-done(((bf16[64,128,128]{2,1,0:T(8,128)(2,1)}), bf16[64,128,128]{2,1,0:T(8,128)(2,1)S(1)}, u32[]{:S(2)}, u32[]{:S(2)}) %all-to-all-start.2) | async-done | bytes 2097184 | tf_op jit(solution)/shard_map/all_to_all | solution.py:201
  110.0 1.3 copy-done
  111.3 5.6 %shard_map.83 = (bf16[4,128,128]{2,1,0:T(8,128)(2,1)}, f32[4,128,128]{2,1,0:T(8,128)}, bf16[64,128,128]{2,1,0:T(8,128)(2,1)}) custom-call(s32[64]{0:T(128)} %gather_fusion.2, s32[64]{0:T(128)} %get-tuple-element.17.send_ref, bf16[64,128,128]{2,1,0:T(8,128)(2,1)} %copy-done, ...), custom_call_target="tpu_custom_call", output_to_operand_aliasing={{1}: (4, {})} | custom-call | tf_op jit(solution)/shard_map/pallas_call | solution.py:87
  116.9 48.5 %all_to_all.40.arrived_ref = bf16[64,128,128]{2,1,0:T(8,128)(2,1)} all-to-all(bf16[64,128,128]{2,1,0:T(8,128)(2,1)} %get-tuple-element.18), channel_id=1, replica_groups=mesh['zh'=4,'zl'=2,'y'=4,'c'=2,'x'=4] {'zl','y','c','x'}, dimensions={0} | all-to-all | bytes 4194304 | tf_op jit(solution)/shard_map/all_to_all | solution.py:201
  165.4 5.6 %shard_map.84 = (bf16[4,128,128]{2,1,0:T(8,128)(2,1)}, f32[4,128,128]{2,1,0:T(8,128)}, bf16[64,128,128]{2,1,0:T(8,128)(2,1)}) custom-call(s32[64]{0:T(128)} %gather_fusion.2, s32[64]{0:T(128)} %get-tuple-element.17.send_ref, bf16[64,128,128]{2,1,0:T(8,128)(2,1)} %all_to_all.40.arrived_ref, ...), custom_call_target="tpu_custom_call", output_to_operand_aliasing={{1}: (4, {})} | custom-call | tf_op jit(solution)/shard_map/pallas_call | solution.py:87
  171.0 34.5 %all_to_all.41.arrived_ref = bf16[64,128,128]{2,1,0:T(8,128)(2,1)} all-to-all(bf16[64,128,128]{2,1,0:T(8,128)(2,1)} %get-tuple-element.20), channel_id=1, replica_groups=mesh['zh'=4,'zl'=2,'y'=4,'c'=2,'x'=4] {'zl','y','c','x'}, dimensions={0} | all-to-all | bytes 4194304 | tf_op jit(solution)/shard_map/all_to_all | solution.py:201
  205.5 5.6 %shard_map.85 = (bf16[4,128,128]{2,1,0:T(8,128)(2,1)}, f32[4,128,128]{2,1,0:T(8,128)}, bf16[64,128,128]{2,1,0:T(8,128)(2,1)}) custom-call(s32[64]{0:T(128)} %gather_fusion.2, s32[64]{0:T(128)} %get-tuple-element.17.send_ref, bf16[64,128,128]{2,1,0:T(8,128)(2,1)} %all_to_all.41.arrived_ref, ...), custom_call_target="tpu_custom_call", output_to_operand_aliasing={{1}: (4, {})} | custom-call | tf_op jit(solution)/shard_map/pallas_call | solution.py:87
  211.1 34.5 %all_to_all.42.arrived_ref = bf16[64,128,128]{2,1,0:T(8,128)(2,1)} all-to-all(bf16[64,128,128]{2,1,0:T(8,128)(2,1)} %get-tuple-element.22), channel_id=1, replica_groups=mesh['zh'=4,'zl'=2,'y'=4,'c'=2,'x'=4] {'zl','y','c','x'}, dimensions={0} | all-to-all | bytes 4194304 | tf_op jit(solution)/shard_map/all_to_all | solution.py:201
  245.6 5.6 %shard_map.86 = (bf16[4,128,128]{2,1,0:T(8,128)(2,1)}, f32[4,128,128]{2,1,0:T(8,128)}, bf16[64,128,128]{2,1,0:T(8,128)(2,1)}) custom-call(s32[64]{0:T(128)} %gather_fusion.2, s32[64]{0:T(128)} %get-tuple-element.17.send_ref, bf16[64,128,128]{2,1,0:T(8,128)(2,1)} %all_to_all.42.arrived_ref, ...), custom_call_target="tpu_custom_call", output_to_operand_aliasing={{1}: (4, {})} | custom-call | tf_op jit(solution)/shard_map/pallas_call | solution.py:87
  251.2 34.4 %all_to_all.43.arrived_ref = bf16[64,128,128]{2,1,0:T(8,128)(2,1)} all-to-all(bf16[64,128,128]{2,1,0:T(8,128)(2,1)} %get-tuple-element.24), channel_id=1, replica_groups=mesh['zh'=4,'zl'=2,'y'=4,'c'=2,'x'=4] {'zl','y','c','x'}, dimensions={0} | all-to-all | bytes 4194304 | tf_op jit(solution)/shard_map/all_to_all | solution.py:201
  285.6 5.6 %shard_map.87 = (bf16[4,128,128]{2,1,0:T(8,128)(2,1)}, f32[4,128,128]{2,1,0:T(8,128)}, bf16[64,128,128]{2,1,0:T(8,128)(2,1)}) custom-call(s32[64]{0:T(128)} %gather_fusion.2, s32[64]{0:T(128)} %get-tuple-element.17.send_ref, bf16[64,128,128]{2,1,0:T(8,128)(2,1)} %all_to_all.43.arrived_ref, ...), custom_call_target="tpu_custom_call", output_to_operand_aliasing={{1}: (4, {})} | custom-call | tf_op jit(solution)/shard_map/pallas_call | solution.py:87
  291.2 34.4 %all_to_all.44.arrived_ref = bf16[64,128,128]{2,1,0:T(8,128)(2,1)} all-to-all(bf16[64,128,128]{2,1,0:T(8,128)(2,1)} %get-tuple-element.26), channel_id=1, replica_groups=mesh['zh'=4,'zl'=2,'y'=4,'c'=2,'x'=4] {'zl','y','c','x'}, dimensions={0} | all-to-all | bytes 4194304 | tf_op jit(solution)/shard_map/all_to_all | solution.py:201
  325.6 4.3 %shard_map.88 = (bf16[4,128,128]{2,1,0:T(8,128)(2,1)}, f32[4,128,128]{2,1,0:T(8,128)}) custom-call(s32[64]{0:T(128)} %gather_fusion.2, s32[64]{0:T(128)} %get-tuple-element.17.send_ref, bf16[64,128,128]{2,1,0:T(8,128)(2,1)} %all_to_all.44.arrived_ref, bf16[4,128,2048]{2,1,0:T(8,128)(2,1)} %copy_bitcast_fusion.coefs_ref, ...), custom_call_target="tpu_custom_call", output_to_operand_aliasing={{1}: (4, {})} | custom-call | tf_op jit(solution)/shard_map/pallas_call | solution.py:87
  330.0 2.3 collective-permute-start.6
  332.2 1.1 reduce_sum.32
  333.3 2.3 collective-permute-start.7
  335.7 6.8 %collective-permute-done.7 = f32[4,128]{1,0:T(4,128)S(1)} collective-permute-done((f32[4,128]{1,0:T(4,128)S(1)}, f32[4,128]{1,0:T(4,128)S(1)}, u32[]{:S(2)}, u32[]{:S(2)}) %collective-permute-start.7) | collective-permute-done | bytes 2080 | tf_op jit(solution)/shard_map/ppermute | solution.py:209
  342.5 10.1 %psum.7 = f32[4,128]{1,0:T(4,128)S(1)} all-reduce(f32[4,128]{1,0:T(4,128)S(1)} %collective-permute-done.7), channel_id=1, replica_groups=mesh['zh'=4,'zl'=2,'y'=4,'c'=2,'x'=4] {'x'}, use_global_device_ids=true, to_apply=%region_7.8 | all-reduce | flops 512 | bytes 4096 | tf_op jit(solution)/shard_map/psum | solution.py:210
  352.6 0.8 multiply_divide_fusion
  (25 shorter events, 0.3 us)
Async XLA Ops:
  0.0 13.1 %collective-permute-start = (s32[128]{0:T(128)}, s32[128]{0:T(128)S(1)}, u32[]{:S(2)}, u32[]{:S(2)}) collective-permute-start(s32[128]{0:T(128)} %param.12), channel_id=1, source_target_pairs={{0,1},{1,2},{2,3},{3,0},{4,5},{5,6},{6,7},{7,4},{8,9},{9,10},{10,1... | collective-permute-start | bytes 1544 | tf_op jit(solution)/shard_map/ppermute | solution.py:158
  1.5 11.6 %collective-permute-start.2 = (s32[128]{0:T(128)}, s32[128]{0:T(128)S(1)}, u32[]{:S(2)}, u32[]{:S(2)}) collective-permute-start(s32[128]{0:T(128)} %param.12), channel_id=1, source_target_pairs={{0,3},{1,0},{2,1},{3,2},{4,7},{5,4},{6,5},{7,6},{8,11},{9,8},{10,9... | collective-permute-start | bytes 1544 | tf_op jit(solution)/shard_map/ppermute | solution.py:158
  3.2 9.9 %collective-permute-start.1 = (s32[128]{0:T(128)}, s32[128]{0:T(128)S(1)}, u32[]{:S(2)}, u32[]{:S(2)}) collective-permute-start(s32[128]{0:T(128)} %param.12), channel_id=1, source_target_pairs={{0,2},{1,3},{2,0},{3,1},{4,6},{5,7},{6,4},{7,5},{8,10},{9,11},{10,... | collective-permute-start | bytes 1544 | tf_op jit(solution)/shard_map/ppermute | solution.py:158
  5.1 8.8 %collective-permute-start.4 = (f32[512]{0:T(512)}, f32[512]{0:T(512)S(1)}, u32[]{:S(2)}, u32[]{:S(2)}) collective-permute-start(f32[512]{0:T(512)} %param.11), channel_id=1, source_target_pairs={{0,0},{225,1},{194,2},{163,3},{164,4},{197,5},{230,6},{7,7},{8,8},... | collective-permute-start | bytes 6152 | tf_op jit(solution)/shard_map/ppermute | solution.py:142
  6.4 7.9 %collective-permute-start.3 = (f32[512,128]{1,0:T(8,128)}, f32[512,128]{1,0:T(8,128)S(1)}, u32[]{:S(2)}, u32[]{:S(2)}) collective-permute-start(f32[512,128]{1,0:T(8,128)} %param.10), channel_id=1, source_target_pairs={{0,0},{225,1},{194,2},{163,3},{164,4},{197,5},{230,6},{7,7},{8,8},... | collective-permute-start | bytes 786440 | tf_op jit(solution)/shard_map/ppermute | solution.py:142
  15.3 25.0 %all-to-all-start = ((f32[64,3,128]{2,1,0:T(4,128)}), f32[64,3,128]{2,1,0:T(4,128)S(1)}, u32[]{:S(2)}, u32[]{:S(2)}) async-start(f32[64,3,128]{2,1,0:T(4,128)} %pad_maximum_fusion), calls=%async_computation | async-start | bytes 262144 | tf_op jit(solution)/shard_map/all_to_all | solution.py:131
  41.0 13.2 %all-to-all-start.1 = ((f32[64,3,128]{2,1,0:T(4,128)}), f32[64,3,128]{2,1,0:T(4,128)S(1)}, u32[]{:S(2)}, u32[]{:S(2)}) async-start(f32[64,3,128]{2,1,0:T(4,128)} %broadcast_in_dim.2), calls=%async_computation.1 | async-start | bytes 262144 | tf_op jit(solution)/shard_map/all_to_all | solution.py:134
  58.8 27.3 %copy-start.1 = (bf16[512,128]{1,0:T(8,128)(2,1)S(1)}, bf16[512,128]{1,0:T(8,128)(2,1)}, u32[]{:S(2)}) copy-start(bf16[512,128]{1,0:T(8,128)(2,1)} %copy.51) | copy-start | bytes 393220
  58.8 51.2 %all-to-all-start.2 = ((bf16[64,128,128]{2,1,0:T(8,128)(2,1)}), bf16[64,128,128]{2,1,0:T(8,128)(2,1)S(1)}, u32[]{:S(2)}, u32[]{:S(2)}) async-start(bf16[64,128,128]{2,1,0:T(8,128)(2,1)} %shard_map.82), calls=%async_computation.2 | async-start | bytes 4194304 | tf_op jit(solution)/shard_map/all_to_all | solution.py:201
  64.9 21.9 %collective-permute-start.5 = (bf16[4,16,128,128]{3,2,1,0:T(8,128)(2,1)}, bf16[4,16,128,128]{3,2,1,0:T(8,128)(2,1)}, u32[]{:S(2)}, u32[]{:S(2)}) collective-permute-start(bf16[4,16,128,128]{3,2,1,0:T(8,128)(2,1)} %param.8), channel_id=1, source_target_pairs={{0,0},{225,1},{194,2},{163,3},{164,4},{197,5},{230,6},{7,7},{8,8},... | collective-permute-start | bytes 6291464 | tf_op jit(solution)/shard_map/ppermute | solution.py:143
  110.0 1.3 copy-start
  330.0 22.7 %collective-permute-start.6 = (f32[4,128,128]{2,1,0:T(8,128)}, f32[4,128,128]{2,1,0:T(8,128)S(1)}, u32[]{:S(2)}, u32[]{:S(2)}) collective-permute-start(f32[4,128,128]{2,1,0:T(8,128)} %get-tuple-element.28), channel_id=1, source_target_pairs={{0,0},{1,224},{2,192},{3,160},{4,164},{5,196},{6,228},{7,4},{8,8},... | collective-permute-start | bytes 786440 | tf_op jit(solution)/shard_map/ppermute | solution.py:209
  333.3 9.1 %collective-permute-start.7 = (f32[4,128]{1,0:T(4,128)S(1)}, f32[4,128]{1,0:T(4,128)S(1)}, u32[]{:S(2)}, u32[]{:S(2)}) collective-permute-start(f32[4,128]{1,0:T(4,128)S(1)} %reduce_sum.32), channel_id=1, source_target_pairs={{0,0},{1,224},{2,192},{3,160},{4,164},{5,196},{6,228},{7,4},{8,8},... | collective-permute-start | bytes 6152 | tf_op jit(solution)/shard_map/ppermute | solution.py:209
